TPU v7x, 128 devices: a whole 4x4x4 slice. The times are simulated.
128 devices in a mesh: req: 16 (over z, x), tp: 8 (over y, core).
Axes of the slice: x: 4, y: 4, z: 4, core: 2. Of those that a mesh axis runs over, the one named last changes fastest.
Arguments:
- queries: bfloat16 [512, 7168], P('req', 'tp')
- new_keys: bfloat16 [512, 1024], P('req', 'tp'), may hold values from -6 to 6
- new_values: bfloat16 [512, 1024], P('req', 'tp'), may hold values from -6 to 6
- cache_keys: bfloat16 [286720, 1024], P('req', 'tp'), may hold values from -6 to 6
- cache_values: bfloat16 [286720, 1024], P('req', 'tp'), may hold values from -6 to 6
- tok_req: int32 [512], P('req'), may hold values from 0 to 16, as said below
- cache_req: int32 [286720], P('req'), may hold values from -1 to 16, as said below
- out_weight: bfloat16 [7168, 7168], P('tp', 'req'), may hold values from -0.0625 to 0.0625
- residual: bfloat16 [512, 7168], P('tp', 'req')
- norm_gain: float32 [7168], replicated, may hold values from 0.1 to 1.9
- gate_weight: bfloat16 [7168, 20480], P(None, ('req', 'tp')), may hold values from -0.0625 to 0.0625
- up_weight: bfloat16 [7168, 20480], P(None, ('req', 'tp')), may hold values from -0.0625 to 0.0625
- down_weight: bfloat16 [20480, 7168], P(('req', 'tp')), may hold values from -0.15625 to 0.15625
Outputs:
- layer_out: bfloat16 [512, 7168], P('tp', 'req')
Inputs may be any that keep to these rules, and one draw needn't show every extreme that they name: `tok_req`: within a group, request 0 is the prefill request, whose tokens stand first and in order; decode requests 1, 2, ... follow with one token each. `cache_req`: -1 marks an empty slot; within a group the owned slots stand first, each request's slots together, requests in increasing order; every request of a group that has tokens owns at least one slot.
All inputs are finite; a program needn't handle non-finite values.
Results may differ from a plain program's by a relative error of at most 0.014.
Values may be sent and summed in bfloat16 or wider, within the bound.
No kernel may reach another device: no remote copies, remote signals or barrier semaphores. Data moves between devices by JAX's collectives and lax.ppermute only.
A program may use at most 128 MiB of HBM per device.

v0:
```python
import math

import jax
import jax.numpy as jnp
from jax import lax
from jax.sharding import PartitionSpec as P

HD = 128


epsilon = 1e-05
masked_value = -1e30
key_block = 512


def attend(queries, new_keys, new_values, cache_keys, cache_values, tok_req, cache_req):
    tokens_here = queries.shape[0]
    head_dim = HD
    kv_here = new_keys.shape[1] // head_dim
    group_size = queries.shape[1] // (kv_here * head_dim)
    score_scale = 1.0 / math.sqrt(head_dim)
    row_count = tokens_here * group_size
    grouped = queries.reshape(tokens_here, kv_here, group_size, head_dim)
    row_req = jnp.repeat(tok_req, group_size)
    row_tok = jnp.repeat(jnp.arange(tokens_here, dtype=jnp.int32), group_size)
    pool_size = cache_keys.shape[0]
    block_width = min(key_block, pool_size)
    live_slots = jnp.sum((cache_req >= 0).astype(jnp.int32))
    live_blocks = (live_slots + block_width - 1) // block_width

    def update(carried, block_keys, block_values, visible):
        running_max, denominator, weighted = carried[0]
        query_rows = grouped[:, 0].reshape(row_count, head_dim)
        scores = (
            jnp.einsum("qd,kd->qk", query_rows, block_keys, preferred_element_type=jnp.float32)
            * score_scale
        )
        masked = jnp.where(visible, scores, masked_value)
        new_max = jnp.maximum(running_max, jnp.max(masked, axis=1))
        weights = jnp.where(visible, jnp.exp(masked - new_max[:, None]), 0.0).astype(jnp.bfloat16)
        factor = jnp.exp(running_max - new_max)
        denominator = denominator * factor + jnp.sum(weights.astype(jnp.float32), axis=1)
        weighted = weighted * factor[:, None] + jnp.dot(
            weights, block_values, preferred_element_type=jnp.float32
        )
        renewed = [(new_max, denominator, weighted)]
        return tuple(renewed)

    initial = tuple(
        (
            (
                jnp.full((row_count,), masked_value, jnp.float32),
                jnp.zeros((row_count,), jnp.float32),
                jnp.zeros((row_count, head_dim), jnp.float32),
            )
            for unused in range(kv_here)
        )
    )

    def consume(block_index, carried):
        first_slot = block_index * block_width
        block_keys = lax.dynamic_slice_in_dim(cache_keys, first_slot, block_width, 0)
        block_values = lax.dynamic_slice_in_dim(cache_values, first_slot, block_width, 0)
        owners = lax.dynamic_slice_in_dim(cache_req, first_slot, block_width, 0)
        visible = owners[None, :] == row_req[:, None]
        return update(carried, block_keys, block_values, visible)

    carried = lax.fori_loop(0, live_blocks, consume, initial)
    causal = (tok_req[None, :] == row_req[:, None]) & (
        jnp.arange(tokens_here, dtype=jnp.int32)[None, :] <= row_tok[:, None]
    )
    carried = update(carried, new_keys, new_values, causal)
    per_head = [
        (weighted / denominator[:, None]).reshape(tokens_here, group_size, head_dim)
        for running_max, denominator, weighted in carried
    ]
    return (
        jnp.stack(per_head, axis=1)
        .reshape(tokens_here, kv_here * group_size * head_dim)
        .astype(jnp.bfloat16)
    )


def per_device(
    queries,
    new_keys,
    new_values,
    cache_keys,
    cache_values,
    tok_req,
    cache_req,
    out_weight,
    residual,
    norm_gain,
    gate_weight,
    up_weight,
    down_weight,
):
    attended = attend(queries, new_keys, new_values, cache_keys, cache_values, tok_req, cache_req)
    partial_out = jnp.dot(
        lax.all_gather(attended, "req", axis=0, tiled=True),
        out_weight,
        preferred_element_type=jnp.float32,
    )
    mixed = lax.psum_scatter(
        partial_out.astype(jnp.bfloat16), "tp", scatter_dimension=0, tiled=True
    ).astype(jnp.float32)
    stream = (residual.astype(jnp.float32) + mixed).astype(jnp.bfloat16)
    group_count = lax.axis_size("req")
    columns = stream.shape[1]
    model_width = columns * group_count
    hidden_here = gate_weight.shape[1]
    total_tokens = stream.shape[0] * lax.axis_size("tp")
    gate_blocks = gate_weight.reshape(group_count, columns, hidden_here)
    up_blocks = up_weight.reshape(group_count, columns, hidden_here)
    own_gain = lax.dynamic_slice_in_dim(norm_gain, lax.axis_index("req") * columns, columns, 0)
    wide = stream.astype(jnp.float32)
    squares = lax.psum(jnp.sum(wide * wide, axis=1), "req")
    normed = (
        wide * lax.rsqrt(squares / model_width + epsilon)[:, None] * own_gain[None, :]
    ).astype(jnp.bfloat16)
    zeros = jnp.zeros((total_tokens, hidden_here), jnp.float32)
    shard_rows = lax.all_gather(normed, ("req", "tp"), axis=0, tiled=True)
    piece_rows = shard_rows.shape[0]
    sub_rows = math.gcd(piece_rows, total_tokens)
    sub_count = piece_rows // sub_rows
    offsets = jnp.arange(sub_count, dtype=jnp.int32) * sub_rows
    column_ids = offsets // total_tokens
    token_ids = offsets % total_tokens // sub_rows
    pieces = shard_rows.reshape(sub_count, sub_rows, columns)
    gate_part = jnp.einsum(
        "nsk,nkf->nsf", pieces, gate_blocks[column_ids], preferred_element_type=jnp.float32
    )
    up_part = jnp.einsum(
        "nsk,nkf->nsf", pieces, up_blocks[column_ids], preferred_element_type=jnp.float32
    )
    gate_sum = (
        zeros.reshape(total_tokens // sub_rows, sub_rows, hidden_here).at[token_ids].add(gate_part)
    )
    up_sum = (
        zeros.reshape(total_tokens // sub_rows, sub_rows, hidden_here).at[token_ids].add(up_part)
    )
    gate = gate_sum.reshape(total_tokens, hidden_here)
    up = up_sum.reshape(total_tokens, hidden_here)
    hidden = (jax.nn.silu(gate) * up).astype(jnp.bfloat16)
    down_blocks = down_weight.reshape(hidden_here, group_count, columns)
    sub_rows = math.gcd(
        total_tokens // lax.axis_size("tp") * lax.axis_size(("req", "tp")), total_tokens
    )
    sub_count = total_tokens // lax.axis_size("tp") * lax.axis_size(("req", "tp")) // sub_rows
    offsets = jnp.arange(sub_count, dtype=jnp.int32) * sub_rows
    column_ids = offsets // total_tokens
    token_ids = offsets % total_tokens // sub_rows
    hidden_rows = hidden.reshape(total_tokens // sub_rows, sub_rows, hidden_here)[token_ids]
    block_weights = jnp.take(down_blocks, column_ids, axis=1)
    product = jnp.einsum(
        "nsf,fnd->nsd", hidden_rows, block_weights, preferred_element_type=jnp.float32
    )
    summed = lax.psum_scatter(
        product.reshape(
            total_tokens // lax.axis_size("tp") * lax.axis_size(("req", "tp")), columns
        ),
        ("req", "tp"),
        scatter_dimension=0,
        tiled=True,
    )
    return (stream.astype(jnp.float32) + summed).astype(jnp.bfloat16)


def solution(mesh):
    in_specs = (
        P("req", "tp"),
        P("req", "tp"),
        P("req", "tp"),
        P("req", "tp"),
        P("req", "tp"),
        P("req"),
        P("req"),
        P("tp", "req"),
        P("tp", "req"),
        P(),
        P(None, ("req", "tp")),
        P(None, ("req", "tp")),
        P(("req", "tp"), None),
    )
    out_specs = P("tp", "req")
    return jax.shard_map(
        per_device, mesh=mesh, in_specs=in_specs, out_specs=out_specs, check_vma=False
    )
```

profile of v0, /device:TPU:0, one launch (start us, length us, event | category | flops | bytes accessed | tf_op | source)
XLA Modules:
  0.0 1002.1 jit_solution(370291849643179909)
XLA Ops:
  6.5 1.7 convert_reduce_fusion.1
  11.8 106.7 %while.16 = (s32[]{:T(128)}, f32[224]{0:T(256)S(1)}, f32[224]{0:T(256)S(1)}, f32[224,128]{1,0:T(8,128)S(1)}, s32[]{:T(128)}, /*index=5*/s32[17920]{0:T(1024)}, b...) while((s32[]{:T(128)}, f32[224]{0:T(256)S(1)}, ...), condition=%wide.wide.region_4.5_spmd.clone, body=%wide.wide.region_1.4_spmd.clone.sunk | while | flops 59924932 | bytes 1951559 | solution.py:68
  13.4 1.2 fusion.59
  21.9 1.2 fusion.59
  30.5 1.2 fusion.59
  39.0 1.2 fusion.59
  47.6 1.2 fusion.59
  64.6 1.2 fusion.59
  73.2 1.2 fusion.59
  90.3 1.2 fusion.59
  120.5 28.7 %all_gather.6 = bf16[512,896]{1,0:T(8,128)(2,1)S(1)} all-gather(bf16[32,896]{1,0:T(8,128)(2,1)S(1)} %convert_element_type.52), channel_id=1, replica_groups=mesh['req'=16,'tp'=8] {'req'}, dimensions={0}, use_global_device_ids=true | all-gather | bytes 974848 | tf_op jit(solution)/shard_map/all_gather | solution.py:101
  149.2 1.5 convolution_convert_fusion
  151.6 29.2 %reduce-scatter.3.cloned.1.call-done = bf16[64,448]{1,0:T(8,128)(2,1)} async-done(((bf16[512,448]{1,0:T(8,128)(2,1)}), bf16[64,448]{1,0:T(8,128)(2,1)}) %reduce-scatter.3.cloned.1.call-update) | async-done | bytes 57360 | tf_op jit(solution)/shard_map/reduce_scatter | solution.py:105
  181.7 40.5 %psum.7 = f32[64]{0:T(128)S(1)} all-reduce(f32[64]{0:T(128)S(1)} %fusion.23), channel_id=1, replica_groups=mesh['req'=16,'tp'=8] {'req'}, use_global_device_ids=true, to_apply=%region_9.10 | all-reduce | flops 64 | bytes 512 | tf_op jit(solution)/shard_map/psum | solution.py:118
  222.2 1.6 fusion.25
  224.1 4.1 reshape.172
  228.2 3.2 copy.20
  231.4 5.6 reshape.173
  237.0 4.8 copy.22
  241.8 2.2 gather_fusion
  244.1 2.5 gather_fusion.1
  246.5 5.6 reshape.174
  252.1 4.8 copy.24
  257.0 4.0 gather_fusion.2
  261.0 26.0 %all-gather.2.cloned.1.call-done = bf16[8192,448]{1,0:T(8,128)(2,1)} async-done(((bf16[64,448]{1,0:T(8,128)(2,1)}), bf16[8192,448]{1,0:T(8,128)(2,1)}) %all-gather.2.cloned.1.call-update) | async-done | bytes 7340048 | tf_op jit(solution)/shard_map/all_gather | solution.py:123
  287.0 9.5 fusion.34
  296.6 5.2 fusion.35
  301.8 6.7 scatter_fusion
  308.6 7.0 scatter_fusion.1
  315.7 8.1 fusion.9
  323.9 670.1 %reduce-scatter.5.cloned.1.call-done = f32[64,448]{1,0:T(8,128)} async-done(((f32[8192,448]{1,0:T(8,128)}), f32[64,448]{1,0:T(8,128)}) %reduce-scatter.5.cloned.1.call-update) | async-done | bytes 114704 | tf_op jit(solution)/shard_map/reduce_scatter | solution.py:159
  994.0 1.6 fusion.26
  (266 shorter events, 102.8 us)
Async XLA Ops:
  6.5 142.7 %copy-start = (bf16[896,448]{0,1:T(8,128)(2,1)S(1)}, bf16[896,448]{0,1:T(8,128)(2,1)}, u32[]{:S(2)}) copy-start(bf16[896,448]{0,1:T(8,128)(2,1)} %param.22) | copy-start | bytes 2408452
  6.5 174.2 %reduce-scatter.3.cloned.1.call-start = ((), (), s32[]{:S(2)}) async-start(), calls=%async_computation.2 | async-start | bytes 589824 | tf_op jit(solution)/shard_map/reduce_scatter | solution.py:105
  11.8 106.8 %copy-start.7 = (bf16[32,128]{1,0:T(8,128)(2,1)S(1)}, bf16[32,128]{1,0:T(8,128)(2,1)}, u32[]{:S(2)}) copy-start(bf16[32,128]{1,0:T(8,128)(2,1)} %param.16) | copy-start | bytes 24580
  11.8 108.4 %copy-start.8 = (bf16[32,128]{1,0:T(8,128)(2,1)S(1)}, bf16[32,128]{1,0:T(8,128)(2,1)}, u32[]{:S(2)}) copy-start(bf16[32,128]{1,0:T(8,128)(2,1)} %param.17) | copy-start | bytes 24580
  119.4 61.4 %copy-start.5 = (bf16[64,448]{1,0:T(8,128)(2,1)S(1)}, bf16[64,448]{1,0:T(8,128)(2,1)}, u32[]{:S(2)}) copy-start(bf16[64,448]{1,0:T(8,128)(2,1)} %param.23) | copy-start | bytes 172036
  120.4 103.6 %copy-start.4 = (bf16[7168,160]{0,1:T(8,128)(2,1)S(1)}, bf16[7168,160]{0,1:T(8,128)(2,1)}, u32[]{:S(2)}) copy-start(bf16[7168,160]{0,1:T(8,128)(2,1)} %param.25) | copy-start | bytes 6881284
  150.8 136.2 %all-gather.2.cloned.1.call-start = ((), (), s32[]{:S(2)}) async-start(), calls=%async_computation.3 | async-start | bytes 8454144 | tf_op jit(solution)/shard_map/all_gather | solution.py:123
  223.8 770.1 %reduce-scatter.5.cloned.1.call-start = ((), (), s32[]{:S(2)}) async-start(), calls=%async_computation.4 | async-start | bytes 16908288 | tf_op jit(solution)/shard_map/reduce_scatter | solution.py:159
  287.0 9.5 copy-start.2
  308.6 7.1 copy-start.3
  323.8 670.1 %copy-start.6 = (bf16[64,448]{1,0:T(8,128)(2,1)S(1)}, bf16[64,448]{1,0:T(8,128)(2,1)}, u32[]{:S(2)}) copy-start(bf16[64,448]{1,0:T(8,128)(2,1)} %reduce-scatter.3.cloned.1.call-done) | copy-start | bytes 172036
  323.9 671.7 %copy-start.1 = (bf16[896,448]{0,1:T(8,128)(2,1)S(1)}, bf16[896,448]{0,1:T(8,128)(2,1)}, u32[]{:S(2)}) copy-start(bf16[896,448]{0,1:T(8,128)(2,1)} %param.22) | copy-start | bytes 2408452
Sparse Core Ops, SparseCore 0:
  150.9 29.8 reduce-scatter.2
  223.9 63.0 all-gather.1
  324.0 669.9 reduce-scatter.4
where the time goes:
time: 1000 us
  waiting for transfers between devices  725 us (72%)
  matrix products  84.2 us (8%)
  local copies, waits for them, and re-layouts  80.5 us (8%)
  blocking collectives  69.2 us (7%)
  other arithmetic  27.3 us (3%)
  between operations  14.1 us (1%)
    reduce_scatter x1, waiting for transfers between devices, per_device(): lax.psum_scatter(product.reshape(total_tokens // lax.axis_size('tp') * la...  670 us
    psum x1, blocking collectives, per_device(): squares = lax.psum(jnp.sum(wide * wide, axis=1), 'req')  40.5 us
    dot_general x26, matrix products, update(): jnp.einsum('qd,kd->qk', query_rows, block_keys, preferred_element_type=jn...  31.3 us
    reduce_scatter x1, waiting for transfers between devices, per_device(): lax.psum_scatter(partial_out.astype(jnp.bfloat16), 'tp', scatter_dimensio...  29.2 us
    all_gather x1, blocking collectives, per_device(): lax.all_gather(attended, 'req', axis=0, tiled=True)  28.7 us
    dot_general x26, matrix products, update(): jnp.dot(weights, block_values, preferred_element_type=jnp.float32)  28.6 us
    all_gather x1, waiting for transfers between devices, per_device(): shard_rows = lax.all_gather(normed, ('req', 'tp'), axis=0, tiled=True)  26 us
  transfers between devices with their start and end apart: 3, of which 3 were waited for; matrix products, arithmetic and copies ran while one was open for 4% of the time, Pallas kernels for 0%

commit v1 on v0

--- a/solution.py
+++ b/solution.py
@@ -10,7 +10,7 @@
 
 epsilon = 1e-05
 masked_value = -1e30
-key_block = 512
+key_block = 2560
 
 
 def attend(queries, new_keys, new_values, cache_keys, cache_values, tok_req, cache_req):
@@ -106,64 +106,31 @@
         partial_out.astype(jnp.bfloat16), "tp", scatter_dimension=0, tiled=True
     ).astype(jnp.float32)
     stream = (residual.astype(jnp.float32) + mixed).astype(jnp.bfloat16)
-    group_count = lax.axis_size("req")
-    columns = stream.shape[1]
-    model_width = columns * group_count
-    hidden_here = gate_weight.shape[1]
-    total_tokens = stream.shape[0] * lax.axis_size("tp")
-    gate_blocks = gate_weight.reshape(group_count, columns, hidden_here)
-    up_blocks = up_weight.reshape(group_count, columns, hidden_here)
-    own_gain = lax.dynamic_slice_in_dim(norm_gain, lax.axis_index("req") * columns, columns, 0)
-    wide = stream.astype(jnp.float32)
-    squares = lax.psum(jnp.sum(wide * wide, axis=1), "req")
-    normed = (
-        wide * lax.rsqrt(squares / model_width + epsilon)[:, None] * own_gain[None, :]
-    ).astype(jnp.bfloat16)
-    zeros = jnp.zeros((total_tokens, hidden_here), jnp.float32)
-    shard_rows = lax.all_gather(normed, ("req", "tp"), axis=0, tiled=True)
-    piece_rows = shard_rows.shape[0]
-    sub_rows = math.gcd(piece_rows, total_tokens)
-    sub_count = piece_rows // sub_rows
-    offsets = jnp.arange(sub_count, dtype=jnp.int32) * sub_rows
-    column_ids = offsets // total_tokens
-    token_ids = offsets % total_tokens // sub_rows
-    pieces = shard_rows.reshape(sub_count, sub_rows, columns)
-    gate_part = jnp.einsum(
-        "nsk,nkf->nsf", pieces, gate_blocks[column_ids], preferred_element_type=jnp.float32
+    req_count = lax.axis_size("req")
+    tp_count = lax.axis_size("tp")
+    full_stream = lax.all_gather(
+        lax.all_gather(stream, "req", axis=1, tiled=True), "tp", axis=0, tiled=True
     )
-    up_part = jnp.einsum(
-        "nsk,nkf->nsf", pieces, up_blocks[column_ids], preferred_element_type=jnp.float32
+    wide_full = full_stream.astype(jnp.float32)
+    mean_square = jnp.mean(wide_full * wide_full, axis=1, keepdims=True)
+    normed = (wide_full * lax.rsqrt(mean_square + epsilon) * norm_gain[None, :]).astype(
+        jnp.bfloat16
     )
-    gate_sum = (
-        zeros.reshape(total_tokens // sub_rows, sub_rows, hidden_here).at[token_ids].add(gate_part)
+    gate = jnp.dot(normed, gate_weight, preferred_element_type=jnp.float32)
+    up = jnp.dot(normed, up_weight, preferred_element_type=jnp.float32)
+    hidden = (jax.nn.silu(gate) * up).astype(jnp.bfloat16)
+    total_tokens, hidden_here = hidden.shape
+    tokens_out = total_tokens // tp_count
+    columns = down_weight.shape[1] // req_count
+    product = jnp.einsum(
+        "tsh,hrf->rtsf",
+        hidden.reshape(tp_count, tokens_out, hidden_here),
+        down_weight.reshape(hidden_here, req_count, columns),
+        preferred_element_type=jnp.float32,
     )
-    up_sum = (
-        zeros.reshape(total_tokens // sub_rows, sub_rows, hidden_here).at[token_ids].add(up_part)
-    )
-    gate = gate_sum.reshape(total_tokens, hidden_here)
-    up = up_sum.reshape(total_tokens, hidden_here)
-    hidden = (jax.nn.silu(gate) * up).astype(jnp.bfloat16)
-    down_blocks = down_weight.reshape(hidden_here, group_count, columns)
-    sub_rows = math.gcd(
-        total_tokens // lax.axis_size("tp") * lax.axis_size(("req", "tp")), total_tokens
-    )
-    sub_count = total_tokens // lax.axis_size("tp") * lax.axis_size(("req", "tp")) // sub_rows
-    offsets = jnp.arange(sub_count, dtype=jnp.int32) * sub_rows
-    column_ids = offsets // total_tokens
-    token_ids = offsets % total_tokens // sub_rows
-    hidden_rows = hidden.reshape(total_tokens // sub_rows, sub_rows, hidden_here)[token_ids]
-    block_weights = jnp.take(down_blocks, column_ids, axis=1)
-    product = jnp.einsum(
-        "nsf,fnd->nsd", hidden_rows, block_weights, preferred_element_type=jnp.float32
-    )
-    summed = lax.psum_scatter(
-        product.reshape(
-            total_tokens // lax.axis_size("tp") * lax.axis_size(("req", "tp")), columns
-        ),
-        ("req", "tp"),
-        scatter_dimension=0,
-        tiled=True,
-    )
+    pieces = product.astype(jnp.bfloat16).reshape(req_count * tp_count, tokens_out, columns)
+    received = lax.all_to_all(pieces, ("req", "tp"), 0, 0, tiled=True)
+    summed = jnp.sum(received.astype(jnp.float32), axis=0)
     return (stream.astype(jnp.float32) + summed).astype(jnp.bfloat16)
 
 

time: 1000 us -> 322 us (0.32)
  waiting for transfers between devices: 725 us -> 67.3 us
  blocking collectives: 69.2 us -> 186 us
  matrix products: 84.2 us -> 21.4 us
  local copies, waits for them, and re-layouts: 80.5 us -> 21.2 us
  other arithmetic: 27.3 us -> 10.8 us
    reduce_scatter x1 -> x0, waiting for transfers between devices: 670 us -> none  [per_device(): lax.psum_scatter(product.reshape(total_tokens // lax.axis_size('tp') * la...]
    all_to_all x0 -> x1, blocking collectives: none -> 107 us  [per_device(): received = lax.all_to_all(pieces, ('req', 'tp'), 0, 0, tiled=True)]
    psum x1 -> x0, blocking collectives: 40.5 us -> none  [per_device(): squares = lax.psum(jnp.sum(wide * wide, axis=1), 'req')]
    dot_general x26 -> x2, matrix products: 31.3 us -> 2.56 us  [update(): jnp.einsum('qd,kd->qk', query_rows, block_keys, preferred_element_type=jn...]
    dot_general x26 -> x2, matrix products: 28.6 us -> 1.77 us  [update(): jnp.dot(weights, block_values, preferred_element_type=jnp.float32)]
    all_gather x1, blocking collectives: 28.7 us -> 53.9 us  [per_device(): lax.all_gather(attended, 'req', axis=0, tiled=True)]
    all_gather x0 -> x1, blocking collectives: none -> 25.1 us  [per_device(): lax.all_gather(stream, 'req', axis=1, tiled=True)]
    reshape x6 -> x2, local copies, waits for them, and re-layouts: 28.2 us -> 5.9 us  [the longest x1 5.76 us: per_device(): down_weight.reshape(hidden_here, req_count, columns)]
  transfers between devices with their start and end apart: 3 -> 2, of which waited for: 3 -> 2; matrix products, arithmetic and copies ran while one was open for 4% -> 2% of each run, Pallas kernels for 0% -> 0%
where the time goes in v1:
time: 322 us; the launch traced here: 321 us
  blocking collectives  186 us (58%)
  waiting for transfers between devices  67.3 us (21%)
  matrix products  21.4 us (7%)
  local copies, waits for them, and re-layouts  21.2 us (7%)
  between operations  14.3 us (4%)
  other arithmetic  10.8 us (3%)
    all_to_all x1, blocking collectives, per_device(): received = lax.all_to_all(pieces, ('req', 'tp'), 0, 0, tiled=True)  107 us
    all_gather x1, blocking collectives, per_device(): lax.all_gather(attended, 'req', axis=0, tiled=True)  53.9 us
    all_gather x1, waiting for transfers between devices, per_device(): lax.all_gather(lax.all_gather(stream, 'req', axis=1, tiled=True), 'tp', a...  36.5 us
    reduce_scatter x1, waiting for transfers between devices, per_device(): lax.psum_scatter(partial_out.astype(jnp.bfloat16), 'tp', scatter_dimensio...  30.8 us
    all_gather x1, blocking collectives, per_device(): lax.all_gather(stream, 'req', axis=1, tiled=True)  25.1 us
    dot_general x1, matrix products, per_device(): jnp.einsum('tsh,hrf->rtsf', hidden.reshape(tp_count, tokens_out, hidden_h...  9.04 us
    convert_element_type x1, local copies, waits for them, and re-layouts, per_device(): product.astype(jnp.bfloat16)  7.71 us
  transfers between devices with their start and end apart: 2, of which 2 were waited for; matrix products, arithmetic and copies ran while one was open for 2% of the time, Pallas kernels for 0%

profile of v1, /device:TPU:0, one launch (start us, length us, event | category | flops | bytes accessed | tf_op | source)
XLA Modules:
  0.0 320.7 jit_solution(12591843233111964548)
XLA Ops:
  6.5 1.7 convert_reduce_fusion.2
  8.9 0.9 reshape_squeeze_reshape.3
  9.8 0.9 squeeze_reshape.4
  10.7 0.7 broadcast_in_dim.42
  11.7 5.6 %while.16 = (s32[]{:T(128)}, f32[224]{0:T(256)S(1)}, f32[224]{0:T(256)S(1)}, f32[224,128]{1,0:T(8,128)S(1)}, s32[]{:T(128)}, /*index=5*/s32[17920]{0:T(1024)}, b...) while((s32[]{:T(128)}, f32[224]{0:T(256)S(1)}, ...), condition=%wide.wide.region_4.5_spmd.clone, body=%wide.wide.region_1.4_spmd.clone.sunk | while | flops 299393472 | bytes 8537927 | solution.py:68
  11.8 0.8 dynamic_slice.26
  12.6 0.7 broadcast_in_dim.60
  13.4 1.7 fusion.54
  15.1 0.6 convert_reduce_fusion.6
  15.8 1.6 convolution_add_fusion.4
  17.4 0.9 fusion.31
  18.3 0.7 convert_reduce_fusion.3
  19.0 0.2 fusion.25
  19.3 53.9 %all_gather.9 = bf16[512,896]{1,0:T(8,128)(2,1)S(1)} all-gather(bf16[32,896]{1,0:T(8,128)(2,1)S(1)} %convert_element_type.62), channel_id=1, replica_groups=mesh['req'=16,'tp'=8] {'req'}, dimensions={0}, use_global_device_ids=true | all-gather | bytes 974848 | tf_op jit(solution)/shard_map/all_gather | solution.py:101
  73.2 2.7 convolution_convert_fusion
  75.9 30.8 %reduce-scatter.2.cloned.1.call-done = bf16[64,448]{1,0:T(8,128)(2,1)} async-done(((bf16[512,448]{1,0:T(8,128)(2,1)}), bf16[64,448]{1,0:T(8,128)(2,1)}) %reduce-scatter.2.cloned.1.call-update) | async-done | bytes 57360 | tf_op jit(solution)/shard_map/reduce_scatter | solution.py:105
  106.8 0.9 fusion.28
  107.6 25.1 %all-gather = bf16[16,448,64]{1,2,0:T(8,128)(2,1)S(1)} all-gather(bf16[1,448,64]{1,2,0:T(8,128)(2,1)S(1)} %fusion.28), channel_id=1, replica_groups=mesh['req'=16,'tp'=8] {'req'}, dimensions={0}, use_global_device_ids=true | all-gather | bytes 974848 | tf_op jit(solution)/shard_map/all_gather | solution.py:112
  132.7 0.6 copy.20
  133.3 2.1 reshape.33
  135.4 5.8 %reshape.30 = bf16[160,16,448]{2,1,0:T(8,128)(2,1)} reshape(bf16[160,7168]{1,0:T(8,128)(2,1)} %param.27) | data formatting | bytes 4587520 | tf_op jit(solution)/shard_map/reshape | solution.py:128
  141.2 36.5 %all-gather.3.cloned.1.call-done = bf16[512,7168]{1,0:T(8,128)(2,1)} async-done(((bf16[64,7168]{1,0:T(8,128)(2,1)}), bf16[512,7168]{1,0:T(8,128)(2,1)}) %all-gather.3.cloned.1.call-update) | async-done | bytes 7340048 | tf_op jit(solution)/shard_map/all_gather | solution.py:111
  177.6 4.7 %fusion.9 = f32[512]{0:T(512)S(1)} fusion(bf16[512,7168]{1,0:T(8,128)(2,1)} %all-gather.3.cloned.1.call-done), kind=kLoop, calls=%fused_computation.17 | loop fusion | flops 11009536 | bytes 7342080 | tf_op jit(solution)/shard_map/reduce_sum | solution.py:115
  182.4 0.4 copy-done.1
  182.8 2.6 fusion.16
  185.5 2.7 fusion.21
  188.2 0.1 copy.25
  188.3 9.0 %convert_bitcast_fusion = bf16[16,8,64,448]{3,2,0,1:T(8,128)(2,1)} fusion(bf16[8,64,160,1]{2,1,3,0:T(8,128)(2,1)S(1)} %bitcast.41, bf16[160,16,448]{2,1,0:T(8,128)(2,1)} %reshape.30), kind=kOutput, calls=%fused_computation.20 | convolution fusion | flops 1178075136 | bytes 9797632 | tf_op jit(solution)/shard_map/tsh,hrf->rtsf/dot_general | solution.py:125
  197.4 7.7 %copy.23 = bf16[16,8,64,448]{3,2,1,0:T(8,128)(2,1)} copy(bf16[16,8,64,448]{3,2,0,1:T(8,128)(2,1)} %convert_bitcast_fusion) | data formatting | bytes 14680064 | tf_op jit(solution)/shard_map/convert_element_type | solution.py:131
  205.1 106.7 %all_to_all.5 = bf16[128,64,448]{2,1,0:T(8,128)(2,1)S(1)} all-to-all(bf16[128,64,448]{2,1,0:T(8,128)(2,1)} %bitcast.39), channel_id=1, replica_groups=mesh['req'=16,'tp'=8] {'req','tp'}, dimensions={0} | all-to-all | bytes 14680064 | tf_op jit(solution)/shard_map/all_to_all | solution.py:132
  311.7 1.5 convert_reduce_fusion.1
  313.2 0.7 add_convert_fusion
  (33 shorter events, 0.6 us)
Async XLA Ops:
  6.5 175.9 %copy-start = (bf16[7168,160]{0,1:T(8,128)(2,1)S(1)}, bf16[7168,160]{0,1:T(8,128)(2,1)}, u32[]{:S(2)}) copy-start(bf16[7168,160]{0,1:T(8,128)(2,1)} %param.25) | copy-start | bytes 6881284
  6.5 100.2 %reduce-scatter.2.cloned.1.call-start = ((), (), s32[]{:S(2)}) async-start(), calls=%async_computation.2 | async-start | bytes 589824 | tf_op jit(solution)/shard_map/reduce_scatter | solution.py:105
  11.7 5.6 %copy-start.6 = (bf16[32,128]{1,0:T(8,128)(2,1)S(1)}, bf16[32,128]{1,0:T(8,128)(2,1)}, u32[]{:S(2)}) copy-start(bf16[32,128]{1,0:T(8,128)(2,1)} %param.16) | copy-start | bytes 24580
  11.7 7.3 %copy-start.7 = (bf16[32,128]{1,0:T(8,128)(2,1)S(1)}, bf16[32,128]{1,0:T(8,128)(2,1)}, u32[]{:S(2)}) copy-start(bf16[32,128]{1,0:T(8,128)(2,1)} %param.17) | copy-start | bytes 24580
  17.4 89.4 %copy-start.2 = (bf16[64,448]{1,0:T(8,128)(2,1)S(1)}, bf16[64,448]{1,0:T(8,128)(2,1)}, u32[]{:S(2)}) copy-start(bf16[64,448]{1,0:T(8,128)(2,1)} %param.23) | copy-start | bytes 172036
  75.9 101.7 %all-gather.3.cloned.1.call-start = ((), (), s32[]{:S(2)}) async-start(), calls=%async_computation.3 | async-start | bytes 8257536 | tf_op jit(solution)/shard_map/all_gather | solution.py:111
  135.4 47.0 %copy-start.5 = (f32[7168]{0:T(1024)S(1)}, f32[7168]{0:T(1024)}, u32[]{:S(2)}) copy-start(f32[7168]{0:T(1024)} %param.24) | copy-start | bytes 86020
  177.6 5.2 %copy-start.1 = (bf16[512,7168]{1,0:T(8,128)(2,1)S(1)}, bf16[512,7168]{1,0:T(8,128)(2,1)}, u32[]{:S(2)}) copy-start(bf16[512,7168]{1,0:T(8,128)(2,1)} %all-gather.3.cloned.1.call-done) | copy-start | bytes 22020100
  182.8 2.7 copy-start.4
  311.7 1.5 copy-start.3
Sparse Core Ops, SparseCore 0:
  76.0 30.6 reduce-scatter.1
  135.5 42.0 all-gather.2

commit v2 on v1

--- a/solution.py
+++ b/solution.py
@@ -96,6 +96,10 @@
     up_weight,
     down_weight,
 ):
+    swap = [(0, 1), (1, 0)]
+    gate_partner = lax.ppermute(gate_weight, "core", swap)
+    up_partner = lax.ppermute(up_weight, "core", swap)
+    down_partner = lax.ppermute(down_weight, "core", swap)
     attended = attend(queries, new_keys, new_values, cache_keys, cache_values, tok_req, cache_req)
     partial_out = jnp.dot(
         lax.all_gather(attended, "req", axis=0, tiled=True),
@@ -103,54 +107,69 @@
         preferred_element_type=jnp.float32,
     )
     mixed = lax.psum_scatter(
-        partial_out.astype(jnp.bfloat16), "tp", scatter_dimension=0, tiled=True
+        partial_out.astype(jnp.bfloat16), ("y", "core"), scatter_dimension=0, tiled=True
     ).astype(jnp.float32)
     stream = (residual.astype(jnp.float32) + mixed).astype(jnp.bfloat16)
     req_count = lax.axis_size("req")
-    tp_count = lax.axis_size("tp")
-    full_stream = lax.all_gather(
-        lax.all_gather(stream, "req", axis=1, tiled=True), "tp", axis=0, tiled=True
+    y_count = lax.axis_size("y")
+    tokens_out, columns = stream.shape
+    gathered = lax.all_gather(stream, ("req", "y"), axis=0, tiled=True)
+    side_stream = (
+        gathered.reshape(req_count, y_count, tokens_out, columns)
+        .transpose(1, 2, 0, 3)
+        .reshape(y_count * tokens_out, req_count * columns)
     )
-    wide_full = full_stream.astype(jnp.float32)
-    mean_square = jnp.mean(wide_full * wide_full, axis=1, keepdims=True)
-    normed = (wide_full * lax.rsqrt(mean_square + epsilon) * norm_gain[None, :]).astype(
+    wide_side = side_stream.astype(jnp.float32)
+    mean_square = jnp.mean(wide_side * wide_side, axis=1, keepdims=True)
+    normed = (wide_side * lax.rsqrt(mean_square + epsilon) * norm_gain[None, :]).astype(
         jnp.bfloat16
     )
-    gate = jnp.dot(normed, gate_weight, preferred_element_type=jnp.float32)
-    up = jnp.dot(normed, up_weight, preferred_element_type=jnp.float32)
-    hidden = (jax.nn.silu(gate) * up).astype(jnp.bfloat16)
-    total_tokens, hidden_here = hidden.shape
-    tokens_out = total_tokens // tp_count
-    columns = down_weight.shape[1] // req_count
-    product = jnp.einsum(
-        "tsh,hrf->rtsf",
-        hidden.reshape(tp_count, tokens_out, hidden_here),
-        down_weight.reshape(hidden_here, req_count, columns),
-        preferred_element_type=jnp.float32,
+
+    def hidden_of(gate_w, up_w):
+        gate = jnp.dot(normed, gate_w, preferred_element_type=jnp.float32)
+        up = jnp.dot(normed, up_w, preferred_element_type=jnp.float32)
+        hidden = (jax.nn.silu(gate) * up).astype(jnp.bfloat16)
+        return hidden.reshape(y_count, tokens_out, hidden.shape[1])
+
+    def down_of(hidden, down_w):
+        return jnp.einsum(
+            "ysh,hrf->rysf",
+            hidden,
+            down_w.reshape(down_w.shape[0], req_count, columns),
+            preferred_element_type=jnp.float32,
+        )
+
+    product = down_of(hidden_of(gate_weight, up_weight), down_weight) + down_of(
+        hidden_of(gate_partner, up_partner), down_partner
     )
-    pieces = product.astype(jnp.bfloat16).reshape(req_count * tp_count, tokens_out, columns)
-    received = lax.all_to_all(pieces, ("req", "tp"), 0, 0, tiled=True)
+    pieces = product.astype(jnp.bfloat16).reshape(req_count * y_count, tokens_out, columns)
+    received = lax.all_to_all(pieces, ("req", "y"), 0, 0, tiled=True)
     summed = jnp.sum(received.astype(jnp.float32), axis=0)
     return (stream.astype(jnp.float32) + summed).astype(jnp.bfloat16)
 
 
 def solution(mesh):
+    req_count, tp_count = mesh.devices.shape
+    split = jax.sharding.Mesh(
+        mesh.devices.reshape(req_count, tp_count // 2, 2), ("req", "y", "core")
+    )
+    tp = ("y", "core")
     in_specs = (
-        P("req", "tp"),
-        P("req", "tp"),
-        P("req", "tp"),
-        P("req", "tp"),
-        P("req", "tp"),
+        P("req", tp),
+        P("req", tp),
+        P("req", tp),
+        P("req", tp),
+        P("req", tp),
         P("req"),
         P("req"),
-        P("tp", "req"),
-        P("tp", "req"),
+        P(tp, "req"),
+        P(tp, "req"),
         P(),
-        P(None, ("req", "tp")),
-        P(None, ("req", "tp")),
-        P(("req", "tp"), None),
+        P(None, ("req",) + tp),
+        P(None, ("req",) + tp),
+        P(("req",) + tp, None),
     )
-    out_specs = P("tp", "req")
+    out_specs = P(tp, "req")
     return jax.shard_map(
-        per_device, mesh=mesh, in_specs=in_specs, out_specs=out_specs, check_vma=False
+        per_device, mesh=split, in_specs=in_specs, out_specs=out_specs, check_vma=False
     )

time: 322 us -> 290 us (0.901)
  blocking collectives: 186 us -> 103 us
  waiting for transfers between devices: 67.3 us -> 90.2 us
  local copies, waits for them, and re-layouts: 21.2 us -> 34.6 us
  matrix products: 21.4 us -> 30.9 us
    all_to_all x1, blocking collectives: 107 us -> 57.7 us  [per_device(): received = lax.all_to_all(pieces, ('req', 'y'), 0, 0, tiled=True)]
    all_gather x1 -> x0, blocking collectives: 25.1 us -> none  [per_device(): lax.all_gather(stream, 'req', axis=1, tiled=True)]
    all_gather x1, waiting for transfers between devices: 36.5 us -> 58 us  [per_device(): gathered = lax.all_gather(stream, ('req', 'y'), axis=0, tiled=True)]
    convert_element_type x0 -> x4, local copies, waits for them, and re-layouts: none -> 17.8 us  [the longest x2 17.6 us: per_device(): wide_side = side_stream.astype(jnp.float32)]
    all_gather x1, blocking collectives: 53.9 us -> 45.7 us  [per_device(): lax.all_gather(attended, 'req', axis=0, tiled=True)]
    dot_general x3 -> x6, matrix products: 14.4 us -> 21.8 us  [the longest x2 7.36 us: hidden_of(): gate = jnp.dot(normed, gate_w, preferred_element_type=jnp.float32)]
    convert_element_type x1, local copies, waits for them, and re-layouts: 7.71 us -> 0.27 us  [per_device(): product.astype(jnp.bfloat16)]
    convert_element_type x0 -> x2, other arithmetic: none -> 5.53 us  [the longest x1 4.05 us: per_device(): (wide_side * lax.rsqrt(mean_square + epsilon) * norm_gain[None, :]).astyp...]
  transfers between devices with their start and end apart: 2 -> 5, of which waited for: 2 -> 2; matrix products, arithmetic and copies ran while one was open for 2% -> 15% of each run, Pallas kernels for 0% -> 0%
where the time goes in v2:
time: 290 us; the launch traced here: 288 us
  blocking collectives  103 us (36%)
  waiting for transfers between devices  90.2 us (31%)
  local copies, waits for them, and re-layouts  34.6 us (12%)
  matrix products  30.9 us (11%)
  between operations  14.3 us (5%)
  other arithmetic  13.7 us (5%)
    all_gather x1, waiting for transfers between devices, per_device(): gathered = lax.all_gather(stream, ('req', 'y'), axis=0, tiled=True)  58 us
    all_to_all x1, blocking collectives, per_device(): received = lax.all_to_all(pieces, ('req', 'y'), 0, 0, tiled=True)  57.7 us
    all_gather x1, blocking collectives, per_device(): lax.all_gather(attended, 'req', axis=0, tiled=True)  45.7 us
    reduce_scatter x1, waiting for transfers between devices, per_device(): lax.psum_scatter(partial_out.astype(jnp.bfloat16), ('y', 'core'), scatter...  32.1 us
    convert_element_type x2, local copies, waits for them, and re-layouts, per_device(): wide_side = side_stream.astype(jnp.float32)  17.6 us
    reshape x2, local copies, waits for them, and re-layouts, down_of(): down_w.reshape(down_w.shape[0], req_count, columns)  10 us
    dot_general x2, matrix products, hidden_of(): gate = jnp.dot(normed, gate_w, preferred_element_type=jnp.float32)  7.36 us
    dot_general x2, matrix products, down_of(): jnp.einsum('ysh,hrf->rysf', hidden, down_w.reshape(down_w.shape[0], req_c...  7.33 us
  transfers between devices with their start and end apart: 5, of which 2 were waited for; matrix products, arithmetic and copies ran while one was open for 15% of the time, Pallas kernels for 0%

profile of v2, /device:TPU:0, one launch (start us, length us, event | category | flops | bytes accessed | tf_op | source)
XLA Modules:
  0.0 288.0 jit_solution(1208514780844075841)
XLA Ops:
  6.5 1.6 convert_reduce_fusion.2
  8.8 0.9 squeeze_reshape.4
  9.7 0.9 reshape_squeeze_reshape.3
  10.7 11.2 %while.16 = (s32[]{:T(128)}, f32[224]{0:T(256)S(1)}, f32[224]{0:T(256)S(1)}, f32[224,128]{1,0:T(8,128)S(1)}, s32[]{:T(128)}, /*index=5*/s32[17920]{0:T(1024)}, b...) while((s32[]{:T(128)}, f32[224]{0:T(256)S(1)}, ...), condition=%wide.wide.region_4.5_spmd.clone, body=%wide.wide.region_1.4_spmd.clone.sunk | while | flops 299393472 | bytes 8537927 | solution.py:68
  10.7 0.8 dynamic_slice.26
  11.5 0.7 broadcast_in_dim.60
  12.4 1.7 fusion.54
  14.7 1.6 convolution_add_fusion.4
  16.3 0.8 dynamic_slice.26
  18.0 1.7 fusion.54
  20.3 1.6 convolution_add_fusion.4
  21.9 0.7 broadcast_in_dim.42
  22.9 0.9 fusion.22
  23.8 0.7 convert_reduce_fusion.3
  24.9 45.7 %all_gather.6 = bf16[512,896]{1,0:T(8,128)(2,1)S(1)} all-gather(bf16[32,896]{1,0:T(8,128)(2,1)S(1)} %convert_element_type.79), channel_id=1, replica_groups=mesh['req'=16,'y'=4,'core'=2] {'req'}, dimensions={0}, use_global_device_ids=true | all-gather | bytes 974848 | tf_op jit(solution)/shard_map/all_gather | solution.py:105
  70.5 1.5 convolution_convert_fusion
  72.1 32.1 %reduce-scatter.2.cloned.1.call-done = bf16[64,448]{1,0:T(8,128)(2,1)} async-done(((bf16[512,448]{1,0:T(8,128)(2,1)}), bf16[64,448]{1,0:T(8,128)(2,1)}) %reduce-scatter.2.cloned.1.call-update) | async-done | bytes 57360 | tf_op jit(solution)/shard_map/reduce_scatter | solution.py:109
  104.2 1.5 add_convert_fusion.2
  106.4 4.5 %reshape.54 = bf16[160,16,448]{2,1,0:T(8,128)(2,1)S(1)} reshape(bf16[160,7168]{1,0:T(8,128)(2,1)} %param.27) | data formatting | bytes 4587520 | tf_op jit(solution)/shard_map/reshape | solution.py:138
  110.9 5.6 %reshape.56 = bf16[160,16,448]{2,1,0:T(8,128)(2,1)} reshape(bf16[160,7168]{1,0:T(8,128)(2,1)} %collective-permute-done.2) | data formatting | bytes 4587520 | tf_op jit(solution)/shard_map/reshape | solution.py:138
  116.5 58.0 %all-gather.2.cloned.1.call-done = bf16[4096,448]{1,0:T(8,128)(2,1)} async-done(((bf16[64,448]{1,0:T(8,128)(2,1)}), bf16[4096,448]{1,0:T(8,128)(2,1)}) %all-gather.2.cloned.1.call-update) | async-done | bytes 3670032 | tf_op jit(solution)/shard_map/all_gather | solution.py:116
  174.5 3.1 %multiply_reduce_fusion = f32[4096]{0:T(1024)S(1)} fusion(bf16[4096,448]{1,0:T(8,128)(2,1)} %all-gather.2.cloned.1.call-done), kind=kLoop, calls=%fused_computation.17 | loop fusion | flops 5500928 | bytes 3686400 | tf_op jit(solution)/shard_map/reduce_sum | solution.py:123
  177.8 7.9 %copy.48 = f32[16,4,64,448]{3,0,2,1:T(8,128)} copy(bf16[16,4,64,448]{3,2,1,0:T(8,128)(2,1)} %bitcast.55) | data formatting | bytes 11010048 | tf_op jit(solution)/shard_map/convert_element_type | solution.py:122
  185.7 9.7 %reshape.58 = f32[256,7168]{1,0:T(8,128)} reshape(f32[4,64,16,448]{3,2,1,0:T(8,128)} %bitcast.54) | data formatting | bytes 14680064 | tf_op jit(solution)/shard_map/convert_element_type | solution.py:122
  195.4 4.0 %multiply_convert_fusion = bf16[256,7168]{1,0:T(8,128)(2,1)S(1)} fusion(f32[256,7168]{1,0:T(8,128)} %reshape.58, f32[7168]{0:T(1024)S(1)} %copy-done.6, f32[256]{0:T(256)S(1)} %rsqrt.12), kind=kLoop, calls=%fused_computation.18 | loop fusion | flops 5505024 | bytes 11039744 | tf_op jit(solution)/shard_map/convert_element_type | solution.py:124
  199.5 4.3 %fusion.23 = f32[256,160]{0,1:T(8,128)S(1)} fusion(bf16[256,7168]{1,0:T(8,128)(2,1)S(1)} %multiply_convert_fusion, bf16[7168,160]{0,1:T(8,128)(2,1)} %param.25), kind=kOutput, calls=%fused_computation.46 | convolution fusion | flops 587202560 | bytes 6127616 | tf_op jit(solution)/shard_map/dot_general | solution.py:129
  203.9 3.0 %fusion.24 = f32[256,160]{0,1:T(8,128)S(1)} fusion(bf16[256,7168]{1,0:T(8,128)(2,1)S(1)} %multiply_convert_fusion, bf16[7168,160]{0,1:T(8,128)(2,1)} %collective-permute-done), kind=kOutput, calls=%fused_computation.47 | convolution fusion | flops 587202560 | bytes 6127616 | tf_op jit(solution)/shard_map/dot_general | solution.py:129
  206.9 3.0 %multiply_convert_fusion.1 = bf16[256,160]{0,1:T(8,128)(2,1)S(1)} fusion(f32[256,160]{0,1:T(8,128)S(1)} %fusion.24, bf16[256,7168]{1,0:T(8,128)(2,1)S(1)} %multiply_convert_fusion, bf16[7168,160]{0,1:T(8,128)(2,1)} %collective-permute-done.1), kind=kOutput, calls=%fused_computation.33 | convolution fusion | flops 587448320 | bytes 6209536 | tf_op jit(solution)/shard_map/dot_general | solution.py:130
  210.0 4.1 %fusion.15 = bf16[256,160]{0,1:T(8,128)(2,1)S(1)} fusion(bf16[256,7168]{1,0:T(8,128)(2,1)} %copy-done.2, bf16[7168,160]{0,1:T(8,128)(2,1)} %param.26, f32[256,160]{0,1:T(8,128)S(1)} %fusion.23), kind=kOutput, calls=%fused_computation.27 | convolution fusion | flops 587448320 | bytes 6209536 | tf_op jit(solution)/shard_map/dot_general | solution.py:130
  214.3 3.6 %fusion.11 = f32[4,64,16,448]{3,1,2,0:T(8,128)S(1)} fusion(bf16[4,64,160,1]{2,1,3,0:T(8,128)(2,1)S(1)} %bitcast.58, bf16[160,16,448]{2,1,0:T(8,128)(2,1)S(1)} %reshape.54), kind=kOutput, calls=%fused_computation.21 | convolution fusion | flops 587202560 | bytes 9715712 | tf_op jit(solution)/shard_map/ysh,hrf->rysf/dot_general | solution.py:135
  217.9 3.7 %fusion.9 = bf16[16,4,64,448]{3,2,0,1:T(8,128)(2,1)S(1)} fusion(f32[4,64,16,448]{3,1,2,0:T(8,128)S(1)} %fusion.11, bf16[4,64,160,1]{2,1,3,0:T(8,128)(2,1)S(1)} %bitcast.57, bf16[160,16,448]{2,1,0:T(8,128)(2,1)S(1)} %copy-done.3), kind=kOutput, calls=%fused_computation.19 | convolution fusion | flops 590872576 | bytes 13385728 | tf_op jit(solution)/shard_map/ysh,hrf->rysf/dot_general | solution.py:135
  221.9 57.7 %all_to_all.5 = bf16[64,64,448]{2,1,0:T(8,128)(2,1)S(1)} all-to-all(bf16[64,64,448]{2,1,0:T(8,128)(2,1)S(1)} %bitcast.56), channel_id=1, replica_groups=mesh['req'=16,'y'=4,'core'=2] {'req','y'}, dimensions={0} | all-to-all | bytes 7340032 | tf_op jit(solution)/shard_map/all_to_all | solution.py:146
  (58 shorter events, 5.8 us)
Async XLA Ops:
  6.5 64.0 %copy-start = (bf16[896,448]{0,1:T(8,128)(2,1)S(1)}, bf16[896,448]{0,1:T(8,128)(2,1)}, u32[]{:S(2)}) copy-start(bf16[896,448]{0,1:T(8,128)(2,1)} %param.22) | copy-start | bytes 2408452
  6.5 97.7 %reduce-scatter.2.cloned.1.call-start = ((), (), s32[]{:S(2)}) async-start(), calls=%async_computation.2 | async-start | bytes 589824 | tf_op jit(solution)/shard_map/reduce_scatter | solution.py:109
  10.7 12.2 %copy-start.7 = (bf16[32,128]{1,0:T(8,128)(2,1)S(1)}, bf16[32,128]{1,0:T(8,128)(2,1)}, u32[]{:S(2)}) copy-start(bf16[32,128]{1,0:T(8,128)(2,1)} %param.16) | copy-start | bytes 24580
  10.7 13.9 %copy-start.8 = (bf16[32,128]{1,0:T(8,128)(2,1)S(1)}, bf16[32,128]{1,0:T(8,128)(2,1)}, u32[]{:S(2)}) copy-start(bf16[32,128]{1,0:T(8,128)(2,1)} %param.17) | copy-start | bytes 24580
  22.9 81.4 %copy-start.5 = (bf16[64,448]{1,0:T(8,128)(2,1)S(1)}, bf16[64,448]{1,0:T(8,128)(2,1)}, u32[]{:S(2)}) copy-start(bf16[64,448]{1,0:T(8,128)(2,1)} %param.23) | copy-start | bytes 172036
  72.1 102.4 %all-gather.2.cloned.1.call-start = ((), (), s32[]{:S(2)}) async-start(), calls=%async_computation.3 | async-start | bytes 4259840 | tf_op jit(solution)/shard_map/all_gather | solution.py:116
  105.7 5.1 %collective-permute-start.2 = (bf16[160,7168]{1,0:T(8,128)(2,1)}, bf16[160,7168]{1,0:T(8,128)(2,1)}, u32[]{:S(2)}, u32[]{:S(2)}) collective-permute-start(bf16[160,7168]{1,0:T(8,128)(2,1)} %param.27), channel_id=1, source_target_pairs={{0,1},{1,0},{2,3},{3,2},{4,5},{5,4},{6,7},{7,6},{8,9},{9,8},{10,11... | collective-permute-start | bytes 6881288 | tf_op jit(solution)/shard_map/ppermute | solution.py:102
  105.8 98.0 %collective-permute-start = (bf16[7168,160]{0,1:T(8,128)(2,1)}, bf16[7168,160]{0,1:T(8,128)(2,1)}, u32[]{:S(2)}, u32[]{:S(2)}) collective-permute-start(bf16[7168,160]{0,1:T(8,128)(2,1)} %param.25), channel_id=1, source_target_pairs={{0,1},{1,0},{2,3},{3,2},{4,5},{5,4},{6,7},{7,6},{8,9},{9,8},{10,11... | collective-permute-start | bytes 6881288 | tf_op jit(solution)/shard_map/ppermute | solution.py:100
  106.3 100.5 %collective-permute-start.1 = (bf16[7168,160]{0,1:T(8,128)(2,1)}, bf16[7168,160]{0,1:T(8,128)(2,1)}, u32[]{:S(2)}, u32[]{:S(2)}) collective-permute-start(bf16[7168,160]{0,1:T(8,128)(2,1)} %param.26), channel_id=1, source_target_pairs={{0,1},{1,0},{2,3},{3,2},{4,5},{5,4},{6,7},{7,6},{8,9},{9,8},{10,11... | collective-permute-start | bytes 6881288 | tf_op jit(solution)/shard_map/ppermute | solution.py:101
  185.7 9.8 %copy-start.6 = (f32[7168]{0:T(1024)S(1)}, f32[7168]{0:T(1024)}, u32[]{:S(2)}) copy-start(f32[7168]{0:T(1024)} %param.24) | copy-start | bytes 86020
  199.5 7.4 %copy-start.2 = (bf16[256,7168]{1,0:T(8,128)(2,1)}, bf16[256,7168]{1,0:T(8,128)(2,1)S(1)}, u32[]{:S(2)}) copy-start(bf16[256,7168]{1,0:T(8,128)(2,1)S(1)} %multiply_convert_fusion) | copy-start | bytes 11010052
  214.3 3.6 %copy-start.3 = (bf16[160,16,448]{2,1,0:T(8,128)(2,1)S(1)}, bf16[160,16,448]{2,1,0:T(8,128)(2,1)}, u32[]{:S(2)}) copy-start(bf16[160,16,448]{2,1,0:T(8,128)(2,1)} %reshape.56) | copy-start | bytes 6881284
  221.9 59.2 %copy-start.1 = (bf16[896,448]{0,1:T(8,128)(2,1)S(1)}, bf16[896,448]{0,1:T(8,128)(2,1)}, u32[]{:S(2)}) copy-start(bf16[896,448]{0,1:T(8,128)(2,1)} %param.22) | copy-start | bytes 2408452
  279.7 0.8 copy-start.4
Sparse Core Ops, SparseCore 0:
  72.2 31.9 reduce-scatter.1
  107.1 67.3 all-gather.1

commit v3 on v2

--- a/solution.py
+++ b/solution.py
@@ -113,11 +113,8 @@
     req_count = lax.axis_size("req")
     y_count = lax.axis_size("y")
     tokens_out, columns = stream.shape
-    gathered = lax.all_gather(stream, ("req", "y"), axis=0, tiled=True)
-    side_stream = (
-        gathered.reshape(req_count, y_count, tokens_out, columns)
-        .transpose(1, 2, 0, 3)
-        .reshape(y_count * tokens_out, req_count * columns)
+    side_stream = lax.all_gather(
+        lax.all_gather(stream, "req", axis=1, tiled=True), "y", axis=0, tiled=True
     )
     wide_side = side_stream.astype(jnp.float32)
     mean_square = jnp.mean(wide_side * wide_side, axis=1, keepdims=True)

time: 290 us -> 272 us (0.938)
  blocking collectives: 103 us -> 132 us
  waiting for transfers between devices: 90.2 us -> 62.2 us
  local copies, waits for them, and re-layouts: 34.6 us -> 24.4 us
  other arithmetic: 13.7 us -> 9.93 us
  matrix products: 30.9 us -> 27.7 us
    all_gather x1, waiting for transfers between devices: 58 us -> 30 us  [per_device(): lax.all_gather(lax.all_gather(stream, 'req', axis=1, tiled=True), 'y', ax...]
    all_gather x0 -> x1, blocking collectives: none -> 25 us  [per_device(): lax.all_gather(stream, 'req', axis=1, tiled=True)]
    convert_element_type x2 -> x0, local copies, waits for them, and re-layouts: 17.6 us -> none  [per_device(): wide_side = side_stream.astype(jnp.float32)]
    unnamed x18 -> x29, local copies, waits for them, and re-layouts: 0.21 us -> 4.7 us
    all_to_all x1, blocking collectives: 57.7 us -> 61 us  [per_device(): received = lax.all_to_all(pieces, ('req', 'y'), 0, 0, tiled=True)]
    convert_element_type x1, other arithmetic: 4.05 us -> 1.04 us  [per_device(): (wide_side * lax.rsqrt(mean_square + epsilon) * norm_gain[None, :]).astyp...]
  transfers between devices with their start and end apart: 5 -> 5, of which waited for: 2 -> 2; matrix products, arithmetic and copies ran while one was open for 15% -> 8% of each run, Pallas kernels for 0% -> 0%
where the time goes in v3:
time: 272 us; the launch traced here: 271 us
  blocking collectives  132 us (49%)
  waiting for transfers between devices  62.2 us (23%)
  matrix products  27.7 us (10%)
  local copies, waits for them, and re-layouts  24.4 us (9%)
  between operations  14.3 us (5%)
  other arithmetic  9.93 us (4%)
    all_to_all x1, blocking collectives, per_device(): received = lax.all_to_all(pieces, ('req', 'y'), 0, 0, tiled=True)  61 us
    all_gather x1, blocking collectives, per_device(): lax.all_gather(attended, 'req', axis=0, tiled=True)  46 us
    reduce_scatter x1, waiting for transfers between devices, per_device(): lax.psum_scatter(partial_out.astype(jnp.bfloat16), ('y', 'core'), scatter...  32.1 us
    all_gather x1, waiting for transfers between devices, per_device(): lax.all_gather(lax.all_gather(stream, 'req', axis=1, tiled=True), 'y', ax...  30 us
    all_gather x1, blocking collectives, per_device(): lax.all_gather(stream, 'req', axis=1, tiled=True)  25 us
    reshape x2, local copies, waits for them, and re-layouts, down_of(): down_w.reshape(down_w.shape[0], req_count, columns)  10.1 us
    dot_general x2, matrix products, down_of(): jnp.einsum('ysh,hrf->rysf', hidden, down_w.reshape(down_w.shape[0], req_c...  7.3 us
    dot_general x2, matrix products, hidden_of(): up = jnp.dot(normed, up_w, preferred_element_type=jnp.float32)  5.65 us
  transfers between devices with their start and end apart: 5, of which 2 were waited for; matrix products, arithmetic and copies ran while one was open for 8% of the time, Pallas kernels for 0%

profile of v3, /device:TPU:0, one launch (start us, length us, event | category | flops | bytes accessed | tf_op | source)
XLA Modules:
  0.0 271.3 jit_solution(14782724081613352109)
XLA Ops:
  6.5 1.6 convert_reduce_fusion.2
  8.8 0.9 reshape_squeeze_reshape.3
  9.7 0.9 squeeze_reshape.4
  11.7 11.2 %while.16 = (s32[]{:T(128)}, f32[224]{0:T(256)S(1)}, f32[224]{0:T(256)S(1)}, f32[224,128]{1,0:T(8,128)S(1)}, s32[]{:T(128)}, /*index=5*/s32[17920]{0:T(1024)}, b...) while((s32[]{:T(128)}, f32[224]{0:T(256)S(1)}, ...), condition=%wide.wide.region_4.5_spmd.clone, body=%wide.wide.region_1.4_spmd.clone.sunk | while | flops 299393472 | bytes 8537927 | solution.py:68
  11.7 0.8 dynamic_slice.26
  13.3 1.7 fusion.58
  15.7 1.6 convolution_add_fusion.4
  17.3 0.8 dynamic_slice.26
  18.9 1.7 fusion.58
  21.3 1.6 convolution_add_fusion.4
  22.9 0.9 fusion.26
  24.8 46.0 %all_gather.9 = bf16[512,896]{1,0:T(8,128)(2,1)S(1)} all-gather(bf16[32,896]{1,0:T(8,128)(2,1)S(1)} %convert_element_type.65), channel_id=1, replica_groups=mesh['req'=16,'y'=4,'core'=2] {'req'}, dimensions={0}, use_global_device_ids=true | all-gather | bytes 974848 | tf_op jit(solution)/shard_map/all_gather | solution.py:105
  70.8 1.5 convolution_convert_fusion
  72.4 32.1 %reduce-scatter.2.cloned.1.call-done = bf16[64,448]{1,0:T(8,128)(2,1)} async-done(((bf16[512,448]{1,0:T(8,128)(2,1)}), bf16[64,448]{1,0:T(8,128)(2,1)}) %reduce-scatter.2.cloned.1.call-update) | async-done | bytes 57360 | tf_op jit(solution)/shard_map/reduce_scatter | solution.py:109
  104.5 0.9 fusion.23
  105.4 25.0 %all-gather = bf16[16,448,64]{1,2,0:T(8,128)(2,1)S(1)} all-gather(bf16[1,448,64]{1,2,0:T(8,128)(2,1)S(1)} %fusion.23), channel_id=1, replica_groups=mesh['req'=16,'y'=4,'core'=2] {'req'}, dimensions={0}, use_global_device_ids=true | all-gather | bytes 974848 | tf_op jit(solution)/shard_map/all_gather | solution.py:117
  131.0 2.1 reshape.41
  133.8 4.5 %reshape.36 = bf16[160,16,448]{2,1,0:T(8,128)(2,1)S(1)} reshape(bf16[160,7168]{1,0:T(8,128)(2,1)} %param.27) | data formatting | bytes 4587520 | tf_op jit(solution)/shard_map/reshape | solution.py:135
  138.3 5.6 %reshape.38 = bf16[160,16,448]{2,1,0:T(8,128)(2,1)} reshape(bf16[160,7168]{1,0:T(8,128)(2,1)} %collective-permute-done.2) | data formatting | bytes 4587520 | tf_op jit(solution)/shard_map/reshape | solution.py:135
  143.9 30.0 %all-gather.3.cloned.1.call-done = bf16[256,7168]{1,0:T(8,128)(2,1)} async-done(((bf16[64,7168]{1,0:T(8,128)(2,1)}), bf16[256,7168]{1,0:T(8,128)(2,1)}) %all-gather.3.cloned.1.call-update) | async-done | bytes 3670032 | tf_op jit(solution)/shard_map/all_gather | solution.py:116
  173.9 3.0 %fusion.9 = f32[256]{0:T(256)S(1)} fusion(bf16[256,7168]{1,0:T(8,128)(2,1)} %all-gather.3.cloned.1.call-done), kind=kLoop, calls=%fused_computation.18 | loop fusion | flops 5504768 | bytes 3671040 | tf_op jit(solution)/shard_map/reduce_sum | solution.py:120
  177.1 1.0 fusion.11
  178.7 1.4 fusion.27
  180.6 1.1 copy-done.11
  181.7 2.0 fusion.18
  183.7 1.0 copy.24
  184.7 4.3 %fusion.28 = f32[256,160]{0,1:T(8,128)S(1)} fusion(bf16[256,7168]{1,0:T(8,128)(2,1)} %copy-done.1, bf16[7168,160]{0,1:T(8,128)(2,1)} %collective-permute-done), kind=kOutput, calls=%fused_computation.50 | convolution fusion | flops 587202560 | bytes 6127616 | tf_op jit(solution)/shard_map/dot_general | solution.py:126
  189.0 3.7 %multiply_convert_fusion = bf16[256,160]{0,1:T(8,128)(2,1)} fusion(f32[256,160]{0,1:T(8,128)S(1)} %fusion.28, bf16[256,7168]{1,0:T(8,128)(2,1)S(1)} %copy-done.2, bf16[7168,160]{0,1:T(8,128)(2,1)} %collective-permute-done.1), kind=kOutput, calls=%fused_computation.35 | convolution fusion | flops 587448320 | bytes 6209536 | tf_op jit(solution)/shard_map/dot_general | solution.py:127
  192.7 1.6 copy.26
  194.3 3.6 %fusion.14 = f32[4,64,16,448]{3,1,2,0:T(8,128)S(1)} fusion(bf16[4,64,160,1]{2,1,3,0:T(8,128)(2,1)S(1)} %bitcast.56, bf16[160,16,448]{2,1,0:T(8,128)(2,1)S(1)} %reshape.36), kind=kOutput, calls=%fused_computation.23 | convolution fusion | flops 587202560 | bytes 9715712 | tf_op jit(solution)/shard_map/ysh,hrf->rysf/dot_general | solution.py:132
  197.9 3.7 %fusion.12 = bf16[16,4,64,448]{3,2,0,1:T(8,128)(2,1)S(1)} fusion(f32[4,64,16,448]{3,1,2,0:T(8,128)S(1)} %fusion.14, bf16[4,64,160,1]{2,1,3,0:T(8,128)(2,1)S(1)} %bitcast.57, bf16[160,16,448]{2,1,0:T(8,128)(2,1)S(1)} %copy-done.4), kind=kOutput, calls=%fused_computation.21 | convolution fusion | flops 590872576 | bytes 13385728 | tf_op jit(solution)/shard_map/ysh,hrf->rysf/dot_general | solution.py:132
  201.9 61.0 %all_to_all.5 = bf16[64,64,448]{2,1,0:T(8,128)(2,1)S(1)} all-to-all(bf16[64,64,448]{2,1,0:T(8,128)(2,1)S(1)} %bitcast.54), channel_id=1, replica_groups=mesh['req'=16,'y'=4,'core'=2] {'req','y'}, dimensions={0} | all-to-all | bytes 7340032 | tf_op jit(solution)/shard_map/all_to_all | solution.py:143
  (66 shorter events, 9.4 us)
Async XLA Ops:
  6.5 64.3 %copy-start = (bf16[896,448]{0,1:T(8,128)(2,1)S(1)}, bf16[896,448]{0,1:T(8,128)(2,1)}, u32[]{:S(2)}) copy-start(bf16[896,448]{0,1:T(8,128)(2,1)} %param.22) | copy-start | bytes 2408452
  6.5 98.0 %reduce-scatter.2.cloned.1.call-start = ((), (), s32[]{:S(2)}) async-start(), calls=%async_computation.2 | async-start | bytes 589824 | tf_op jit(solution)/shard_map/reduce_scatter | solution.py:109
  11.6 11.2 %copy-start.12 = (bf16[32,128]{1,0:T(8,128)(2,1)S(1)}, bf16[32,128]{1,0:T(8,128)(2,1)}, u32[]{:S(2)}) copy-start(bf16[32,128]{1,0:T(8,128)(2,1)} %param.16) | copy-start | bytes 24580
  11.6 12.9 %copy-start.13 = (bf16[32,128]{1,0:T(8,128)(2,1)S(1)}, bf16[32,128]{1,0:T(8,128)(2,1)}, u32[]{:S(2)}) copy-start(bf16[32,128]{1,0:T(8,128)(2,1)} %param.17) | copy-start | bytes 24580
  22.9 81.6 %copy-start.7 = (bf16[64,448]{1,0:T(8,128)(2,1)S(1)}, bf16[64,448]{1,0:T(8,128)(2,1)}, u32[]{:S(2)}) copy-start(bf16[64,448]{1,0:T(8,128)(2,1)} %param.23) | copy-start | bytes 172036
  72.4 101.6 %all-gather.3.cloned.1.call-start = ((), (), s32[]{:S(2)}) async-start(), calls=%async_computation.3 | async-start | bytes 4587520 | tf_op jit(solution)/shard_map/all_gather | solution.py:116
  133.1 5.1 %collective-permute-start.2 = (bf16[160,7168]{1,0:T(8,128)(2,1)}, bf16[160,7168]{1,0:T(8,128)(2,1)}, u32[]{:S(2)}, u32[]{:S(2)}) collective-permute-start(bf16[160,7168]{1,0:T(8,128)(2,1)} %param.27), channel_id=1, source_target_pairs={{0,1},{1,0},{2,3},{3,2},{4,5},{5,4},{6,7},{7,6},{8,9},{9,8},{10,11... | collective-permute-start | bytes 6881288 | tf_op jit(solution)/shard_map/ppermute | solution.py:102
  133.2 51.5 %collective-permute-start = (bf16[7168,160]{0,1:T(8,128)(2,1)}, bf16[7168,160]{0,1:T(8,128)(2,1)}, u32[]{:S(2)}, u32[]{:S(2)}) collective-permute-start(bf16[7168,160]{0,1:T(8,128)(2,1)} %param.25), channel_id=1, source_target_pairs={{0,1},{1,0},{2,3},{3,2},{4,5},{5,4},{6,7},{7,6},{8,9},{9,8},{10,11... | collective-permute-start | bytes 6881288 | tf_op jit(solution)/shard_map/ppermute | solution.py:100
  133.7 55.3 %collective-permute-start.1 = (bf16[7168,160]{0,1:T(8,128)(2,1)}, bf16[7168,160]{0,1:T(8,128)(2,1)}, u32[]{:S(2)}, u32[]{:S(2)}) collective-permute-start(bf16[7168,160]{0,1:T(8,128)(2,1)} %param.26), channel_id=1, source_target_pairs={{0,1},{1,0},{2,3},{3,2},{4,5},{5,4},{6,7},{7,6},{8,9},{9,8},{10,11... | collective-permute-start | bytes 6881288 | tf_op jit(solution)/shard_map/ppermute | solution.py:101
  138.3 38.7 %copy-start.10 = (f32[7168]{0:T(1024)S(1)}, f32[7168]{0:T(1024)}, u32[]{:S(2)}) copy-start(f32[7168]{0:T(1024)} %param.24) | copy-start | bytes 86020
  173.9 3.1 %copy-start.3 = (bf16[256,7168]{1,0:T(8,128)(2,1)S(1)}, bf16[256,7168]{1,0:T(8,128)(2,1)}, u32[]{:S(2)}) copy-start(bf16[256,7168]{1,0:T(8,128)(2,1)} %all-gather.3.cloned.1.call-done) | copy-start | bytes 11010052
  177.1 1.6 copy-start.5
  178.7 1.9 copy-start.1
  178.7 3.0 %copy-start.11 = (bf16[7168,160]{0,1:T(8,128)(2,1)S(1)}, bf16[7168,160]{0,1:T(8,128)(2,1)}, u32[]{:S(2)}) copy-start(bf16[7168,160]{0,1:T(8,128)(2,1)} %param.26) | copy-start | bytes 6881284
  184.7 4.3 %copy-start.2 = (bf16[256,7168]{1,0:T(8,128)(2,1)S(1)}, bf16[256,7168]{1,0:T(8,128)(2,1)}, u32[]{:S(2)}) copy-start(bf16[256,7168]{1,0:T(8,128)(2,1)} %copy-done.1) | copy-start | bytes 11010052
  194.3 3.6 %copy-start.4 = (bf16[160,16,448]{2,1,0:T(8,128)(2,1)S(1)}, bf16[160,16,448]{2,1,0:T(8,128)(2,1)}, u32[]{:S(2)}) copy-start(bf16[160,16,448]{2,1,0:T(8,128)(2,1)} %reshape.38) | copy-start | bytes 6881284
  194.3 3.6 %copy-start.6 = (bf16[256,160]{1,0:T(8,128)(2,1)S(1)}, bf16[256,160]{1,0:T(8,128)(2,1)}, u32[]{:S(2)}) copy-start(bf16[256,160]{1,0:T(8,128)(2,1)} %copy.26) | copy-start | bytes 245764
  262.9 0.8 copy-start.8
  262.9 0.9 copy-start.9
Sparse Core Ops, SparseCore 0:
  72.5 31.9 reduce-scatter.1
  133.2 40.6 all-gather.2

commit v4 on v3

--- a/solution.py
+++ b/solution.py
@@ -4,6 +4,7 @@
 import jax.numpy as jnp
 from jax import lax
 from jax.sharding import PartitionSpec as P
+
 
 HD = 128
 
@@ -53,7 +54,7 @@
                 jnp.zeros((row_count,), jnp.float32),
                 jnp.zeros((row_count, head_dim), jnp.float32),
             )
-            for unused in range(kv_here)
+            for _ in range(kv_here)
         )
     )
 
@@ -97,9 +98,12 @@
     down_weight,
 ):
     swap = [(0, 1), (1, 0)]
+    req_count = lax.axis_size("req")
+    columns = down_weight.shape[1] // req_count
+    down_blocks = down_weight.reshape(down_weight.shape[0], req_count, columns)
     gate_partner = lax.ppermute(gate_weight, "core", swap)
     up_partner = lax.ppermute(up_weight, "core", swap)
-    down_partner = lax.ppermute(down_weight, "core", swap)
+    down_partner = lax.ppermute(down_blocks, "core", swap)
     attended = attend(queries, new_keys, new_values, cache_keys, cache_values, tok_req, cache_req)
     partial_out = jnp.dot(
         lax.all_gather(attended, "req", axis=0, tiled=True),
@@ -110,9 +114,8 @@
         partial_out.astype(jnp.bfloat16), ("y", "core"), scatter_dimension=0, tiled=True
     ).astype(jnp.float32)
     stream = (residual.astype(jnp.float32) + mixed).astype(jnp.bfloat16)
-    req_count = lax.axis_size("req")
     y_count = lax.axis_size("y")
-    tokens_out, columns = stream.shape
+    tokens_out = stream.shape[0]
     side_stream = lax.all_gather(
         lax.all_gather(stream, "req", axis=1, tiled=True), "y", axis=0, tiled=True
     )
@@ -132,11 +135,11 @@
         return jnp.einsum(
             "ysh,hrf->rysf",
             hidden,
-            down_w.reshape(down_w.shape[0], req_count, columns),
+            down_w,
             preferred_element_type=jnp.float32,
         )
 
-    product = down_of(hidden_of(gate_weight, up_weight), down_weight) + down_of(
+    product = down_of(hidden_of(gate_weight, up_weight), down_blocks) + down_of(
         hidden_of(gate_partner, up_partner), down_partner
     )
     pieces = product.astype(jnp.bfloat16).reshape(req_count * y_count, tokens_out, columns)

time: 272 us -> 263 us (0.967)
  blocking collectives: 132 us -> 111 us
  matrix products: 27.7 us -> 35.5 us
    all_gather x1, blocking collectives: 46 us -> 24.7 us  [per_device(): lax.all_gather(attended, 'req', axis=0, tiled=True)]
    dot_general x3 -> x6, matrix products: 4.24 us -> 9.28 us  [update(): jnp.einsum('qd,kd->qk', query_rows, block_keys, preferred_element_type=jn...]
    dot_general x3 -> x6, matrix products: 3.34 us -> 8.05 us  [update(): jnp.dot(weights, block_values, preferred_element_type=jnp.float32)]
  transfers between devices with their start and end apart: 5 -> 5, of which waited for: 2 -> 2; matrix products, arithmetic and copies ran while one was open for 8% -> 10% of each run, Pallas kernels for 0% -> 0%
where the time goes in v4:
time: 263 us; the launch traced here: 262 us
  blocking collectives  111 us (42%)
  waiting for transfers between devices  64 us (24%)
  matrix products  35.5 us (13%)
  local copies, waits for them, and re-layouts  24.3 us (9%)
  between operations  14.3 us (5%)
  other arithmetic  11.9 us (5%)
    all_to_all x1, blocking collectives, per_device(): received = lax.all_to_all(pieces, ('req', 'y'), 0, 0, tiled=True)  61.1 us
    all_gather x1, waiting for transfers between devices, per_device(): lax.all_gather(lax.all_gather(stream, 'req', axis=1, tiled=True), 'y', ax...  32.7 us
    reduce_scatter x1, waiting for transfers between devices, per_device(): lax.psum_scatter(partial_out.astype(jnp.bfloat16), ('y', 'core'), scatter...  31.2 us
    all_gather x1, blocking collectives, per_device(): lax.all_gather(stream, 'req', axis=1, tiled=True)  25 us
    all_gather x1, blocking collectives, per_device(): lax.all_gather(attended, 'req', axis=0, tiled=True)  24.7 us
    dot_general x6, matrix products, update(): jnp.einsum('qd,kd->qk', query_rows, block_keys, preferred_element_type=jn...  9.28 us
    dot_general x6, matrix products, update(): jnp.dot(weights, block_values, preferred_element_type=jnp.float32)  8.05 us
    reshape x2, local copies, waits for them, and re-layouts, per_device(): down_blocks = down_weight.reshape(down_weight.shape[0], req_count, columns)  7.39 us
  transfers between devices with their start and end apart: 5, of which 2 were waited for; matrix products, arithmetic and copies ran while one was open for 10% of the time, Pallas kernels for 0%

profile of v4, /device:TPU:0, one launch (start us, length us, event | category | flops | bytes accessed | tf_op | source)
XLA Modules:
  0.0 261.9 jit_solution(895049282695985905)
XLA Ops:
  6.5 1.6 convert_reduce_fusion.2
  8.8 0.9 reshape_squeeze_reshape.3
  9.7 0.9 squeeze_reshape.4
  11.7 28.0 %while.16 = (s32[]{:T(128)}, f32[224]{0:T(256)S(1)}, f32[224]{0:T(256)S(1)}, f32[224,128]{1,0:T(8,128)S(1)}, s32[]{:T(128)}, /*index=5*/s32[17920]{0:T(1024)}, b...) while((s32[]{:T(128)}, f32[224]{0:T(256)S(1)}, ...), condition=%wide.wide.region_4.5_spmd.clone, body=%wide.wide.region_1.4_spmd.clone.sunk | while | flops 299393472 | bytes 8537927 | solution.py:69
  13.3 1.7 fusion.57
  15.7 1.6 convolution_add_fusion.4
  18.9 1.7 fusion.57
  21.3 1.6 convolution_add_fusion.4
  24.5 1.7 fusion.57
  26.9 1.6 convolution_add_fusion.4
  30.1 1.7 fusion.57
  32.5 1.6 convolution_add_fusion.4
  35.7 1.7 fusion.57
  38.0 1.6 convolution_add_fusion.4
  41.6 24.7 %all_gather.9 = bf16[512,896]{1,0:T(8,128)(2,1)S(1)} all-gather(bf16[32,896]{1,0:T(8,128)(2,1)S(1)} %convert_element_type.65), channel_id=1, replica_groups=mesh['req'=16,'y'=4,'core'=2] {'req'}, dimensions={0}, use_global_device_ids=true | all-gather | bytes 974848 | tf_op jit(solution)/shard_map/all_gather | solution.py:109
  66.3 1.5 convolution_convert_fusion
  67.9 31.2 %reduce-scatter.2.cloned.1.call-done = bf16[64,448]{1,0:T(8,128)(2,1)} async-done(((bf16[512,448]{1,0:T(8,128)(2,1)}), bf16[64,448]{1,0:T(8,128)(2,1)}) %reduce-scatter.2.cloned.1.call-update) | async-done | bytes 57360 | tf_op jit(solution)/shard_map/reduce_scatter | solution.py:113
  100.0 25.0 %all-gather = bf16[16,448,64]{1,2,0:T(8,128)(2,1)S(1)} all-gather(bf16[1,448,64]{1,2,0:T(8,128)(2,1)S(1)} %fusion.21), channel_id=1, replica_groups=mesh['req'=16,'y'=4,'core'=2] {'req'}, dimensions={0}, use_global_device_ids=true | all-gather | bytes 974848 | tf_op jit(solution)/shard_map/all_gather | solution.py:120
  125.6 2.1 reshape.37
  128.3 4.5 %reshape.33 = bf16[160,16,448]{2,1,0:T(8,128)(2,1)S(1)} reshape(bf16[160,7168]{1,0:T(8,128)(2,1)} %param.27) | data formatting | bytes 4587520 | tf_op jit(solution)/shard_map/reshape | solution.py:103
  132.8 2.9 %copy.24 = bf16[160,16,448]{2,0,1:T(8,128)(2,1)} copy(bf16[160,16,448]{2,1,0:T(8,128)(2,1)S(1)} %reshape.33) | data formatting | bytes 4587520 | tf_op jit(solution)/shard_map/reshape | solution.py:103
  135.8 32.7 %all-gather.3.cloned.1.call-done = bf16[256,7168]{1,0:T(8,128)(2,1)} async-done(((bf16[64,7168]{1,0:T(8,128)(2,1)}), bf16[256,7168]{1,0:T(8,128)(2,1)}) %all-gather.3.cloned.1.call-update) | async-done | bytes 3670032 | tf_op jit(solution)/shard_map/all_gather | solution.py:119
  168.5 3.0 %fusion.9 = f32[256]{0:T(256)S(1)} fusion(bf16[256,7168]{1,0:T(8,128)(2,1)} %all-gather.3.cloned.1.call-done), kind=kLoop, calls=%fused_computation.18 | loop fusion | flops 5504768 | bytes 3671040 | tf_op jit(solution)/shard_map/reduce_sum | solution.py:123
  171.7 1.0 fusion.11
  173.3 1.4 fusion.26
  175.2 1.1 copy-done.9
  176.3 1.4 fusion.16
  177.8 4.3 %fusion.27 = f32[256,160]{0,1:T(8,128)S(1)} fusion(bf16[256,7168]{1,0:T(8,128)(2,1)} %copy-done.2, bf16[7168,160]{0,1:T(8,128)(2,1)} %collective-permute-done), kind=kOutput, calls=%fused_computation.49 | convolution fusion | flops 587202560 | bytes 6127616 | tf_op jit(solution)/shard_map/dot_general | solution.py:129
  182.1 3.0 %multiply_convert_fusion = bf16[256,160]{0,1:T(8,128)(2,1)S(1)} fusion(f32[256,160]{0,1:T(8,128)S(1)} %fusion.27, bf16[256,7168]{1,0:T(8,128)(2,1)S(1)} %copy-done.3, bf16[7168,160]{0,1:T(8,128)(2,1)} %collective-permute-done.1), kind=kOutput, calls=%fused_computation.33 | convolution fusion | flops 587448320 | bytes 6209536 | tf_op jit(solution)/shard_map/dot_general | solution.py:130
  185.3 3.6 %fusion.14 = f32[4,64,16,448]{3,1,2,0:T(8,128)S(1)} fusion(bf16[4,64,160,1]{2,1,3,0:T(8,128)(2,1)S(1)} %bitcast.57, bf16[160,16,448]{2,1,0:T(8,128)(2,1)S(1)} %reshape.33), kind=kOutput, calls=%fused_computation.23 | convolution fusion | flops 587202560 | bytes 9715712 | tf_op jit(solution)/shard_map/ysh,hrf->rysf/dot_general | solution.py:135
  188.9 3.1 %fusion.12 = bf16[16,4,64,448]{3,2,0,1:T(8,128)(2,1)S(1)} fusion(f32[4,64,16,448]{3,1,2,0:T(8,128)S(1)} %fusion.14, bf16[4,64,160,1]{2,1,3,0:T(8,128)(2,1)S(1)} %bitcast.56, bf16[160,16,448]{2,0,1:T(8,128)(2,1)} %collective-permute-done.2), kind=kOutput, calls=%fused_computation.21 | convolution fusion | flops 590872576 | bytes 13385728 | tf_op jit(solution)/shard_map/ysh,hrf->rysf/dot_general | solution.py:135
  192.4 61.1 %all_to_all.5 = bf16[64,64,448]{2,1,0:T(8,128)(2,1)S(1)} all-to-all(bf16[64,64,448]{2,1,0:T(8,128)(2,1)S(1)} %bitcast.54), channel_id=1, replica_groups=mesh['req'=16,'y'=4,'core'=2] {'req','y'}, dimensions={0} | all-to-all | bytes 7340032 | tf_op jit(solution)/shard_map/all_to_all | solution.py:146
  (89 shorter events, 20.0 us)
Async XLA Ops:
  6.5 59.8 %copy-start = (bf16[896,448]{0,1:T(8,128)(2,1)S(1)}, bf16[896,448]{0,1:T(8,128)(2,1)}, u32[]{:S(2)}) copy-start(bf16[896,448]{0,1:T(8,128)(2,1)} %param.22) | copy-start | bytes 2408452
  6.5 92.6 %reduce-scatter.2.cloned.1.call-start = ((), (), s32[]{:S(2)}) async-start(), calls=%async_computation.2 | async-start | bytes 589824 | tf_op jit(solution)/shard_map/reduce_scatter | solution.py:113
  11.6 28.0 %copy-start.10 = (bf16[32,128]{1,0:T(8,128)(2,1)S(1)}, bf16[32,128]{1,0:T(8,128)(2,1)}, u32[]{:S(2)}) copy-start(bf16[32,128]{1,0:T(8,128)(2,1)} %param.16) | copy-start | bytes 24580
  11.6 29.7 %copy-start.11 = (bf16[32,128]{1,0:T(8,128)(2,1)S(1)}, bf16[32,128]{1,0:T(8,128)(2,1)}, u32[]{:S(2)}) copy-start(bf16[32,128]{1,0:T(8,128)(2,1)} %param.17) | copy-start | bytes 24580
  39.6 59.5 %copy-start.6 = (bf16[64,448]{1,0:T(8,128)(2,1)S(1)}, bf16[64,448]{1,0:T(8,128)(2,1)}, u32[]{:S(2)}) copy-start(bf16[64,448]{1,0:T(8,128)(2,1)} %param.23) | copy-start | bytes 172036
  67.9 100.7 %all-gather.3.cloned.1.call-start = ((), (), s32[]{:S(2)}) async-start(), calls=%async_computation.3 | async-start | bytes 4587520 | tf_op jit(solution)/shard_map/all_gather | solution.py:119
  127.7 50.1 %collective-permute-start = (bf16[7168,160]{0,1:T(8,128)(2,1)}, bf16[7168,160]{0,1:T(8,128)(2,1)}, u32[]{:S(2)}, u32[]{:S(2)}) collective-permute-start(bf16[7168,160]{0,1:T(8,128)(2,1)} %param.25), channel_id=1, source_target_pairs={{0,1},{1,0},{2,3},{3,2},{4,5},{5,4},{6,7},{7,6},{8,9},{9,8},{10,11... | collective-permute-start | bytes 6881288 | tf_op jit(solution)/shard_map/ppermute | solution.py:104
  127.8 54.3 %collective-permute-start.1 = (bf16[7168,160]{0,1:T(8,128)(2,1)}, bf16[7168,160]{0,1:T(8,128)(2,1)}, u32[]{:S(2)}, u32[]{:S(2)}) collective-permute-start(bf16[7168,160]{0,1:T(8,128)(2,1)} %param.26), channel_id=1, source_target_pairs={{0,1},{1,0},{2,3},{3,2},{4,5},{5,4},{6,7},{7,6},{8,9},{9,8},{10,11... | collective-permute-start | bytes 6881288 | tf_op jit(solution)/shard_map/ppermute | solution.py:105
  132.8 38.8 %copy-start.8 = (f32[7168]{0:T(1024)S(1)}, f32[7168]{0:T(1024)}, u32[]{:S(2)}) copy-start(f32[7168]{0:T(1024)} %param.24) | copy-start | bytes 86020
  135.7 53.1 %collective-permute-start.2 = (bf16[160,16,448]{2,0,1:T(8,128)(2,1)}, bf16[160,16,448]{2,0,1:T(8,128)(2,1)}, u32[]{:S(2)}, u32[]{:S(2)}) collective-permute-start(bf16[160,16,448]{2,0,1:T(8,128)(2,1)} %copy.24), channel_id=1, source_target_pairs={{0,1},{1,0},{2,3},{3,2},{4,5},{5,4},{6,7},{7,6},{8,9},{9,8},{10,11... | collective-permute-start | bytes 6881288 | tf_op jit(solution)/shard_map/ppermute | solution.py:106
  168.5 3.1 %copy-start.4 = (bf16[256,7168]{1,0:T(8,128)(2,1)S(1)}, bf16[256,7168]{1,0:T(8,128)(2,1)}, u32[]{:S(2)}) copy-start(bf16[256,7168]{1,0:T(8,128)(2,1)} %all-gather.3.cloned.1.call-done) | copy-start | bytes 11010052
  171.7 1.6 copy-start.5
  173.3 1.9 copy-start.2
  173.3 3.0 %copy-start.9 = (bf16[7168,160]{0,1:T(8,128)(2,1)S(1)}, bf16[7168,160]{0,1:T(8,128)(2,1)}, u32[]{:S(2)}) copy-start(bf16[7168,160]{0,1:T(8,128)(2,1)} %param.26) | copy-start | bytes 6881284
  177.8 4.3 %copy-start.3 = (bf16[256,7168]{1,0:T(8,128)(2,1)S(1)}, bf16[256,7168]{1,0:T(8,128)(2,1)}, u32[]{:S(2)}) copy-start(bf16[256,7168]{1,0:T(8,128)(2,1)} %copy-done.2) | copy-start | bytes 11010052
  192.4 62.6 %copy-start.1 = (bf16[896,448]{0,1:T(8,128)(2,1)S(1)}, bf16[896,448]{0,1:T(8,128)(2,1)}, u32[]{:S(2)}) copy-start(bf16[896,448]{0,1:T(8,128)(2,1)} %param.22) | copy-start | bytes 2408452
  253.5 0.8 copy-start.7
Sparse Core Ops, SparseCore 0:
  68.0 31.0 reduce-scatter.1
  127.8 40.6 all-gather.2

commit v5 on v4

--- a/solution.py
+++ b/solution.py
@@ -1,8 +1,11 @@
+import functools
 import math
 
 import jax
 import jax.numpy as jnp
 from jax import lax
+from jax.experimental import pallas as pl
+from jax.experimental.pallas import tpu as pltpu
 from jax.sharding import PartitionSpec as P
 
 
@@ -11,7 +14,88 @@
 
 epsilon = 1e-05
 masked_value = -1e30
-key_block = 2560
+key_block = 1792
+
+
+def _cache_kernel(live_ref, q_ref, k_ref, v_ref, owner_ref, rowreq_ref, m_out, l_out, acc_out, m_s, l_s, acc_s, *, scale):
+    i = pl.program_id(0)
+
+    @pl.when(i == 0)
+    def _init():
+        m_s[...] = jnp.full(m_s.shape, masked_value, jnp.float32)
+        l_s[...] = jnp.zeros(l_s.shape, jnp.float32)
+        acc_s[...] = jnp.zeros(acc_s.shape, jnp.float32)
+
+    @pl.when(i < live_ref[0])
+    def _step():
+        scores = lax.dot_general(q_ref[...], k_ref[...], (((1,), (1,)), ((), ())),
+                                 preferred_element_type=jnp.float32) * scale
+        visible = owner_ref[...] == rowreq_ref[...]
+        masked = jnp.where(visible, scores, masked_value)
+        running = m_s[...]
+        new_max = jnp.maximum(running, jnp.max(masked, axis=1, keepdims=True))
+        weights = jnp.where(visible, jnp.exp(masked - new_max), 0.0).astype(jnp.bfloat16)
+        factor = jnp.exp(running - new_max)
+        l_s[...] = l_s[...] * factor + jnp.sum(weights.astype(jnp.float32), axis=1, keepdims=True)
+        acc_s[...] = acc_s[...] * factor + jnp.dot(weights, v_ref[...], preferred_element_type=jnp.float32)
+        m_s[...] = new_max
+
+    @pl.when(i == pl.num_programs(0) - 1)
+    def _done():
+        m_out[...] = m_s[...]
+        l_out[...] = l_s[...]
+        acc_out[...] = acc_s[...]
+
+
+def cache_attention(query_rows, cache_keys, cache_values, cache_req, row_req, live_blocks, block, scale):
+    rows, hd = query_rows.shape
+    pool = cache_keys.shape[0]
+    nb = pool // block
+
+    def kv_map(i, live):
+        return (jnp.maximum(jnp.minimum(i, live[0] - 1), 0), 0)
+
+    def own_map(i, live):
+        return (0, jnp.maximum(jnp.minimum(i, live[0] - 1), 0))
+
+    full = lambda i, live: (0, 0)
+    grid_spec = pltpu.PrefetchScalarGridSpec(
+        num_scalar_prefetch=1,
+        grid=(nb,),
+        in_specs=[
+            pl.BlockSpec((rows, hd), full),
+            pl.BlockSpec((block, hd), kv_map),
+            pl.BlockSpec((block, hd), kv_map),
+            pl.BlockSpec((1, block), own_map),
+            pl.BlockSpec((rows, 1), full),
+        ],
+        out_specs=[
+            pl.BlockSpec((rows, 1), full),
+            pl.BlockSpec((rows, 1), full),
+            pl.BlockSpec((rows, hd), full),
+        ],
+        scratch_shapes=[
+            pltpu.VMEM((rows, 1), jnp.float32),
+            pltpu.VMEM((rows, 1), jnp.float32),
+            pltpu.VMEM((rows, hd), jnp.float32),
+        ],
+    )
+    flops = 4 * rows * pool * hd
+    cost = pl.CostEstimate(flops=flops, transcendentals=rows * pool,
+                           bytes_accessed=2 * pool * hd * 2 + pool * 4 + rows * hd * 6)
+    m, l, acc = pl.pallas_call(
+        functools.partial(_cache_kernel, scale=scale),
+        grid_spec=grid_spec,
+        out_shape=[
+            jax.ShapeDtypeStruct((rows, 1), jnp.float32),
+            jax.ShapeDtypeStruct((rows, 1), jnp.float32),
+            jax.ShapeDtypeStruct((rows, hd), jnp.float32),
+        ],
+        compiler_params=pltpu.CompilerParams(dimension_semantics=("arbitrary",)),
+        cost_estimate=cost,
+    )(live_blocks.reshape(1).astype(jnp.int32), query_rows, cache_keys, cache_values,
+      cache_req.reshape(1, pool), row_req.reshape(rows, 1))
+    return m[:, 0], l[:, 0], acc
 
 
 def attend(queries, new_keys, new_values, cache_keys, cache_values, tok_req, cache_req):
@@ -58,15 +142,12 @@
         )
     )
 
-    def consume(block_index, carried):
-        first_slot = block_index * block_width
-        block_keys = lax.dynamic_slice_in_dim(cache_keys, first_slot, block_width, 0)
-        block_values = lax.dynamic_slice_in_dim(cache_values, first_slot, block_width, 0)
-        owners = lax.dynamic_slice_in_dim(cache_req, first_slot, block_width, 0)
-        visible = owners[None, :] == row_req[:, None]
-        return update(carried, block_keys, block_values, visible)
-
-    carried = lax.fori_loop(0, live_blocks, consume, initial)
+    carried = (
+        cache_attention(
+            grouped[:, 0].reshape(row_count, head_dim), cache_keys, cache_values,
+            cache_req, row_req, live_blocks, block_width, score_scale,
+        ),
+    )
     causal = (tok_req[None, :] == row_req[:, None]) & (
         jnp.arange(tokens_here, dtype=jnp.int32)[None, :] <= row_tok[:, None]
     )

time: 263 us -> 254 us (0.966)
  matrix products: 35.5 us -> 21.8 us
  Pallas kernels: 0 us -> 10.6 us
  local copies, waits for them, and re-layouts: 24.3 us -> 19.4 us
    pallas_call x0 -> x1, Pallas kernels: none -> 10.6 us  [cache_attention(): pl.pallas_call(functools.partial(_cache_kernel, scale=scale), grid_spec=g...]
    dot_general x6 -> x1, matrix products: 9.28 us -> 0.91 us  [update(): jnp.einsum('qd,kd->qk', query_rows, block_keys, preferred_element_type=jn...]
    dot_general x6 -> x1, matrix products: 8.05 us -> 1.1 us  [update(): jnp.dot(weights, block_values, preferred_element_type=jnp.float32)]
    dynamic_slice x5 -> x0, local copies, waits for them, and re-layouts: 4 us -> none  [consume(): owners = lax.dynamic_slice_in_dim(cache_req, first_slot, block_width, 0)]
    reduce_sum x6 -> x1, other arithmetic: 3.96 us -> 0.09 us  [update(): jnp.sum(weights.astype(jnp.float32), axis=1)]
    broadcast_in_dim x6 -> x1, local copies, waits for them, and re-layouts: 4.35 us -> 0.72 us  [attend(): row_req = jnp.repeat(tok_req, group_size)]
  transfers between devices with their start and end apart: 5 -> 5, of which waited for: 2 -> 2; matrix products, arithmetic and copies ran while one was open for 10% -> 11% of each run, Pallas kernels for 0% -> 0%
where the time goes in v5:
time: 254 us; the launch traced here: 253 us
  blocking collectives  113 us (44%)
  waiting for transfers between devices  63.6 us (25%)
  matrix products  21.8 us (9%)
  local copies, waits for them, and re-layouts  19.4 us (8%)
  between operations  14.3 us (6%)
  Pallas kernels  10.6 us (4%)
  other arithmetic  10.1 us (4%)
    all_to_all x1, blocking collectives, per_device(): received = lax.all_to_all(pieces, ('req', 'y'), 0, 0, tiled=True)  61 us
    all_gather x1, waiting for transfers between devices, per_device(): lax.all_gather(lax.all_gather(stream, 'req', axis=1, tiled=True), 'y', ax...  32.7 us
    reduce_scatter x1, waiting for transfers between devices, per_device(): lax.psum_scatter(partial_out.astype(jnp.bfloat16), ('y', 'core'), scatter...  30.8 us
    all_gather x1, blocking collectives, per_device(): lax.all_gather(attended, 'req', axis=0, tiled=True)  26.5 us
    all_gather x1, blocking collectives, per_device(): lax.all_gather(stream, 'req', axis=1, tiled=True)  25 us
    pallas_call x1, Pallas kernels, cache_attention(): pl.pallas_call(functools.partial(_cache_kernel, scale=scale), grid_spec=g...  10.6 us
    dot_general x2, matrix products, down_of(): jnp.einsum('ysh,hrf->rysf', hidden, down_w, preferred_element_type=jnp.fl...  7.55 us
    reshape x2, local copies, waits for them, and re-layouts, per_device(): down_blocks = down_weight.reshape(down_weight.shape[0], req_count, columns)  7.41 us
  transfers between devices with their start and end apart: 5, of which 2 were waited for; matrix products, arithmetic and copies ran while one was open for 11% of the time, Pallas kernels for 0%

profile of v5, /device:TPU:0, one launch (start us, length us, event | category | flops | bytes accessed | tf_op | source)
XLA Modules:
  0.0 253.0 jit_solution(3271458216104049448)
XLA Ops:
  6.5 1.6 convert_reduce_fusion.1
  8.8 1.6 reshape.36.owner_ref
  10.4 0.7 broadcast_in_dim.20
  11.2 0.7 reshape_reshape.4.rowreq_ref
  12.1 0.9 reshape_squeeze_reshape.4.q_ref
  13.0 0.9 fusion.15
  14.1 10.6 %shard_map.127 = (f32[224,1]{1,0:T(8,128)}, f32[224,1]{1,0:T(8,128)}, f32[224,128]{1,0:T(8,128)}) custom-call(s32[1]{0:T(128)} %bitcast.live_ref, bf16[224,128]{1,0:T(8,128)(2,1)} %copy-done.8, bf16[17920,128]{1,0:T(8,128)(2,1)} %k_ref.1, bf16[17920,128]{1,0:T(8,128)(2,1)} %v_ref.1, s32[1,17920]{1,0:T(1,128)} %reshape.36.owner_ref, ...), custom_call_target="tpu_custom_call" | custom-call | flops 2055208960 | bytes 9418752 | tf_op jit(solution)/shard_map/pallas_call | solution.py:86
  24.7 1.0 maximum_reduce_fusion
  26.0 1.1 fusion.11
  27.1 1.1 fusion.9
  28.3 26.5 %all_gather.9 = bf16[512,896]{1,0:T(8,128)(2,1)S(1)} all-gather(bf16[32,896]{1,0:T(8,128)(2,1)S(1)} %convert_element_type.59), channel_id=1, replica_groups=mesh['req'=16,'y'=4,'core'=2] {'req'}, dimensions={0}, use_global_device_ids=true | all-gather | bytes 974848 | tf_op jit(solution)/shard_map/all_gather | solution.py:190
  54.9 1.5 convolution_convert_fusion
  56.5 30.8 %reduce-scatter.2.cloned.1.call-done = bf16[64,448]{1,0:T(8,128)(2,1)} async-done(((bf16[512,448]{1,0:T(8,128)(2,1)}), bf16[64,448]{1,0:T(8,128)(2,1)}) %reduce-scatter.2.cloned.1.call-update) | async-done | bytes 57360 | tf_op jit(solution)/shard_map/reduce_scatter | solution.py:194
  87.3 0.9 fusion.13
  88.1 25.0 %all-gather = bf16[16,448,64]{1,2,0:T(8,128)(2,1)S(1)} all-gather(bf16[1,448,64]{1,2,0:T(8,128)(2,1)S(1)} %fusion.13), channel_id=1, replica_groups=mesh['req'=16,'y'=4,'core'=2] {'req'}, dimensions={0}, use_global_device_ids=true | all-gather | bytes 974848 | tf_op jit(solution)/shard_map/all_gather | solution.py:201
  113.7 2.1 reshape.42
  116.4 4.5 %reshape.38 = bf16[160,16,448]{2,1,0:T(8,128)(2,1)S(1)} reshape(bf16[160,7168]{1,0:T(8,128)(2,1)} %param.25) | data formatting | bytes 4587520 | tf_op jit(solution)/shard_map/reshape | solution.py:184
  120.9 3.0 %copy.30 = bf16[160,16,448]{2,0,1:T(8,128)(2,1)} copy(bf16[160,16,448]{2,1,0:T(8,128)(2,1)S(1)} %reshape.38) | data formatting | bytes 4587520 | tf_op jit(solution)/shard_map/reshape | solution.py:184
  124.0 32.7 %all-gather.3.cloned.1.call-done = bf16[256,7168]{1,0:T(8,128)(2,1)} async-done(((bf16[64,7168]{1,0:T(8,128)(2,1)}), bf16[256,7168]{1,0:T(8,128)(2,1)}) %all-gather.3.cloned.1.call-update) | async-done | bytes 3670032 | tf_op jit(solution)/shard_map/all_gather | solution.py:200
  156.7 3.0 %fusion = f32[256]{0:T(256)S(1)} fusion(bf16[256,7168]{1,0:T(8,128)(2,1)} %all-gather.3.cloned.1.call-done), kind=kLoop, calls=%fused_computation.4 | loop fusion | flops 5504768 | bytes 3671040 | tf_op jit(solution)/shard_map/reduce_sum | solution.py:204
  159.8 1.0 fusion.2
  161.5 1.4 fusion.16
  163.3 1.1 copy-done.11
  164.4 1.4 fusion.7
  165.8 0.8 copy.29
  166.6 4.3 %fusion.17 = f32[256,160]{0,1:T(8,128)S(1)} fusion(bf16[256,7168]{1,0:T(8,128)(2,1)} %copy-done.1, bf16[7168,160]{0,1:T(8,128)(2,1)} %collective-permute-done), kind=kOutput, calls=%fused_computation.36 | convolution fusion | flops 587202560 | bytes 6127616 | tf_op jit(solution)/shard_map/dot_general | solution.py:210
  170.9 3.7 %multiply_convert_fusion = bf16[256,160]{0,1:T(8,128)(2,1)} fusion(f32[256,160]{0,1:T(8,128)S(1)} %fusion.17, bf16[256,7168]{1,0:T(8,128)(2,1)S(1)} %copy-done.2, bf16[7168,160]{0,1:T(8,128)(2,1)} %collective-permute-done.1), kind=kOutput, calls=%fused_computation.19 | convolution fusion | flops 587448320 | bytes 6209536 | tf_op jit(solution)/shard_map/dot_general | solution.py:211
  174.6 1.0 copy.31
  175.5 4.5 %fusion.5 = f32[4,64,16,448]{3,1,2,0:T(8,128)S(1)} fusion(bf16[4,64,160,1]{2,1,3,0:T(8,128)(2,1)} %bitcast.48, bf16[160,16,448]{2,1,0:T(8,128)(2,1)S(1)} %reshape.38), kind=kOutput, calls=%fused_computation.9 | convolution fusion | flops 587202560 | bytes 9715712 | tf_op jit(solution)/shard_map/ysh,hrf->rysf/dot_general | solution.py:216
  180.1 3.0 %fusion.3 = bf16[16,4,64,448]{3,2,0,1:T(8,128)(2,1)S(1)} fusion(f32[4,64,16,448]{3,1,2,0:T(8,128)S(1)} %fusion.5, bf16[4,64,160,1]{2,1,3,0:T(8,128)(2,1)S(1)} %bitcast.47, bf16[160,16,448]{2,0,1:T(8,128)(2,1)} %collective-permute-done.2), kind=kOutput, calls=%fused_computation.7 | convolution fusion | flops 590872576 | bytes 13385728 | tf_op jit(solution)/shard_map/ysh,hrf->rysf/dot_general | solution.py:216
  183.6 61.0 %all_to_all.5 = bf16[64,64,448]{2,1,0:T(8,128)(2,1)S(1)} all-to-all(bf16[64,64,448]{2,1,0:T(8,128)(2,1)S(1)} %bitcast.45), channel_id=1, replica_groups=mesh['req'=16,'y'=4,'core'=2] {'req','y'}, dimensions={0} | all-to-all | bytes 7340032 | tf_op jit(solution)/shard_map/all_to_all | solution.py:227
  244.6 0.7 convert_reduce_fusion
  (46 shorter events, 4.6 us)
Async XLA Ops:
  6.5 48.3 %copy-start = (bf16[896,448]{0,1:T(8,128)(2,1)S(1)}, bf16[896,448]{0,1:T(8,128)(2,1)}, u32[]{:S(2)}) copy-start(bf16[896,448]{0,1:T(8,128)(2,1)} %param.20) | copy-start | bytes 2408452
  6.5 80.7 %reduce-scatter.2.cloned.1.call-start = ((), (), s32[]{:S(2)}) async-start(), calls=%async_computation.2 | async-start | bytes 589824 | tf_op jit(solution)/shard_map/reduce_scatter | solution.py:194
  13.0 1.1 copy-start.8
  14.1 11.7 %copy-start.10 = (s32[32]{0:T(128)S(1)}, s32[32]{0:T(128)}, u32[]{:S(2)}) copy-start(s32[32]{0:T(128)} %param.18) | copy-start | bytes 388
  14.1 13.0 %copy-start.12 = (bf16[32,128]{1,0:T(8,128)(2,1)S(1)}, bf16[32,128]{1,0:T(8,128)(2,1)}, u32[]{:S(2)}) copy-start(bf16[32,128]{1,0:T(8,128)(2,1)} %param.15) | copy-start | bytes 24580
  24.7 62.6 %copy-start.5 = (bf16[64,448]{1,0:T(8,128)(2,1)S(1)}, bf16[64,448]{1,0:T(8,128)(2,1)}, u32[]{:S(2)}) copy-start(bf16[64,448]{1,0:T(8,128)(2,1)} %param.21) | copy-start | bytes 172036
  56.4 100.3 %all-gather.3.cloned.1.call-start = ((), (), s32[]{:S(2)}) async-start(), calls=%async_computation.3 | async-start | bytes 4587520 | tf_op jit(solution)/shard_map/all_gather | solution.py:200
  115.9 50.7 %collective-permute-start = (bf16[7168,160]{0,1:T(8,128)(2,1)}, bf16[7168,160]{0,1:T(8,128)(2,1)}, u32[]{:S(2)}, u32[]{:S(2)}) collective-permute-start(bf16[7168,160]{0,1:T(8,128)(2,1)} %param.23), channel_id=1, source_target_pairs={{0,1},{1,0},{2,3},{3,2},{4,5},{5,4},{6,7},{7,6},{8,9},{9,8},{10,11... | collective-permute-start | bytes 6881288 | tf_op jit(solution)/shard_map/ppermute | solution.py:185
  116.0 54.9 %collective-permute-start.1 = (bf16[7168,160]{0,1:T(8,128)(2,1)}, bf16[7168,160]{0,1:T(8,128)(2,1)}, u32[]{:S(2)}, u32[]{:S(2)}) collective-permute-start(bf16[7168,160]{0,1:T(8,128)(2,1)} %param.24), channel_id=1, source_target_pairs={{0,1},{1,0},{2,3},{3,2},{4,5},{5,4},{6,7},{7,6},{8,9},{9,8},{10,11... | collective-permute-start | bytes 6881288 | tf_op jit(solution)/shard_map/ppermute | solution.py:186
  120.9 38.8 %copy-start.9 = (f32[7168]{0:T(1024)S(1)}, f32[7168]{0:T(1024)}, u32[]{:S(2)}) copy-start(f32[7168]{0:T(1024)} %param.22) | copy-start | bytes 86020
  123.9 56.2 %collective-permute-start.2 = (bf16[160,16,448]{2,0,1:T(8,128)(2,1)}, bf16[160,16,448]{2,0,1:T(8,128)(2,1)}, u32[]{:S(2)}, u32[]{:S(2)}) collective-permute-start(bf16[160,16,448]{2,0,1:T(8,128)(2,1)} %copy.30), channel_id=1, source_target_pairs={{0,1},{1,0},{2,3},{3,2},{4,5},{5,4},{6,7},{7,6},{8,9},{9,8},{10,11... | collective-permute-start | bytes 6881288 | tf_op jit(solution)/shard_map/ppermute | solution.py:187
  156.7 3.1 %copy-start.3 = (bf16[256,7168]{1,0:T(8,128)(2,1)S(1)}, bf16[256,7168]{1,0:T(8,128)(2,1)}, u32[]{:S(2)}) copy-start(bf16[256,7168]{1,0:T(8,128)(2,1)} %all-gather.3.cloned.1.call-done) | copy-start | bytes 11010052
  159.8 1.6 copy-start.4
  161.5 1.9 copy-start.1
  161.5 3.0 %copy-start.11 = (bf16[7168,160]{0,1:T(8,128)(2,1)S(1)}, bf16[7168,160]{0,1:T(8,128)(2,1)}, u32[]{:S(2)}) copy-start(bf16[7168,160]{0,1:T(8,128)(2,1)} %param.24) | copy-start | bytes 6881284
  166.6 4.3 %copy-start.2 = (bf16[256,7168]{1,0:T(8,128)(2,1)S(1)}, bf16[256,7168]{1,0:T(8,128)(2,1)}, u32[]{:S(2)}) copy-start(bf16[256,7168]{1,0:T(8,128)(2,1)} %copy-done.1) | copy-start | bytes 11010052
  244.6 0.8 copy-start.6
  244.6 0.9 copy-start.7
Sparse Core Ops, SparseCore 0:
  56.5 30.6 reduce-scatter.1
  116.0 40.6 all-gather.2

commit v6 on v5

--- a/solution.py
+++ b/solution.py
@@ -180,26 +180,30 @@
 ):
     swap = [(0, 1), (1, 0)]
     req_count = lax.axis_size("req")
-    columns = down_weight.shape[1] // req_count
-    down_blocks = down_weight.reshape(down_weight.shape[0], req_count, columns)
+    y_count = lax.axis_size("y")
+    core_count = lax.axis_size("core")
+    tokens_out, columns = residual.shape
     gate_partner = lax.ppermute(gate_weight, "core", swap)
     up_partner = lax.ppermute(up_weight, "core", swap)
-    down_partner = lax.ppermute(down_blocks, "core", swap)
+    down_partner = lax.ppermute(down_weight, "core", swap)
     attended = attend(queries, new_keys, new_values, cache_keys, cache_values, tok_req, cache_req)
     partial_out = jnp.dot(
         lax.all_gather(attended, "req", axis=0, tiled=True),
         out_weight,
         preferred_element_type=jnp.float32,
     )
-    mixed = lax.psum_scatter(
-        partial_out.astype(jnp.bfloat16), ("y", "core"), scatter_dimension=0, tiled=True
-    ).astype(jnp.float32)
-    stream = (residual.astype(jnp.float32) + mixed).astype(jnp.bfloat16)
-    y_count = lax.axis_size("y")
-    tokens_out = stream.shape[0]
-    side_stream = lax.all_gather(
-        lax.all_gather(stream, "req", axis=1, tiled=True), "y", axis=0, tiled=True
-    )
+    core = lax.axis_index("core")
+    first_row = (lax.axis_index("y") * core_count + core) * tokens_out
+    own_rows = lax.dynamic_slice_in_dim(partial_out, first_row, tokens_out, 0)
+    partial_out = lax.dynamic_update_slice_in_dim(
+        partial_out, own_rows + residual.astype(jnp.float32), first_row, 0
+    )
+    stream_rows = lax.psum(partial_out, ("y", "core")).astype(jnp.bfloat16)
+    stream = lax.dynamic_slice_in_dim(stream_rows, first_row, tokens_out, 0)
+    side_rows = lax.dynamic_index_in_dim(
+        stream_rows.reshape(y_count, core_count, tokens_out, columns), core, 1, keepdims=False
+    ).reshape(y_count * tokens_out, columns)
+    side_stream = lax.all_gather(side_rows, "req", axis=1, tiled=True)
     wide_side = side_stream.astype(jnp.float32)
     mean_square = jnp.mean(wide_side * wide_side, axis=1, keepdims=True)
     normed = (wide_side * lax.rsqrt(mean_square + epsilon) * norm_gain[None, :]).astype(
@@ -220,8 +224,11 @@
             preferred_element_type=jnp.float32,
         )
 
-    product = down_of(hidden_of(gate_weight, up_weight), down_blocks) + down_of(
-        hidden_of(gate_partner, up_partner), down_partner
+    def blocks_of(down_w):
+        return down_w.reshape(down_w.shape[0], req_count, columns)
+
+    product = down_of(hidden_of(gate_weight, up_weight), blocks_of(down_weight)) + down_of(
+        hidden_of(gate_partner, up_partner), blocks_of(down_partner)
     )
     pieces = product.astype(jnp.bfloat16).reshape(req_count * y_count, tokens_out, columns)
     received = lax.all_to_all(pieces, ("req", "y"), 0, 0, tiled=True)

time: 254 us -> 255 us (level)
  waiting for transfers between devices: 63.6 us -> 38.4 us
  blocking collectives: 113 us -> 137 us
    psum x0 -> x1, blocking collectives: none -> 50.3 us  [per_device(): stream_rows = lax.psum(partial_out, ('y', 'core')).astype(jnp.bfloat16)]
    reduce_scatter x1 -> x0, waiting for transfers between devices: 30.8 us -> none  [per_device(): lax.psum_scatter(partial_out.astype(jnp.bfloat16), ('y', 'core'), scatter...]
    all_gather x1 -> x0, blocking collectives: 25 us -> none  [per_device(): lax.all_gather(stream, 'req', axis=1, tiled=True)]
    all_gather x1, waiting for transfers between devices: 32.7 us -> 38.4 us  [per_device(): side_stream = lax.all_gather(side_rows, 'req', axis=1, tiled=True)]
    unnamed x27 -> x26, local copies, waits for them, and re-layouts: 4.68 us -> 0.18 us
    reshape x2 -> x3, local copies, waits for them, and re-layouts: 7.41 us -> 10.9 us  [the longest x2 10 us: blocks_of(): return down_w.reshape(down_w.shape[0], req_count, columns)]
  transfers between devices with their start and end apart: 5 -> 4, of which waited for: 2 -> 1; matrix products, arithmetic and copies ran while one was open for 11% -> 10% of each run, Pallas kernels for 0% -> 0%
where the time goes in v6:
time: 255 us; the launch traced here: 254 us
  blocking collectives  137 us (54%)
  waiting for transfers between devices  38.4 us (15%)
  matrix products  22.1 us (9%)
  local copies, waits for them, and re-layouts  18.5 us (7%)
  between operations  14.4 us (6%)
  other arithmetic  12.4 us (5%)
  Pallas kernels  10.6 us (4%)
    all_to_all x1, blocking collectives, per_device(): received = lax.all_to_all(pieces, ('req', 'y'), 0, 0, tiled=True)  59.7 us
    psum x1, blocking collectives, per_device(): stream_rows = lax.psum(partial_out, ('y', 'core')).astype(jnp.bfloat16)  50.3 us
    all_gather x1, waiting for transfers between devices, per_device(): side_stream = lax.all_gather(side_rows, 'req', axis=1, tiled=True)  38.4 us
    all_gather x1, blocking collectives, per_device(): lax.all_gather(attended, 'req', axis=0, tiled=True)  26.5 us
    pallas_call x1, Pallas kernels, cache_attention(): pl.pallas_call(functools.partial(_cache_kernel, scale=scale), grid_spec=g...  10.6 us
    reshape x2, local copies, waits for them, and re-layouts, blocks_of(): return down_w.reshape(down_w.shape[0], req_count, columns)  10 us
    dot_general x2, matrix products, hidden_of(): gate = jnp.dot(normed, gate_w, preferred_element_type=jnp.float32)  7.46 us
    dot_general x2, matrix products, down_of(): jnp.einsum('ysh,hrf->rysf', hidden, down_w, preferred_element_type=jnp.fl...  7.3 us
  transfers between devices with their start and end apart: 4, of which 1 were waited for; matrix products, arithmetic and copies ran while one was open for 10% of the time, Pallas kernels for 0%

profile of v6, /device:TPU:0, one launch (start us, length us, event | category | flops | bytes accessed | tf_op | source)
XLA Modules:
  0.0 253.6 jit_solution(12675910002865378369)
XLA Ops:
  6.5 1.6 convert_reduce_fusion.1
  8.8 1.6 reshape.46.owner_ref
  10.4 0.7 broadcast_in_dim.20
  11.2 0.7 reshape_reshape.4.rowreq_ref
  12.1 0.9 reshape_squeeze_reshape.4.q_ref
  13.0 0.9 fusion.15
  14.1 10.6 %shard_map.127 = (f32[224,1]{1,0:T(8,128)}, f32[224,1]{1,0:T(8,128)}, f32[224,128]{1,0:T(8,128)}) custom-call(s32[1]{0:T(128)} %bitcast.live_ref, bf16[224,128]{1,0:T(8,128)(2,1)} %copy-done.7, bf16[17920,128]{1,0:T(8,128)(2,1)} %k_ref.1, bf16[17920,128]{1,0:T(8,128)(2,1)} %v_ref.1, s32[1,17920]{1,0:T(1,128)} %reshape.46.owner_ref, ...), custom_call_target="tpu_custom_call" | custom-call | flops 2055208960 | bytes 9418752 | tf_op jit(solution)/shard_map/pallas_call | solution.py:86
  24.7 1.0 maximum_reduce_fusion
  26.0 1.1 fusion.13
  27.1 1.1 fusion.11
  28.3 26.5 %all_gather.6 = bf16[512,896]{1,0:T(8,128)(2,1)S(1)} all-gather(bf16[32,896]{1,0:T(8,128)(2,1)S(1)} %convert_element_type.52), channel_id=1, replica_groups=mesh['req'=16,'y'=4,'core'=2] {'req'}, dimensions={0}, use_global_device_ids=true | all-gather | bytes 974848 | tf_op jit(solution)/shard_map/all_gather | solution.py:191
  54.9 0.7 fusion.16
  55.6 50.3 %all-reduce.1 = bf16[512,448]{1,0:T(8,128)(2,1)S(1)} all-reduce(f32[512,448]{1,0:T(8,128)S(1)} %add_dynamic-update-slice_fusion), channel_id=1, replica_groups=mesh['req'=16,'y'=4,'core'=2] {'y','core'}, use_global_device_ids=true, to_apply=%region_3.4 | all-reduce | flops 229376 | bytes 1376256 | tf_op jit(solution)/shard_map/psum | solution.py:201
  106.0 0.9 copy.48
  107.0 0.5 collective-permute-start
  107.6 4.5 %reshape.50 = bf16[160,16,448]{2,1,0:T(8,128)(2,1)S(1)} reshape(bf16[160,7168]{1,0:T(8,128)(2,1)} %param.25) | data formatting | bytes 4587520 | tf_op jit(solution)/shard_map/reshape | solution.py:228
  112.1 5.6 %reshape.52 = bf16[160,16,448]{2,1,0:T(8,128)(2,1)} reshape(bf16[160,7168]{1,0:T(8,128)(2,1)} %collective-permute-done.2) | data formatting | bytes 4587520 | tf_op jit(solution)/shard_map/reshape | solution.py:228
  117.7 38.4 %all-gather.2.cloned.1.call-done = bf16[256,7168]{0,1:T(8,128)(2,1)} async-done(((bf16[256,448]{0,1:T(8,128)(2,1)}), bf16[256,7168]{0,1:T(8,128)(2,1)}) %all-gather.2.cloned.1.call-update) | async-done | bytes 3670032 | tf_op jit(solution)/shard_map/all_gather | solution.py:206
  156.0 3.2 %fusion = f32[256]{0:T(256)S(1)} fusion(bf16[256,7168]{0,1:T(8,128)(2,1)} %all-gather.2.cloned.1.call-done), kind=kLoop, calls=%fused_computation.4 | loop fusion | flops 5504768 | bytes 3671040 | tf_op jit(solution)/shard_map/reduce_sum | solution.py:208
  159.2 3.2 %fusion.2 = bf16[256,7168]{0,1:T(8,128)(2,1)S(1)} fusion(bf16[256,7168]{0,1:T(8,128)(2,1)S(1)} %copy-done.3, f32[7168]{0:T(1024)S(1)} %copy-done.9, f32[256]{0:T(256)S(1)} %add_rsqrt_fusion), kind=kLoop, calls=%fused_computation.6 | loop fusion | flops 7340032 | bytes 7369728 | tf_op jit(solution)/shard_map/convert_element_type | solution.py:209
  162.4 3.8 %fusion.17 = f32[256,160]{0,1:T(8,128)S(1)} fusion(bf16[7168,160]{0,1:T(8,128)(2,1)} %param.23, bf16[256,7168]{0,1:T(8,128)(2,1)S(1)} %fusion.2), kind=kOutput, calls=%fused_computation.36 | convolution fusion | flops 587202560 | bytes 6127616 | tf_op jit(solution)/shard_map/dot_general | solution.py:214
  166.3 1.5 fusion.9
  167.7 1.0 copy.49
  168.8 3.6 %fusion.18 = f32[256,160]{0,1:T(8,128)S(1)} fusion(bf16[7168,160]{0,1:T(8,128)(2,1)} %collective-permute-done, bf16[256,7168]{0,1:T(8,128)(2,1)} %copy-done.1), kind=kOutput, calls=%fused_computation.37 | convolution fusion | flops 587202560 | bytes 6127616 | tf_op jit(solution)/shard_map/dot_general | solution.py:214
  172.5 3.1 %multiply_convert_fusion = bf16[256,160]{0,1:T(8,128)(2,1)} fusion(f32[256,160]{0,1:T(8,128)S(1)} %fusion.18, bf16[7168,160]{0,1:T(8,128)(2,1)} %collective-permute-done.1, bf16[256,7168]{0,1:T(8,128)(2,1)S(1)} %copy-done.2), kind=kOutput, calls=%fused_computation.20 | convolution fusion | flops 587448320 | bytes 6209536 | tf_op jit(solution)/shard_map/dot_general | solution.py:215
  175.6 1.6 copy.51
  177.3 3.6 %fusion.5 = f32[4,64,16,448]{3,1,2,0:T(8,128)S(1)} fusion(bf16[4,64,160,1]{2,1,3,0:T(8,128)(2,1)S(1)} %bitcast.43, bf16[160,16,448]{2,1,0:T(8,128)(2,1)S(1)} %reshape.50), kind=kOutput, calls=%fused_computation.9 | convolution fusion | flops 587202560 | bytes 9715712 | tf_op jit(solution)/shard_map/ysh,hrf->rysf/dot_general | solution.py:220
  180.9 3.7 %fusion.3 = bf16[16,4,64,448]{3,2,0,1:T(8,128)(2,1)S(1)} fusion(f32[4,64,16,448]{3,1,2,0:T(8,128)S(1)} %fusion.5, bf16[4,64,160,1]{2,1,3,0:T(8,128)(2,1)S(1)} %bitcast.44, bf16[160,16,448]{2,1,0:T(8,128)(2,1)S(1)} %copy-done.4), kind=kOutput, calls=%fused_computation.7 | convolution fusion | flops 590872576 | bytes 13385728 | tf_op jit(solution)/shard_map/ysh,hrf->rysf/dot_general | solution.py:220
  184.6 0.3 copy.53
  184.9 59.7 %all_to_all.5 = bf16[64,64,448]{2,1,0:T(8,128)(2,1)S(1)} all-to-all(bf16[64,64,448]{2,1,0:T(8,128)(2,1)S(1)} %bitcast.40), channel_id=1, replica_groups=mesh['req'=16,'y'=4,'core'=2] {'req','y'}, dimensions={0} | all-to-all | bytes 7340032 | tf_op jit(solution)/shard_map/all_to_all | solution.py:234
  244.6 0.7 convert_reduce_fusion
  245.3 1.5 add_convert_fusion.1
  (43 shorter events, 1.1 us)
Async XLA Ops:
  6.5 48.3 %copy-start = (bf16[896,448]{0,1:T(8,128)(2,1)S(1)}, bf16[896,448]{0,1:T(8,128)(2,1)}, u32[]{:S(2)}) copy-start(bf16[896,448]{0,1:T(8,128)(2,1)} %param.20) | copy-start | bytes 2408452
  6.5 149.5 %all-gather.2.cloned.1.call-start = ((), (), s32[]{:S(2)}) async-start(), calls=%async_computation.1 | async-start | bytes 3899392 | tf_op jit(solution)/shard_map/all_gather | solution.py:206
  13.0 1.1 copy-start.7
  14.0 11.7 %copy-start.10 = (s32[32]{0:T(128)S(1)}, s32[32]{0:T(128)}, u32[]{:S(2)}) copy-start(s32[32]{0:T(128)} %param.18) | copy-start | bytes 388
  14.1 13.0 %copy-start.12 = (bf16[32,128]{1,0:T(8,128)(2,1)S(1)}, bf16[32,128]{1,0:T(8,128)(2,1)}, u32[]{:S(2)}) copy-start(bf16[32,128]{1,0:T(8,128)(2,1)} %param.15) | copy-start | bytes 24580
  24.7 30.9 %copy-start.8 = (bf16[64,448]{1,0:T(8,128)(2,1)S(1)}, bf16[64,448]{1,0:T(8,128)(2,1)}, u32[]{:S(2)}) copy-start(bf16[64,448]{1,0:T(8,128)(2,1)} %param.21) | copy-start | bytes 172036
  106.0 1.5 copy-start.5
  106.9 5.2 %collective-permute-start.2 = (bf16[160,7168]{1,0:T(8,128)(2,1)}, bf16[160,7168]{1,0:T(8,128)(2,1)}, u32[]{:S(2)}, u32[]{:S(2)}) collective-permute-start(bf16[160,7168]{1,0:T(8,128)(2,1)} %param.25), channel_id=1, source_target_pairs={{0,1},{1,0},{2,3},{3,2},{4,5},{5,4},{6,7},{7,6},{8,9},{9,8},{10,11... | collective-permute-start | bytes 6881288 | tf_op jit(solution)/shard_map/ppermute | solution.py:188
  107.0 61.7 %collective-permute-start = (bf16[7168,160]{0,1:T(8,128)(2,1)}, bf16[7168,160]{0,1:T(8,128)(2,1)}, u32[]{:S(2)}, u32[]{:S(2)}) collective-permute-start(bf16[7168,160]{0,1:T(8,128)(2,1)} %param.23), channel_id=1, source_target_pairs={{0,1},{1,0},{2,3},{3,2},{4,5},{5,4},{6,7},{7,6},{8,9},{9,8},{10,11... | collective-permute-start | bytes 6881288 | tf_op jit(solution)/shard_map/ppermute | solution.py:186
  107.5 64.9 %collective-permute-start.1 = (bf16[7168,160]{0,1:T(8,128)(2,1)}, bf16[7168,160]{0,1:T(8,128)(2,1)}, u32[]{:S(2)}, u32[]{:S(2)}) collective-permute-start(bf16[7168,160]{0,1:T(8,128)(2,1)} %param.24), channel_id=1, source_target_pairs={{0,1},{1,0},{2,3},{3,2},{4,5},{5,4},{6,7},{7,6},{8,9},{9,8},{10,11... | collective-permute-start | bytes 6881288 | tf_op jit(solution)/shard_map/ppermute | solution.py:187
  112.1 47.1 %copy-start.9 = (f32[7168]{0:T(1024)S(1)}, f32[7168]{0:T(1024)}, u32[]{:S(2)}) copy-start(f32[7168]{0:T(1024)} %param.22) | copy-start | bytes 86020
  156.0 3.2 %copy-start.3 = (bf16[256,7168]{0,1:T(8,128)(2,1)S(1)}, bf16[256,7168]{0,1:T(8,128)(2,1)}, u32[]{:S(2)}) copy-start(bf16[256,7168]{0,1:T(8,128)(2,1)} %all-gather.2.cloned.1.call-done) | copy-start | bytes 11010052
  162.4 3.9 %copy-start.1 = (bf16[256,7168]{0,1:T(8,128)(2,1)}, bf16[256,7168]{0,1:T(8,128)(2,1)S(1)}, u32[]{:S(2)}) copy-start(bf16[256,7168]{0,1:T(8,128)(2,1)S(1)} %fusion.2) | copy-start | bytes 11010052
  162.4 3.9 %copy-start.11 = (bf16[7168,160]{0,1:T(8,128)(2,1)S(1)}, bf16[7168,160]{0,1:T(8,128)(2,1)}, u32[]{:S(2)}) copy-start(bf16[7168,160]{0,1:T(8,128)(2,1)} %param.24) | copy-start | bytes 6881284
  168.7 3.8 %copy-start.2 = (bf16[256,7168]{0,1:T(8,128)(2,1)S(1)}, bf16[256,7168]{0,1:T(8,128)(2,1)}, u32[]{:S(2)}) copy-start(bf16[256,7168]{0,1:T(8,128)(2,1)} %copy-done.1) | copy-start | bytes 11010052
  177.3 3.6 %copy-start.4 = (bf16[160,16,448]{2,1,0:T(8,128)(2,1)S(1)}, bf16[160,16,448]{2,1,0:T(8,128)(2,1)}, u32[]{:S(2)}) copy-start(bf16[160,16,448]{2,1,0:T(8,128)(2,1)} %reshape.52) | copy-start | bytes 6881284
  177.3 3.6 %copy-start.6 = (bf16[256,160]{1,0:T(8,128)(2,1)S(1)}, bf16[256,160]{1,0:T(8,128)(2,1)}, u32[]{:S(2)}) copy-start(bf16[256,160]{1,0:T(8,128)(2,1)} %copy.51) | copy-start | bytes 245764
Sparse Core Ops, SparseCore 0:
  107.0 48.9 all-gather.1

commit v7 on v6

--- a/solution.py
+++ b/solution.py
@@ -198,11 +198,13 @@
     partial_out = lax.dynamic_update_slice_in_dim(
         partial_out, own_rows + residual.astype(jnp.float32), first_row, 0
     )
-    stream_rows = lax.psum(partial_out, ("y", "core")).astype(jnp.bfloat16)
-    stream = lax.dynamic_slice_in_dim(stream_rows, first_row, tokens_out, 0)
-    side_rows = lax.dynamic_index_in_dim(
-        stream_rows.reshape(y_count, core_count, tokens_out, columns), core, 1, keepdims=False
-    ).reshape(y_count * tokens_out, columns)
+    parts = partial_out.reshape(y_count, core_count, tokens_out, columns)
+    mine = lax.dynamic_index_in_dim(parts, core, 1, keepdims=False)
+    theirs = lax.dynamic_index_in_dim(parts, 1 - core, 1, keepdims=False)
+    side_partial = mine + lax.ppermute(theirs, "core", swap)
+    side_rows = lax.psum(side_partial, "y").astype(jnp.bfloat16)
+    stream = lax.dynamic_index_in_dim(side_rows, lax.axis_index("y"), 0, keepdims=False)
+    side_rows = side_rows.reshape(y_count * tokens_out, columns)
     side_stream = lax.all_gather(side_rows, "req", axis=1, tiled=True)
     wide_side = side_stream.astype(jnp.float32)
     mean_square = jnp.mean(wide_side * wide_side, axis=1, keepdims=True)

time: 255 us -> 235 us (0.922)
  blocking collectives: 137 us -> 48.8 us
  waiting for transfers between devices: 38.4 us -> 93 us
  starting transfers between devices: 0.68 us -> 9.08 us
  local copies, waits for them, and re-layouts: 18.5 us -> 24.8 us
  matrix products: 22.1 us -> 18.9 us
    all_to_all x1 -> x0, blocking collectives: 59.7 us -> none  [per_device(): received = lax.all_to_all(pieces, ('req', 'y'), 0, 0, tiled=True)]
    all_to_all x0 -> x1, waiting for transfers between devices: none -> 54.3 us  [per_device(): received = lax.all_to_all(pieces, ('req', 'y'), 0, 0, tiled=True)]
    psum x1, blocking collectives: 50.3 us -> 22.3 us  [per_device(): side_rows = lax.psum(side_partial, 'y').astype(jnp.bfloat16)]
    all_to_all x0 -> x1, starting transfers between devices: none -> 8.32 us  [per_device(): received = lax.all_to_all(pieces, ('req', 'y'), 0, 0, tiled=True)]
    dot_general x2, matrix products: 7.46 us -> 4.4 us  [hidden_of(): gate = jnp.dot(normed, gate_w, preferred_element_type=jnp.float32)]
  transfers between devices with their start and end apart: 4 -> 6, of which waited for: 1 -> 3; matrix products, arithmetic and copies ran while one was open for 10% -> 10% of each run, Pallas kernels for 0% -> 0%
where the time goes in v7:
time: 235 us; the launch traced here: 234 us
  waiting for transfers between devices  93 us (40%)
  blocking collectives  48.8 us (21%)
  local copies, waits for them, and re-layouts  24.8 us (11%)
  matrix products  18.9 us (8%)
  other arithmetic  14.7 us (6%)
  between operations  14.4 us (6%)
  Pallas kernels  10.6 us (5%)
  starting transfers between devices  9.08 us (4%)
    all_to_all x1, waiting for transfers between devices, per_device(): received = lax.all_to_all(pieces, ('req', 'y'), 0, 0, tiled=True)  54.3 us
    all_gather x1, waiting for transfers between devices, per_device(): side_stream = lax.all_gather(side_rows, 'req', axis=1, tiled=True)  36.8 us
    all_gather x1, blocking collectives, per_device(): lax.all_gather(attended, 'req', axis=0, tiled=True)  26.5 us
    psum x1, blocking collectives, per_device(): side_rows = lax.psum(side_partial, 'y').astype(jnp.bfloat16)  22.3 us
    pallas_call x1, Pallas kernels, cache_attention(): pl.pallas_call(functools.partial(_cache_kernel, scale=scale), grid_spec=g...  10.6 us
    reshape x2, local copies, waits for them, and re-layouts, blocks_of(): return down_w.reshape(down_w.shape[0], req_count, columns)  10 us
    all_to_all x1, starting transfers between devices, per_device(): received = lax.all_to_all(pieces, ('req', 'y'), 0, 0, tiled=True)  8.32 us
    dot_general x2, matrix products, down_of(): jnp.einsum('ysh,hrf->rysf', hidden, down_w, preferred_element_type=jnp.fl...  7.3 us
  transfers between devices with their start and end apart: 6, of which 3 were waited for; matrix products, arithmetic and copies ran while one was open for 10% of the time, Pallas kernels for 0%

profile of v7, /device:TPU:0, one launch (start us, length us, event | category | flops | bytes accessed | tf_op | source)
XLA Modules:
  0.0 234.4 jit_solution(17031268258703949919)
XLA Ops:
  6.5 1.6 convert_reduce_fusion.1
  8.8 1.6 reshape.47.owner_ref
  12.1 0.9 reshape_squeeze_reshape.4.q_ref
  13.0 0.9 fusion.16
  14.1 10.6 %shard_map.127 = (f32[224,1]{1,0:T(8,128)}, f32[224,1]{1,0:T(8,128)}, f32[224,128]{1,0:T(8,128)}) custom-call(s32[1]{0:T(128)} %bitcast.live_ref, bf16[224,128]{1,0:T(8,128)(2,1)} %copy-done.8, bf16[17920,128]{1,0:T(8,128)(2,1)} %k_ref.1, bf16[17920,128]{1,0:T(8,128)(2,1)} %v_ref.1, s32[1,17920]{1,0:T(1,128)} %reshape.47.owner_ref, ...), custom_call_target="tpu_custom_call" | custom-call | flops 2055208960 | bytes 9418752 | tf_op jit(solution)/shard_map/pallas_call | solution.py:86
  24.7 1.0 maximum_reduce_fusion
  26.0 1.1 fusion.14
  27.1 1.1 fusion.11
  28.4 26.5 %all_gather.6 = bf16[512,896]{1,0:T(8,128)(2,1)S(1)} all-gather(bf16[32,896]{1,0:T(8,128)(2,1)S(1)} %convert_element_type.55), channel_id=1, replica_groups=mesh['req'=16,'y'=4,'core'=2] {'req'}, dimensions={0}, use_global_device_ids=true | all-gather | bytes 974848 | tf_op jit(solution)/shard_map/all_gather | solution.py:191
  55.8 1.7 dynamic_update_slice.3
  58.0 1.9 collective-permute-done
  60.0 22.3 %all-reduce.1 = bf16[4,64,448]{2,1,0:T(8,128)(2,1)S(1)} all-reduce(f32[4,64,448]{2,1,0:T(8,128)S(1)} %bitcast_add_fusion), channel_id=1, replica_groups=mesh['req'=16,'y'=4,'core'=2] {'y'}, use_global_device_ids=true, to_apply=%region_3.4 | all-reduce | flops 114688 | bytes 688128 | tf_op jit(solution)/shard_map/psum | solution.py:205
  82.3 0.8 copy.46
  83.9 4.5 %reshape.51 = bf16[160,16,448]{2,1,0:T(8,128)(2,1)S(1)} reshape(bf16[160,7168]{1,0:T(8,128)(2,1)} %param.25) | data formatting | bytes 4587520 | tf_op jit(solution)/shard_map/reshape | solution.py:230
  88.4 5.6 %reshape.53 = bf16[160,16,448]{2,1,0:T(8,128)(2,1)} reshape(bf16[160,7168]{1,0:T(8,128)(2,1)} %collective-permute-done.3) | data formatting | bytes 4587520 | tf_op jit(solution)/shard_map/reshape | solution.py:230
  94.0 36.8 %all-gather.2.cloned.1.call-done = bf16[256,7168]{0,1:T(8,128)(2,1)} async-done(((bf16[256,448]{0,1:T(8,128)(2,1)}), bf16[256,7168]{0,1:T(8,128)(2,1)}) %all-gather.2.cloned.1.call-update) | async-done | bytes 3670032 | tf_op jit(solution)/shard_map/all_gather | solution.py:208
  130.7 3.2 %fusion = f32[256]{0:T(256)S(1)} fusion(bf16[256,7168]{0,1:T(8,128)(2,1)} %all-gather.2.cloned.1.call-done), kind=kLoop, calls=%fused_computation.4 | loop fusion | flops 5504768 | bytes 3671040 | tf_op jit(solution)/shard_map/reduce_sum | solution.py:210
  133.9 3.2 %fusion.2 = bf16[256,7168]{0,1:T(8,128)(2,1)S(1)} fusion(bf16[256,7168]{0,1:T(8,128)(2,1)S(1)} %copy-done.3, f32[7168]{0:T(1024)S(1)} %copy-done.10, f32[256]{0:T(256)S(1)} %add_rsqrt_fusion), kind=kLoop, calls=%fused_computation.6 | loop fusion | flops 7340032 | bytes 7369728 | tf_op jit(solution)/shard_map/convert_element_type | solution.py:211
  137.9 1.1 copy-done.1
  139.0 1.1 copy-done.12
  140.1 1.4 fusion.9
  141.5 1.0 copy.47
  142.5 3.6 %fusion.19 = f32[256,160]{0,1:T(8,128)S(1)} fusion(bf16[7168,160]{0,1:T(8,128)(2,1)} %collective-permute-done.1, bf16[256,7168]{0,1:T(8,128)(2,1)} %copy-done.1), kind=kOutput, calls=%fused_computation.39 | convolution fusion | flops 587202560 | bytes 6127616 | tf_op jit(solution)/shard_map/dot_general | solution.py:216
  146.3 3.1 %multiply_convert_fusion = bf16[256,160]{0,1:T(8,128)(2,1)} fusion(f32[256,160]{0,1:T(8,128)S(1)} %fusion.19, bf16[7168,160]{0,1:T(8,128)(2,1)} %collective-permute-done.2, bf16[256,7168]{0,1:T(8,128)(2,1)S(1)} %copy-done.2), kind=kOutput, calls=%fused_computation.23 | convolution fusion | flops 587448320 | bytes 6209536 | tf_op jit(solution)/shard_map/dot_general | solution.py:217
  149.4 1.6 copy.49
  151.0 3.6 %fusion.5 = f32[4,64,16,448]{3,1,2,0:T(8,128)S(1)} fusion(bf16[4,64,160,1]{2,1,3,0:T(8,128)(2,1)S(1)} %bitcast.51, bf16[160,16,448]{2,1,0:T(8,128)(2,1)S(1)} %reshape.51), kind=kOutput, calls=%fused_computation.9 | convolution fusion | flops 587202560 | bytes 9715712 | tf_op jit(solution)/shard_map/ysh,hrf->rysf/dot_general | solution.py:222
  154.6 3.7 %fusion.3 = bf16[16,4,64,448]{3,2,0,1:T(8,128)(2,1)S(1)} fusion(f32[4,64,16,448]{3,1,2,0:T(8,128)S(1)} %fusion.5, bf16[4,64,160,1]{2,1,3,0:T(8,128)(2,1)S(1)} %bitcast.52, bf16[160,16,448]{2,1,0:T(8,128)(2,1)S(1)} %copy-done.4), kind=kOutput, calls=%fused_computation.7 | convolution fusion | flops 590872576 | bytes 13385728 | tf_op jit(solution)/shard_map/ysh,hrf->rysf/dot_general | solution.py:222
  158.4 2.2 copy.51
  160.6 8.3 %all-to-all-start = ((bf16[64,64,448]{2,1,0:T(8,128)(2,1)}), bf16[64,64,448]{2,1,0:T(8,128)(2,1)}, u32[]{:S(2)}, u32[]{:S(2)}) async-start(bf16[64,64,448]{2,1,0:T(8,128)(2,1)} %bitcast.47), calls=%async_computation | async-start | bytes 8388608 | tf_op jit(solution)/shard_map/all_to_all | solution.py:236
  168.9 54.3 %all-to-all-done = bf16[64,64,448]{2,1,0:T(8,128)(2,1)} async-done(((bf16[64,64,448]{2,1,0:T(8,128)(2,1)}), bf16[64,64,448]{2,1,0:T(8,128)(2,1)}, u32[]{:S(2)}, u32[]{:S(2)}) %all-to-all-start) | async-done | bytes 3670048 | tf_op jit(solution)/shard_map/all_to_all | solution.py:236
  223.2 2.9 %convert_reduce_fusion = f32[64,448]{1,0:T(8,128)S(1)} fusion(bf16[64,64,448]{2,1,0:T(8,128)(2,1)} %all-to-all-done), kind=kLoop, calls=%fused_computation.2 | loop fusion | flops 3641344 | bytes 3784704 | tf_op jit(solution)/shard_map/reduce_sum | solution.py:237
  226.1 1.5 fusion.13
  (52 shorter events, 5.2 us)
Async XLA Ops:
  6.5 48.5 %copy-start = (bf16[896,448]{0,1:T(8,128)(2,1)S(1)}, bf16[896,448]{0,1:T(8,128)(2,1)}, u32[]{:S(2)}) copy-start(bf16[896,448]{0,1:T(8,128)(2,1)} %param.20) | copy-start | bytes 2408452
  6.5 124.2 %all-gather.2.cloned.1.call-start = ((), (), s32[]{:S(2)}) async-start(), calls=%async_computation.1 | async-start | bytes 3899392 | tf_op jit(solution)/shard_map/all_gather | solution.py:208
  13.0 1.1 copy-start.8
  14.0 11.7 %copy-start.11 = (s32[32]{0:T(128)S(1)}, s32[32]{0:T(128)}, u32[]{:S(2)}) copy-start(s32[32]{0:T(128)} %param.18) | copy-start | bytes 388
  14.1 13.0 %copy-start.13 = (bf16[32,128]{1,0:T(8,128)(2,1)S(1)}, bf16[32,128]{1,0:T(8,128)(2,1)}, u32[]{:S(2)}) copy-start(bf16[32,128]{1,0:T(8,128)(2,1)} %param.15) | copy-start | bytes 24580
  14.1 14.2 %copy-start.9 = (bf16[64,448]{1,0:T(8,128)(2,1)S(1)}, bf16[64,448]{1,0:T(8,128)(2,1)}, u32[]{:S(2)}) copy-start(bf16[64,448]{1,0:T(8,128)(2,1)} %param.21) | copy-start | bytes 172036
  58.0 2.0 collective-permute-start
  82.3 1.5 copy-start.6
  83.2 5.2 %collective-permute-start.3 = (bf16[160,7168]{1,0:T(8,128)(2,1)}, bf16[160,7168]{1,0:T(8,128)(2,1)}, u32[]{:S(2)}, u32[]{:S(2)}) collective-permute-start(bf16[160,7168]{1,0:T(8,128)(2,1)} %param.25), channel_id=1, source_target_pairs={{0,1},{1,0},{2,3},{3,2},{4,5},{5,4},{6,7},{7,6},{8,9},{9,8},{10,11... | collective-permute-start | bytes 6881288 | tf_op jit(solution)/shard_map/ppermute | solution.py:188
  83.3 59.2 %collective-permute-start.1 = (bf16[7168,160]{0,1:T(8,128)(2,1)}, bf16[7168,160]{0,1:T(8,128)(2,1)}, u32[]{:S(2)}, u32[]{:S(2)}) collective-permute-start(bf16[7168,160]{0,1:T(8,128)(2,1)} %param.23), channel_id=1, source_target_pairs={{0,1},{1,0},{2,3},{3,2},{4,5},{5,4},{6,7},{7,6},{8,9},{9,8},{10,11... | collective-permute-start | bytes 6881288 | tf_op jit(solution)/shard_map/ppermute | solution.py:186
  83.8 62.4 %collective-permute-start.2 = (bf16[7168,160]{0,1:T(8,128)(2,1)}, bf16[7168,160]{0,1:T(8,128)(2,1)}, u32[]{:S(2)}, u32[]{:S(2)}) collective-permute-start(bf16[7168,160]{0,1:T(8,128)(2,1)} %param.24), channel_id=1, source_target_pairs={{0,1},{1,0},{2,3},{3,2},{4,5},{5,4},{6,7},{7,6},{8,9},{9,8},{10,11... | collective-permute-start | bytes 6881288 | tf_op jit(solution)/shard_map/ppermute | solution.py:187
  88.3 45.6 %copy-start.10 = (f32[7168]{0:T(1024)S(1)}, f32[7168]{0:T(1024)}, u32[]{:S(2)}) copy-start(f32[7168]{0:T(1024)} %param.22) | copy-start | bytes 86020
  130.7 3.2 %copy-start.3 = (bf16[256,7168]{0,1:T(8,128)(2,1)S(1)}, bf16[256,7168]{0,1:T(8,128)(2,1)}, u32[]{:S(2)}) copy-start(bf16[256,7168]{0,1:T(8,128)(2,1)} %all-gather.2.cloned.1.call-done) | copy-start | bytes 11010052
  133.9 3.2 %copy-start.5 = (bf16[7168,160]{0,1:T(8,128)(2,1)S(1)}, bf16[7168,160]{0,1:T(8,128)(2,1)}, u32[]{:S(2)}) copy-start(bf16[7168,160]{0,1:T(8,128)(2,1)} %param.23) | copy-start | bytes 6881284
  137.1 1.9 copy-start.1
  137.1 3.0 %copy-start.12 = (bf16[7168,160]{0,1:T(8,128)(2,1)S(1)}, bf16[7168,160]{0,1:T(8,128)(2,1)}, u32[]{:S(2)}) copy-start(bf16[7168,160]{0,1:T(8,128)(2,1)} %param.24) | copy-start | bytes 6881284
  142.5 3.8 %copy-start.2 = (bf16[256,7168]{0,1:T(8,128)(2,1)S(1)}, bf16[256,7168]{0,1:T(8,128)(2,1)}, u32[]{:S(2)}) copy-start(bf16[256,7168]{0,1:T(8,128)(2,1)} %copy-done.1) | copy-start | bytes 11010052
  151.0 3.6 %copy-start.4 = (bf16[160,16,448]{2,1,0:T(8,128)(2,1)S(1)}, bf16[160,16,448]{2,1,0:T(8,128)(2,1)}, u32[]{:S(2)}) copy-start(bf16[160,16,448]{2,1,0:T(8,128)(2,1)} %reshape.53) | copy-start | bytes 6881284
  151.0 3.6 %copy-start.7 = (bf16[256,160]{1,0:T(8,128)(2,1)S(1)}, bf16[256,160]{1,0:T(8,128)(2,1)}, u32[]{:S(2)}) copy-start(bf16[256,160]{1,0:T(8,128)(2,1)} %copy.49) | copy-start | bytes 245764
  160.6 62.6 %all-to-all-start = ((bf16[64,64,448]{2,1,0:T(8,128)(2,1)}), bf16[64,64,448]{2,1,0:T(8,128)(2,1)}, u32[]{:S(2)}, u32[]{:S(2)}) async-start(bf16[64,64,448]{2,1,0:T(8,128)(2,1)} %bitcast.47), calls=%async_computation | async-start | bytes 8388608 | tf_op jit(solution)/shard_map/all_to_all | solution.py:236
Sparse Core Ops, SparseCore 0:
  83.3 47.3 all-gather.1

commit v8 on v7

--- a/solution.py
+++ b/solution.py
@@ -212,29 +212,32 @@
         jnp.bfloat16
     )
 
-    def hidden_of(gate_w, up_w):
-        gate = jnp.dot(normed, gate_w, preferred_element_type=jnp.float32)
-        up = jnp.dot(normed, up_w, preferred_element_type=jnp.float32)
-        hidden = (jax.nn.silu(gate) * up).astype(jnp.bfloat16)
-        return hidden.reshape(y_count, tokens_out, hidden.shape[1])
+    normed_blocks = normed.reshape(y_count, tokens_out, normed.shape[1])
+
+    def hidden_of(rows, gate_w, up_w):
+        gate = jnp.dot(rows, gate_w, preferred_element_type=jnp.float32)
+        up = jnp.dot(rows, up_w, preferred_element_type=jnp.float32)
+        return (jax.nn.silu(gate) * up).astype(jnp.bfloat16)
 
     def down_of(hidden, down_w):
         return jnp.einsum(
             "ysh,hrf->rysf",
-            hidden,
-            down_w,
+            hidden.reshape(y_count, -1, hidden.shape[1]),
+            down_w.reshape(down_w.shape[0], req_count, columns),
             preferred_element_type=jnp.float32,
         )
 
-    def blocks_of(down_w):
-        return down_w.reshape(down_w.shape[0], req_count, columns)
-
-    product = down_of(hidden_of(gate_weight, up_weight), blocks_of(down_weight)) + down_of(
-        hidden_of(gate_partner, up_partner), blocks_of(down_partner)
-    )
-    pieces = product.astype(jnp.bfloat16).reshape(req_count * y_count, tokens_out, columns)
-    received = lax.all_to_all(pieces, ("req", "y"), 0, 0, tiled=True)
-    summed = jnp.sum(received.astype(jnp.float32), axis=0)
+    halves = []
+    half = tokens_out // 2
+    for first in range(0, tokens_out, half):
+        rows = normed_blocks[:, first : first + half].reshape(y_count * half, -1)
+        product = down_of(hidden_of(rows, gate_weight, up_weight), down_weight) + down_of(
+            hidden_of(rows, gate_partner, up_partner), down_partner
+        )
+        pieces = product.astype(jnp.bfloat16).reshape(req_count * y_count, half, columns)
+        received = lax.all_to_all(pieces, ("req", "y"), 0, 0, tiled=True)
+        halves.append(jnp.sum(received.astype(jnp.float32), axis=0))
+    summed = jnp.concatenate(halves, axis=0)
     return (stream.astype(jnp.float32) + summed).astype(jnp.bfloat16)
 
 

time: 235 us -> 244 us (1.038)
  matrix products: 18.9 us -> 39.8 us
  waiting for transfers between devices: 93 us -> 76.6 us
  starting transfers between devices: 9.08 us -> 15.1 us
  other arithmetic: 14.7 us -> 11.1 us
    dot_general x6 -> x12, matrix products: 16.2 us -> 37.1 us  [the longest x4 17.1 us: down_of(): jnp.einsum('ysh,hrf->rysf', hidden.reshape(y_count, -1, hidden.shape[1]),...]
    all_to_all x1 -> x2, waiting for transfers between devices: 54.3 us -> 37.4 us  [per_device(): received = lax.all_to_all(pieces, ('req', 'y'), 0, 0, tiled=True)]
    all_to_all x1 -> x2, starting transfers between devices: 8.32 us -> 14.4 us  [per_device(): received = lax.all_to_all(pieces, ('req', 'y'), 0, 0, tiled=True)]
    all_gather x0 -> x1, local copies, waits for them, and re-layouts: none -> 5.94 us  [per_device(): side_stream = lax.all_gather(side_rows, 'req', axis=1, tiled=True)]
  transfers between devices with their start and end apart: 6 -> 7, of which waited for: 3 -> 4; matrix products, arithmetic and copies ran while one was open for 10% -> 20% of each run, Pallas kernels for 0% -> 0%
where the time goes in v8:
time: 244 us; the launch traced here: 243 us
  waiting for transfers between devices  76.6 us (31%)
  blocking collectives  48.8 us (20%)
  matrix products  39.8 us (16%)
  local copies, waits for them, and re-layouts  26.8 us (11%)
  starting transfers between devices  15.1 us (6%)
  between operations  14.5 us (6%)
  other arithmetic  11.1 us (5%)
  Pallas kernels  10.7 us (4%)
    all_to_all x2, waiting for transfers between devices, per_device(): received = lax.all_to_all(pieces, ('req', 'y'), 0, 0, tiled=True)  37.4 us
    all_gather x1, waiting for transfers between devices, per_device(): side_stream = lax.all_gather(side_rows, 'req', axis=1, tiled=True)  37.3 us
    all_gather x1, blocking collectives, per_device(): lax.all_gather(attended, 'req', axis=0, tiled=True)  26.5 us
    psum x1, blocking collectives, per_device(): side_rows = lax.psum(side_partial, 'y').astype(jnp.bfloat16)  22.3 us
    dot_general x4, matrix products, down_of(): jnp.einsum('ysh,hrf->rysf', hidden.reshape(y_count, -1, hidden.shape[1]),...  17.1 us
    all_to_all x2, starting transfers between devices, per_device(): received = lax.all_to_all(pieces, ('req', 'y'), 0, 0, tiled=True)  14.4 us
    pallas_call x1, Pallas kernels, cache_attention(): pl.pallas_call(functools.partial(_cache_kernel, scale=scale), grid_spec=g...  10.7 us
    dot_general x4, matrix products, hidden_of(): gate = jnp.dot(rows, gate_w, preferred_element_type=jnp.float32)  10.4 us
  transfers between devices with their start and end apart: 7, of which 4 were waited for; matrix products, arithmetic and copies ran while one was open for 20% of the time, Pallas kernels for 0%

profile of v8, /device:TPU:0, one launch (start us, length us, event | category | flops | bytes accessed | tf_op | source)
XLA Modules:
  0.0 243.4 jit_solution(5943104757159952078)
XLA Ops:
  6.5 1.6 convert_reduce_fusion.2
  8.8 1.6 reshape.67.owner_ref
  14.1 10.7 %shard_map.127 = (f32[224,1]{1,0:T(8,128)}, f32[224,1]{1,0:T(8,128)}, f32[224,128]{1,0:T(8,128)}) custom-call(s32[1]{0:T(128)} %bitcast.live_ref, bf16[224,128]{1,0:T(8,128)(2,1)} %copy-done.7, bf16[17920,128]{1,0:T(8,128)(2,1)} %k_ref.1, bf16[17920,128]{1,0:T(8,128)(2,1)} %v_ref.1, s32[1,17920]{1,0:T(1,128)} %reshape.67.owner_ref, ...), custom_call_target="tpu_custom_call" | custom-call | flops 2055208960 | bytes 9418752 | tf_op jit(solution)/shard_map/pallas_call | solution.py:86
  26.0 1.1 fusion.27
  28.4 26.5 %all_gather.6 = bf16[512,896]{1,0:T(8,128)(2,1)S(1)} all-gather(bf16[32,896]{1,0:T(8,128)(2,1)S(1)} %convert_element_type.70), channel_id=1, replica_groups=mesh['req'=16,'y'=4,'core'=2] {'req'}, dimensions={0}, use_global_device_ids=true | all-gather | bytes 974848 | tf_op jit(solution)/shard_map/all_gather | solution.py:191
  55.8 1.7 dynamic_update_slice.3
  58.1 1.9 collective-permute-done
  60.0 22.3 %all-reduce.1 = bf16[4,64,448]{2,1,0:T(8,128)(2,1)S(1)} all-reduce(f32[4,64,448]{2,1,0:T(8,128)S(1)} %bitcast_add_fusion), channel_id=1, replica_groups=mesh['req'=16,'y'=4,'core'=2] {'y'}, use_global_device_ids=true, to_apply=%region_3.4 | all-reduce | flops 114688 | bytes 688128 | tf_op jit(solution)/shard_map/psum | solution.py:205
  83.9 5.5 %reshape.73 = bf16[160,16,448]{2,1,0:T(8,128)(2,1)} reshape(bf16[160,7168]{1,0:T(8,128)(2,1)} %param.25) | data formatting | bytes 4587520 | tf_op jit(solution)/shard_map/reshape | solution.py:226
  89.4 4.0 %reshape.75 = bf16[160,16,448]{2,1,0:T(8,128)(2,1)} reshape(bf16[160,7168]{1,0:T(8,128)(2,1)S(1)} %collective-permute-done.3) | data formatting | bytes 4587520 | tf_op jit(solution)/shard_map/reshape | solution.py:226
  93.4 37.3 %all-gather.2.cloned.1.call-done = bf16[256,7168]{0,1:T(8,128)(2,1)} async-done(((bf16[256,448]{0,1:T(8,128)(2,1)}), bf16[256,7168]{0,1:T(8,128)(2,1)}) %all-gather.2.cloned.1.call-update) | async-done | bytes 3670032 | tf_op jit(solution)/shard_map/all_gather | solution.py:208
  130.7 5.9 %copy.60 = bf16[256,7168]{1,0:T(8,128)(2,1)} copy(bf16[256,7168]{0,1:T(8,128)(2,1)} %all-gather.2.cloned.1.call-done) | data formatting | bytes 7340032 | tf_op jit(solution)/shard_map/all_gather | solution.py:208
  136.7 3.0 %fusion = f32[256]{0:T(256)S(1)} fusion(bf16[256,7168]{1,0:T(8,128)(2,1)} %copy.60), kind=kLoop, calls=%fused_computation.2 | loop fusion | flops 5504768 | bytes 3671040 | tf_op jit(solution)/shard_map/reduce_sum | solution.py:210
  141.1 3.1 %fusion.34 = f32[128,160]{0,1:T(8,128)S(1)} fusion(bf16[128,7168]{1,0:T(8,128)(2,1)S(1)} %bitcast.87, bf16[7168,160]{0,1:T(8,128)(2,1)} %param.23), kind=kOutput, calls=%fused_computation.54 | convolution fusion | flops 293601280 | bytes 4210688 | tf_op jit(solution)/shard_map/dot_general | solution.py:218
  144.2 2.4 fusion.24
  146.7 2.5 %fusion.32 = f32[128,160]{0,1:T(8,128)S(1)} fusion(bf16[128,7168]{1,0:T(8,128)(2,1)S(1)} %bitcast.83, bf16[7168,160]{0,1:T(8,128)(2,1)} %param.23), kind=kOutput, calls=%fused_computation.52 | convolution fusion | flops 293601280 | bytes 4210688 | tf_op jit(solution)/shard_map/dot_general | solution.py:218
  149.3 2.4 fusion.35
  151.7 2.4 multiply_convert_fusion
  154.2 5.2 %fusion.7 = f32[4,32,16,448]{3,1,2,0:T(8,128)S(1)} fusion(bf16[4,32,160,1]{2,1,3,0:T(8,128)(2,1)S(1)} %bitcast.96, bf16[160,16,448]{2,1,0:T(8,128)(2,1)} %reshape.73), kind=kOutput, calls=%fused_computation.13 | convolution fusion | flops 293601280 | bytes 6004736 | tf_op jit(solution)/shard_map/ysh,hrf->rysf/dot_general | solution.py:223
  159.4 3.4 %fusion.16 = bf16[16,4,32,448]{3,2,0,1:T(8,128)(2,1)S(1)} fusion(f32[4,32,16,448]{3,1,2,0:T(8,128)S(1)} %fusion.7, bf16[4,32,160,1]{2,1,3,0:T(8,128)(2,1)S(1)} %bitcast.99, bf16[160,16,448]{2,1,0:T(8,128)(2,1)S(1)} %copy-done.5), kind=kOutput, calls=%fused_computation.22 | convolution fusion | flops 295436288 | bytes 7839744 | tf_op jit(solution)/shard_map/ysh,hrf->rysf/dot_general | solution.py:223
  162.8 1.4 copy.70
  164.2 8.3 %all-to-all-start.1 = ((bf16[64,32,448]{2,1,0:T(8,128)(2,1)}), bf16[64,32,448]{2,1,0:T(8,128)(2,1)}, u32[]{:S(2)}, u32[]{:S(2)}) async-start(bf16[64,32,448]{2,1,0:T(8,128)(2,1)} %bitcast.92), calls=%async_computation.1 | async-start | bytes 4194304 | tf_op jit(solution)/shard_map/all_to_all | solution.py:238
  172.6 2.4 fusion.23
  175.1 2.4 fusion.33
  177.5 2.4 multiply_convert_fusion.1
  180.0 5.2 %fusion.9 = f32[4,32,16,448]{3,1,2,0:T(8,128)S(1)} fusion(bf16[4,32,160,1]{2,1,3,0:T(8,128)(2,1)S(1)} %bitcast.97, bf16[160,16,448]{2,1,0:T(8,128)(2,1)} %reshape.73), kind=kOutput, calls=%fused_computation.15 | convolution fusion | flops 293601280 | bytes 6004736 | tf_op jit(solution)/shard_map/ysh,hrf->rysf/dot_general | solution.py:223
  185.2 3.4 %fusion.15 = bf16[16,4,32,448]{3,2,0,1:T(8,128)(2,1)S(1)} fusion(f32[4,32,16,448]{3,1,2,0:T(8,128)S(1)} %fusion.9, bf16[4,32,160,1]{2,1,3,0:T(8,128)(2,1)S(1)} %bitcast.98, bf16[160,16,448]{2,1,0:T(8,128)(2,1)S(1)} %copy-done.6), kind=kOutput, calls=%fused_computation.21 | convolution fusion | flops 295436288 | bytes 7839744 | tf_op jit(solution)/shard_map/ysh,hrf->rysf/dot_general | solution.py:223
  188.6 1.5 copy.65
  190.1 11.8 %all-to-all-done.1 = bf16[64,32,448]{2,1,0:T(8,128)(2,1)} async-done(((bf16[64,32,448]{2,1,0:T(8,128)(2,1)}), bf16[64,32,448]{2,1,0:T(8,128)(2,1)}, u32[]{:S(2)}, u32[]{:S(2)}) %all-to-all-start.1) | async-done | bytes 1835040 | tf_op jit(solution)/shard_map/all_to_all | solution.py:238
  201.8 6.0 %all-to-all-start = ((bf16[64,32,448]{2,1,0:T(8,128)(2,1)}), bf16[64,32,448]{2,1,0:T(8,128)(2,1)S(1)}, u32[]{:S(2)}, u32[]{:S(2)}) async-start(bf16[64,32,448]{2,1,0:T(8,128)(2,1)} %bitcast.19), calls=%async_computation | async-start | bytes 4194304 | tf_op jit(solution)/shard_map/all_to_all | solution.py:238
  207.9 2.0 convert_reduce_fusion
  209.9 25.6 %all-to-all-done = bf16[64,32,448]{2,1,0:T(8,128)(2,1)S(1)} async-done(((bf16[64,32,448]{2,1,0:T(8,128)(2,1)}), bf16[64,32,448]{2,1,0:T(8,128)(2,1)S(1)}, u32[]{:S(2)}, u32[]{:S(2)}) %all-to-all-start) | async-done | bytes 1835040 | tf_op jit(solution)/shard_map/all_to_all | solution.py:238
  (62 shorter events, 11.9 us)
Async XLA Ops:
  6.5 48.5 %copy-start = (bf16[896,448]{0,1:T(8,128)(2,1)S(1)}, bf16[896,448]{0,1:T(8,128)(2,1)}, u32[]{:S(2)}) copy-start(bf16[896,448]{0,1:T(8,128)(2,1)} %param.20) | copy-start | bytes 2408452
  6.5 124.2 %all-gather.2.cloned.1.call-start = ((), (), s32[]{:S(2)}) async-start(), calls=%async_computation.2 | async-start | bytes 3899392 | tf_op jit(solution)/shard_map/all_gather | solution.py:208
  13.0 1.1 copy-start.7
  14.0 11.7 %copy-start.10 = (s32[32]{0:T(128)S(1)}, s32[32]{0:T(128)}, u32[]{:S(2)}) copy-start(s32[32]{0:T(128)} %param.18) | copy-start | bytes 388
  14.1 13.0 %copy-start.11 = (bf16[32,128]{1,0:T(8,128)(2,1)S(1)}, bf16[32,128]{1,0:T(8,128)(2,1)}, u32[]{:S(2)}) copy-start(bf16[32,128]{1,0:T(8,128)(2,1)} %param.15) | copy-start | bytes 24580
  14.1 14.2 %copy-start.8 = (bf16[64,448]{1,0:T(8,128)(2,1)S(1)}, bf16[64,448]{1,0:T(8,128)(2,1)}, u32[]{:S(2)}) copy-start(bf16[64,448]{1,0:T(8,128)(2,1)} %param.21) | copy-start | bytes 172036
  58.0 2.0 collective-permute-start
  83.2 6.2 %collective-permute-start.3 = (bf16[160,7168]{1,0:T(8,128)(2,1)}, bf16[160,7168]{1,0:T(8,128)(2,1)S(1)}, u32[]{:S(2)}, u32[]{:S(2)}) collective-permute-start(bf16[160,7168]{1,0:T(8,128)(2,1)} %param.25), channel_id=1, source_target_pairs={{0,1},{1,0},{2,3},{3,2},{4,5},{5,4},{6,7},{7,6},{8,9},{9,8},{10,11... | collective-permute-start | bytes 6881288 | tf_op jit(solution)/shard_map/ppermute | solution.py:188
  83.3 66.0 %collective-permute-start.1 = (bf16[7168,160]{0,1:T(8,128)(2,1)}, bf16[7168,160]{0,1:T(8,128)(2,1)}, u32[]{:S(2)}, u32[]{:S(2)}) collective-permute-start(bf16[7168,160]{0,1:T(8,128)(2,1)} %param.23), channel_id=1, source_target_pairs={{0,1},{1,0},{2,3},{3,2},{4,5},{5,4},{6,7},{7,6},{8,9},{9,8},{10,11... | collective-permute-start | bytes 6881288 | tf_op jit(solution)/shard_map/ppermute | solution.py:186
  83.8 67.9 %collective-permute-start.2 = (bf16[7168,160]{0,1:T(8,128)(2,1)}, bf16[7168,160]{0,1:T(8,128)(2,1)}, u32[]{:S(2)}, u32[]{:S(2)}) collective-permute-start(bf16[7168,160]{0,1:T(8,128)(2,1)} %param.24), channel_id=1, source_target_pairs={{0,1},{1,0},{2,3},{3,2},{4,5},{5,4},{6,7},{7,6},{8,9},{9,8},{10,11... | collective-permute-start | bytes 6881288 | tf_op jit(solution)/shard_map/ppermute | solution.py:187
  130.7 9.0 %copy-start.9 = (f32[7168]{0:T(1024)S(1)}, f32[7168]{0:T(1024)}, u32[]{:S(2)}) copy-start(f32[7168]{0:T(1024)} %param.22) | copy-start | bytes 86020
  136.7 3.1 %copy-start.4 = (bf16[256,7168]{1,0:T(8,128)(2,1)S(1)}, bf16[256,7168]{1,0:T(8,128)(2,1)}, u32[]{:S(2)}) copy-start(bf16[256,7168]{1,0:T(8,128)(2,1)} %copy.60) | copy-start | bytes 11010052
  141.1 3.1 %copy-start.2 = (bf16[4,32,7168]{2,1,0:T(8,128)(2,1)}, bf16[4,32,7168]{2,1,0:T(8,128)(2,1)S(1)}, u32[]{:S(2)}) copy-start(bf16[4,32,7168]{2,1,0:T(8,128)(2,1)S(1)} %get-tuple-element.16) | copy-start | bytes 5505028
  146.7 2.6 %copy-start.3 = (bf16[4,32,7168]{2,1,0:T(8,128)(2,1)S(1)}, bf16[4,32,7168]{2,1,0:T(8,128)(2,1)}, u32[]{:S(2)}) copy-start(bf16[4,32,7168]{2,1,0:T(8,128)(2,1)} %copy-done.2) | copy-start | bytes 5505028
  154.2 5.2 %copy-start.5 = (bf16[160,16,448]{2,1,0:T(8,128)(2,1)S(1)}, bf16[160,16,448]{2,1,0:T(8,128)(2,1)}, u32[]{:S(2)}) copy-start(bf16[160,16,448]{2,1,0:T(8,128)(2,1)} %reshape.75) | copy-start | bytes 6881284
  164.2 37.6 %all-to-all-start.1 = ((bf16[64,32,448]{2,1,0:T(8,128)(2,1)}), bf16[64,32,448]{2,1,0:T(8,128)(2,1)}, u32[]{:S(2)}, u32[]{:S(2)}) async-start(bf16[64,32,448]{2,1,0:T(8,128)(2,1)} %bitcast.92), calls=%async_computation.1 | async-start | bytes 4194304 | tf_op jit(solution)/shard_map/all_to_all | solution.py:238
  180.0 5.2 %copy-start.6 = (bf16[160,16,448]{2,1,0:T(8,128)(2,1)S(1)}, bf16[160,16,448]{2,1,0:T(8,128)(2,1)}, u32[]{:S(2)}) copy-start(bf16[160,16,448]{2,1,0:T(8,128)(2,1)} %reshape.75) | copy-start | bytes 6881284
  201.8 33.7 %all-to-all-start = ((bf16[64,32,448]{2,1,0:T(8,128)(2,1)}), bf16[64,32,448]{2,1,0:T(8,128)(2,1)S(1)}, u32[]{:S(2)}, u32[]{:S(2)}) async-start(bf16[64,32,448]{2,1,0:T(8,128)(2,1)} %bitcast.19), calls=%async_computation | async-start | bytes 4194304 | tf_op jit(solution)/shard_map/all_to_all | solution.py:238
  207.9 28.6 %copy-start.1 = (bf16[896,448]{0,1:T(8,128)(2,1)S(1)}, bf16[896,448]{0,1:T(8,128)(2,1)}, u32[]{:S(2)}) copy-start(bf16[896,448]{0,1:T(8,128)(2,1)} %param.20) | copy-start | bytes 2408452
Sparse Core Ops, SparseCore 0:
  83.3 47.3 all-gather.1

commit v9 on v7

--- a/solution.py
+++ b/solution.py
@@ -187,8 +187,15 @@
     up_partner = lax.ppermute(up_weight, "core", swap)
     down_partner = lax.ppermute(down_weight, "core", swap)
     attended = attend(queries, new_keys, new_values, cache_keys, cache_values, tok_req, cache_req)
+    shifted = [attended] + [
+        lax.ppermute(attended, "req", [(j, (j + k) % req_count) for j in range(req_count)])
+        for k in range(1, req_count)
+    ]
+    by_distance = jnp.stack(shifted)
+    order = (lax.axis_index("req") - jnp.arange(req_count, dtype=jnp.int32)) % req_count
+    all_groups = jnp.take(by_distance, order, axis=0).reshape(-1, attended.shape[1])
     partial_out = jnp.dot(
-        lax.all_gather(attended, "req", axis=0, tiled=True),
+        all_groups,
         out_weight,
         preferred_element_type=jnp.float32,
     )

time: 235 us -> 291 us (1.24)
  waiting for transfers between devices: 93 us -> 165 us
  blocking collectives: 48.8 us -> 22.3 us
  starting transfers between devices: 9.08 us -> 21.1 us
    ppermute x0 -> x15, waiting for transfers between devices: none -> 71.2 us  [per_device(): lax.ppermute(attended, 'req', [(j, (j + k) % req_count) for j in range(re...]
    all_gather x1 -> x0, blocking collectives: 26.5 us -> none  [per_device(): lax.all_gather(attended, 'req', axis=0, tiled=True)]
    ppermute x0 -> x15, starting transfers between devices: none -> 12 us  [per_device(): lax.ppermute(attended, 'req', [(j, (j + k) % req_count) for j in range(re...]
  transfers between devices with their start and end apart: 6 -> 21, of which waited for: 3 -> 14; matrix products, arithmetic and copies ran while one was open for 10% -> 8% of each run, Pallas kernels for 0% -> 0%
where the time goes in v9:
time: 291 us; the launch traced here: 290 us
  waiting for transfers between devices  165 us (57%)
  local copies, waits for them, and re-layouts  23.5 us (8%)
  blocking collectives  22.3 us (8%)
  starting transfers between devices  21.1 us (7%)
  matrix products  17.6 us (6%)
  other arithmetic  15 us (5%)
  between operations  14.6 us (5%)
  Pallas kernels  10.6 us (4%)
    ppermute x15, waiting for transfers between devices, per_device(): lax.ppermute(attended, 'req', [(j, (j + k) % req_count) for j in range(re...  71.2 us
    all_to_all x1, waiting for transfers between devices, per_device(): received = lax.all_to_all(pieces, ('req', 'y'), 0, 0, tiled=True)  54.2 us
    all_gather x1, waiting for transfers between devices, per_device(): side_stream = lax.all_gather(side_rows, 'req', axis=1, tiled=True)  37.8 us
    psum x1, blocking collectives, per_device(): side_rows = lax.psum(side_partial, 'y').astype(jnp.bfloat16)  22.3 us
    ppermute x15, starting transfers between devices, per_device(): lax.ppermute(attended, 'req', [(j, (j + k) % req_count) for j in range(re...  12 us
    pallas_call x1, Pallas kernels, cache_attention(): pl.pallas_call(functools.partial(_cache_kernel, scale=scale), grid_spec=g...  10.6 us
    reshape x2, local copies, waits for them, and re-layouts, blocks_of(): return down_w.reshape(down_w.shape[0], req_count, columns)  10 us
    all_to_all x1, starting transfers between devices, per_device(): received = lax.all_to_all(pieces, ('req', 'y'), 0, 0, tiled=True)  8.31 us
  transfers between devices with their start and end apart: 21, of which 14 were waited for; matrix products, arithmetic and copies ran while one was open for 8% of the time, Pallas kernels for 0%

profile of v9, /device:TPU:0, one launch (start us, length us, event | category | flops | bytes accessed | tf_op | source)
XLA Modules:
  0.0 290.0 jit_solution(11553787134500254468)
XLA Ops:
  6.5 1.6 convert_reduce_fusion.1
  14.1 10.6 %shard_map.127 = (f32[224,1]{1,0:T(8,128)}, f32[224,1]{1,0:T(8,128)}, f32[224,128]{1,0:T(8,128)}) custom-call(s32[1]{0:T(128)} %bitcast.live_ref, bf16[224,128]{1,0:T(8,128)(2,1)} %copy-done.8, bf16[17920,128]{1,0:T(8,128)(2,1)} %k_ref.1, bf16[17920,128]{1,0:T(8,128)(2,1)} %v_ref.1, s32[1,17920]{1,0:T(1,128)} %reshape.115.owner_ref, ...), custom_call_target="tpu_custom_call" | custom-call | flops 2055208960 | bytes 9418752 | tf_op jit(solution)/shard_map/pallas_call | solution.py:86
  28.3 3.8 %collective-permute-start.14 = (bf16[32,896]{1,0:T(8,128)(2,1)S(1)}, bf16[32,896]{1,0:T(8,128)(2,1)S(1)}, u32[]{:S(2)}, u32[]{:S(2)}) collective-permute-start(bf16[32,896]{1,0:T(8,128)(2,1)S(1)} %convert_element_type.66), channel_id=1, source_target_pairs={{0,120},{8,0},{16,8},{24,16},{32,24},{40,32},{48,40},{56,48},{64,5... | collective-permute-start | bytes 172040 | tf_op jit(solution)/shard_map/ppermute | solution.py:191
  32.1 4.7 %collective-permute-start.13 = (bf16[32,896]{1,0:T(8,128)(2,1)S(1)}, bf16[32,896]{1,0:T(8,128)(2,1)S(1)}, u32[]{:S(2)}, u32[]{:S(2)}) collective-permute-start(bf16[32,896]{1,0:T(8,128)(2,1)S(1)} %convert_element_type.66), channel_id=1, source_target_pairs={{0,112},{8,120},{16,0},{24,8},{32,16},{40,24},{48,32},{56,40},{64,... | collective-permute-start | bytes 172040 | tf_op jit(solution)/shard_map/ppermute | solution.py:191
  36.8 2.1 collective-permute-start.11
  39.4 7.0 %collective-permute-done = bf16[32,896]{1,0:T(8,128)(2,1)S(1)} collective-permute-done((bf16[32,896]{1,0:T(8,128)(2,1)S(1)}, bf16[32,896]{1,0:T(8,128)(2,1)S(1)}, u32[]{:S(2)}, u32[]{:S(2)}) %collective-permute-start) | collective-permute-done | bytes 57376 | tf_op jit(solution)/shard_map/ppermute | solution.py:191
  46.5 7.8 %collective-permute-done.1 = bf16[32,896]{1,0:T(8,128)(2,1)S(1)} collective-permute-done((bf16[32,896]{1,0:T(8,128)(2,1)S(1)}, bf16[32,896]{1,0:T(8,128)(2,1)S(1)}, u32[]{:S(2)}, u32[]{:S(2)}) %collective-permute-start.1) | collective-permute-done | bytes 57376 | tf_op jit(solution)/shard_map/ppermute | solution.py:191
  54.3 6.4 %collective-permute-done.2 = bf16[32,896]{1,0:T(8,128)(2,1)S(1)} collective-permute-done((bf16[32,896]{1,0:T(8,128)(2,1)S(1)}, bf16[32,896]{1,0:T(8,128)(2,1)S(1)}, u32[]{:S(2)}, u32[]{:S(2)}) %collective-permute-start.2) | collective-permute-done | bytes 57376 | tf_op jit(solution)/shard_map/ppermute | solution.py:191
  60.7 5.4 %collective-permute-done.3 = bf16[32,896]{1,0:T(8,128)(2,1)S(1)} collective-permute-done((bf16[32,896]{1,0:T(8,128)(2,1)S(1)}, bf16[32,896]{1,0:T(8,128)(2,1)S(1)}, u32[]{:S(2)}, u32[]{:S(2)}) %collective-permute-start.3) | collective-permute-done | bytes 57376 | tf_op jit(solution)/shard_map/ppermute | solution.py:191
  66.1 7.8 %collective-permute-done.4 = bf16[32,896]{1,0:T(8,128)(2,1)S(1)} collective-permute-done((bf16[32,896]{1,0:T(8,128)(2,1)S(1)}, bf16[32,896]{1,0:T(8,128)(2,1)S(1)}, u32[]{:S(2)}, u32[]{:S(2)}) %collective-permute-start.4) | collective-permute-done | bytes 57376 | tf_op jit(solution)/shard_map/ppermute | solution.py:191
  73.9 8.1 %collective-permute-done.5 = bf16[32,896]{1,0:T(8,128)(2,1)S(1)} collective-permute-done((bf16[32,896]{1,0:T(8,128)(2,1)S(1)}, bf16[32,896]{1,0:T(8,128)(2,1)S(1)}, u32[]{:S(2)}, u32[]{:S(2)}) %collective-permute-start.5) | collective-permute-done | bytes 57376 | tf_op jit(solution)/shard_map/ppermute | solution.py:191
  82.0 6.6 %collective-permute-done.6 = bf16[32,896]{1,0:T(8,128)(2,1)S(1)} collective-permute-done((bf16[32,896]{1,0:T(8,128)(2,1)S(1)}, bf16[32,896]{1,0:T(8,128)(2,1)S(1)}, u32[]{:S(2)}, u32[]{:S(2)}) %collective-permute-start.6) | collective-permute-done | bytes 57376 | tf_op jit(solution)/shard_map/ppermute | solution.py:191
  88.5 5.7 %collective-permute-done.7 = bf16[32,896]{1,0:T(8,128)(2,1)S(1)} collective-permute-done((bf16[32,896]{1,0:T(8,128)(2,1)S(1)}, bf16[32,896]{1,0:T(8,128)(2,1)S(1)}, u32[]{:S(2)}, u32[]{:S(2)}) %collective-permute-start.7) | collective-permute-done | bytes 57376 | tf_op jit(solution)/shard_map/ppermute | solution.py:191
  94.2 6.3 %collective-permute-done.8 = bf16[32,896]{1,0:T(8,128)(2,1)S(1)} collective-permute-done((bf16[32,896]{1,0:T(8,128)(2,1)S(1)}, bf16[32,896]{1,0:T(8,128)(2,1)S(1)}, u32[]{:S(2)}, u32[]{:S(2)}) %collective-permute-start.8) | collective-permute-done | bytes 57376 | tf_op jit(solution)/shard_map/ppermute | solution.py:191
  100.5 6.6 %collective-permute-done.9 = bf16[32,896]{1,0:T(8,128)(2,1)S(1)} collective-permute-done((bf16[32,896]{1,0:T(8,128)(2,1)S(1)}, bf16[32,896]{1,0:T(8,128)(2,1)S(1)}, u32[]{:S(2)}, u32[]{:S(2)}) %collective-permute-start.9) | collective-permute-done | bytes 57376 | tf_op jit(solution)/shard_map/ppermute | solution.py:191
  108.4 3.7 %collective-permute-done.10 = bf16[32,896]{1,0:T(8,128)(2,1)S(1)} collective-permute-done((bf16[32,896]{1,0:T(8,128)(2,1)S(1)}, bf16[32,896]{1,0:T(8,128)(2,1)S(1)}, u32[]{:S(2)}, u32[]{:S(2)}) %collective-permute-start.10) | collective-permute-done | bytes 57376 | tf_op jit(solution)/shard_map/ppermute | solution.py:191
  114.0 1.7 dynamic_update_slice.3
  116.3 1.9 collective-permute-done.15
  118.2 22.3 %all-reduce.1 = bf16[4,64,448]{2,1,0:T(8,128)(2,1)S(1)} all-reduce(f32[4,64,448]{2,1,0:T(8,128)S(1)} %bitcast_add_fusion), channel_id=1, replica_groups=mesh['req'=16,'y'=4,'core'=2] {'y'}, use_global_device_ids=true, to_apply=%region_3.4 | all-reduce | flops 114688 | bytes 688128 | tf_op jit(solution)/shard_map/psum | solution.py:212
  142.1 4.5 %reshape.119 = bf16[160,16,448]{2,1,0:T(8,128)(2,1)S(1)} reshape(bf16[160,7168]{1,0:T(8,128)(2,1)} %param.25) | data formatting | bytes 4587520 | tf_op jit(solution)/shard_map/reshape | solution.py:237
  146.6 5.6 %reshape.121 = bf16[160,16,448]{2,1,0:T(8,128)(2,1)} reshape(bf16[160,7168]{1,0:T(8,128)(2,1)} %collective-permute-done.18) | data formatting | bytes 4587520 | tf_op jit(solution)/shard_map/reshape | solution.py:237
  152.1 37.8 %all-gather.2.cloned.1.call-done = bf16[256,7168]{0,1:T(8,128)(2,1)} async-done(((bf16[256,448]{0,1:T(8,128)(2,1)}), bf16[256,7168]{0,1:T(8,128)(2,1)}) %all-gather.2.cloned.1.call-update) | async-done | bytes 3670032 | tf_op jit(solution)/shard_map/all_gather | solution.py:215
  190.0 3.2 %fusion = f32[256]{0:T(256)S(1)} fusion(bf16[256,7168]{0,1:T(8,128)(2,1)} %all-gather.2.cloned.1.call-done), kind=kLoop, calls=%fused_computation.5 | loop fusion | flops 5504768 | bytes 3671040 | tf_op jit(solution)/shard_map/reduce_sum | solution.py:217
  193.2 3.2 %fusion.2 = bf16[256,7168]{0,1:T(8,128)(2,1)S(1)} fusion(bf16[256,7168]{0,1:T(8,128)(2,1)S(1)} %copy-done.4, f32[7168]{0:T(1024)S(1)} %copy-done.10, f32[256]{0:T(256)S(1)} %add_rsqrt_fusion), kind=kLoop, calls=%fused_computation.7 | loop fusion | flops 7340032 | bytes 7369728 | tf_op jit(solution)/shard_map/convert_element_type | solution.py:218
  200.3 3.6 %fusion.22 = f32[256,160]{0,1:T(8,128)S(1)} fusion(bf16[7168,160]{0,1:T(8,128)(2,1)} %collective-permute-done.16, bf16[256,7168]{0,1:T(8,128)(2,1)} %copy-done.2), kind=kOutput, calls=%fused_computation.70 | convolution fusion | flops 587202560 | bytes 6127616 | tf_op jit(solution)/shard_map/dot_general | solution.py:223
  204.1 2.4 multiply_convert_fusion
  206.6 3.6 %fusion.5 = f32[4,64,16,448]{3,1,2,0:T(8,128)S(1)} fusion(bf16[4,64,160,1]{2,1,3,0:T(8,128)(2,1)S(1)} %bitcast.85, bf16[160,16,448]{2,1,0:T(8,128)(2,1)S(1)} %reshape.119), kind=kOutput, calls=%fused_computation.10 | convolution fusion | flops 587202560 | bytes 9715712 | tf_op jit(solution)/shard_map/ysh,hrf->rysf/dot_general | solution.py:229
  210.3 3.7 %fusion.3 = bf16[16,4,64,448]{3,2,0,1:T(8,128)(2,1)S(1)} fusion(f32[4,64,16,448]{3,1,2,0:T(8,128)S(1)} %fusion.5, bf16[4,64,160,1]{2,1,3,0:T(8,128)(2,1)S(1)} %bitcast.86, bf16[160,16,448]{2,1,0:T(8,128)(2,1)S(1)} %copy-done.5), kind=kOutput, calls=%fused_computation.8 | convolution fusion | flops 590872576 | bytes 13385728 | tf_op jit(solution)/shard_map/ysh,hrf->rysf/dot_general | solution.py:229
  214.0 2.2 copy.51
  216.2 8.3 %all-to-all-start = ((bf16[64,64,448]{2,1,0:T(8,128)(2,1)}), bf16[64,64,448]{2,1,0:T(8,128)(2,1)}, u32[]{:S(2)}, u32[]{:S(2)}) async-start(bf16[64,64,448]{2,1,0:T(8,128)(2,1)} %bitcast.81), calls=%async_computation | async-start | bytes 8388608 | tf_op jit(solution)/shard_map/all_to_all | solution.py:243
  224.6 54.2 %all-to-all-done = bf16[64,64,448]{2,1,0:T(8,128)(2,1)} async-done(((bf16[64,64,448]{2,1,0:T(8,128)(2,1)}), bf16[64,64,448]{2,1,0:T(8,128)(2,1)}, u32[]{:S(2)}, u32[]{:S(2)}) %all-to-all-start) | async-done | bytes 3670048 | tf_op jit(solution)/shard_map/all_to_all | solution.py:243
  278.8 2.9 convert_reduce_fusion
  (105 shorter events, 20.0 us)
Async XLA Ops:
  6.5 106.7 %copy-start = (bf16[896,448]{0,1:T(8,128)(2,1)S(1)}, bf16[896,448]{0,1:T(8,128)(2,1)}, u32[]{:S(2)}) copy-start(bf16[896,448]{0,1:T(8,128)(2,1)} %param.20) | copy-start | bytes 2408452
  6.5 183.4 %all-gather.2.cloned.1.call-start = ((), (), s32[]{:S(2)}) async-start(), calls=%async_computation.1 | async-start | bytes 3899392 | tf_op jit(solution)/shard_map/all_gather | solution.py:215
  14.1 11.7 %copy-start.11 = (s32[32]{0:T(128)S(1)}, s32[32]{0:T(128)}, u32[]{:S(2)}) copy-start(s32[32]{0:T(128)} %param.18) | copy-start | bytes 388
  14.1 13.0 %copy-start.13 = (bf16[32,128]{1,0:T(8,128)(2,1)S(1)}, bf16[32,128]{1,0:T(8,128)(2,1)}, u32[]{:S(2)}) copy-start(bf16[32,128]{1,0:T(8,128)(2,1)} %param.15) | copy-start | bytes 24580
  14.1 25.2 %copy-start.9 = (bf16[64,448]{1,0:T(8,128)(2,1)S(1)}, bf16[64,448]{1,0:T(8,128)(2,1)}, u32[]{:S(2)}) copy-start(bf16[64,448]{1,0:T(8,128)(2,1)} %param.21) | copy-start | bytes 172036
  28.3 83.9 %collective-permute-start.14 = (bf16[32,896]{1,0:T(8,128)(2,1)S(1)}, bf16[32,896]{1,0:T(8,128)(2,1)S(1)}, u32[]{:S(2)}, u32[]{:S(2)}) collective-permute-start(bf16[32,896]{1,0:T(8,128)(2,1)S(1)} %convert_element_type.66), channel_id=1, source_target_pairs={{0,120},{8,0},{16,8},{24,16},{32,24},{40,32},{48,40},{56,48},{64,5... | collective-permute-start | bytes 172040 | tf_op jit(solution)/shard_map/ppermute | solution.py:191
  32.1 80.1 %collective-permute-start.13 = (bf16[32,896]{1,0:T(8,128)(2,1)S(1)}, bf16[32,896]{1,0:T(8,128)(2,1)S(1)}, u32[]{:S(2)}, u32[]{:S(2)}) collective-permute-start(bf16[32,896]{1,0:T(8,128)(2,1)S(1)} %convert_element_type.66), channel_id=1, source_target_pairs={{0,112},{8,120},{16,0},{24,8},{32,16},{40,24},{48,32},{56,40},{64,... | collective-permute-start | bytes 172040 | tf_op jit(solution)/shard_map/ppermute | solution.py:191
  36.8 75.4 %collective-permute-start.12 = (bf16[32,896]{1,0:T(8,128)(2,1)S(1)}, bf16[32,896]{1,0:T(8,128)(2,1)S(1)}, u32[]{:S(2)}, u32[]{:S(2)}) collective-permute-start(bf16[32,896]{1,0:T(8,128)(2,1)S(1)} %convert_element_type.66), channel_id=1, source_target_pairs={{0,104},{8,112},{16,120},{24,0},{32,8},{40,16},{48,24},{56,32},{64... | collective-permute-start | bytes 172040 | tf_op jit(solution)/shard_map/ppermute | solution.py:191
  36.8 75.3 %collective-permute-start.11 = (bf16[32,896]{1,0:T(8,128)(2,1)S(1)}, bf16[32,896]{1,0:T(8,128)(2,1)S(1)}, u32[]{:S(2)}, u32[]{:S(2)}) collective-permute-start(bf16[32,896]{1,0:T(8,128)(2,1)S(1)} %convert_element_type.66), channel_id=1, source_target_pairs={{0,96},{8,104},{16,112},{24,120},{32,0},{40,8},{48,16},{56,24},{64... | collective-permute-start | bytes 172040 | tf_op jit(solution)/shard_map/ppermute | solution.py:191
  39.0 7.5 %collective-permute-start = (bf16[32,896]{1,0:T(8,128)(2,1)S(1)}, bf16[32,896]{1,0:T(8,128)(2,1)S(1)}, u32[]{:S(2)}, u32[]{:S(2)}) collective-permute-start(bf16[32,896]{1,0:T(8,128)(2,1)S(1)} %convert_element_type.66), channel_id=1, source_target_pairs={{0,8},{8,16},{16,24},{24,32},{32,40},{40,48},{48,56},{56,64},{64,7... | collective-permute-start | bytes 172040 | tf_op jit(solution)/shard_map/ppermute | solution.py:191
  46.5 7.8 %collective-permute-start.1 = (bf16[32,896]{1,0:T(8,128)(2,1)S(1)}, bf16[32,896]{1,0:T(8,128)(2,1)S(1)}, u32[]{:S(2)}, u32[]{:S(2)}) collective-permute-start(bf16[32,896]{1,0:T(8,128)(2,1)S(1)} %convert_element_type.66), channel_id=1, source_target_pairs={{0,16},{8,24},{16,32},{24,40},{32,48},{40,56},{48,64},{56,72},{64,... | collective-permute-start | bytes 172040 | tf_op jit(solution)/shard_map/ppermute | solution.py:191
  54.3 6.4 %collective-permute-start.2 = (bf16[32,896]{1,0:T(8,128)(2,1)S(1)}, bf16[32,896]{1,0:T(8,128)(2,1)S(1)}, u32[]{:S(2)}, u32[]{:S(2)}) collective-permute-start(bf16[32,896]{1,0:T(8,128)(2,1)S(1)} %convert_element_type.66), channel_id=1, source_target_pairs={{0,24},{8,32},{16,40},{24,48},{32,56},{40,64},{48,72},{56,80},{64,... | collective-permute-start | bytes 172040 | tf_op jit(solution)/shard_map/ppermute | solution.py:191
  60.7 5.4 %collective-permute-start.3 = (bf16[32,896]{1,0:T(8,128)(2,1)S(1)}, bf16[32,896]{1,0:T(8,128)(2,1)S(1)}, u32[]{:S(2)}, u32[]{:S(2)}) collective-permute-start(bf16[32,896]{1,0:T(8,128)(2,1)S(1)} %convert_element_type.66), channel_id=1, source_target_pairs={{0,32},{8,40},{16,48},{24,56},{32,64},{40,72},{48,80},{56,88},{64,... | collective-permute-start | bytes 172040 | tf_op jit(solution)/shard_map/ppermute | solution.py:191
  66.0 7.8 %collective-permute-start.4 = (bf16[32,896]{1,0:T(8,128)(2,1)S(1)}, bf16[32,896]{1,0:T(8,128)(2,1)S(1)}, u32[]{:S(2)}, u32[]{:S(2)}) collective-permute-start(bf16[32,896]{1,0:T(8,128)(2,1)S(1)} %convert_element_type.66), channel_id=1, source_target_pairs={{0,40},{8,48},{16,56},{24,64},{32,72},{40,80},{48,88},{56,96},{64,... | collective-permute-start | bytes 172040 | tf_op jit(solution)/shard_map/ppermute | solution.py:191
  73.8 8.1 %collective-permute-start.5 = (bf16[32,896]{1,0:T(8,128)(2,1)S(1)}, bf16[32,896]{1,0:T(8,128)(2,1)S(1)}, u32[]{:S(2)}, u32[]{:S(2)}) collective-permute-start(bf16[32,896]{1,0:T(8,128)(2,1)S(1)} %convert_element_type.66), channel_id=1, source_target_pairs={{0,48},{8,56},{16,64},{24,72},{32,80},{40,88},{48,96},{56,104},{64... | collective-permute-start | bytes 172040 | tf_op jit(solution)/shard_map/ppermute | solution.py:191
  81.9 6.6 %collective-permute-start.6 = (bf16[32,896]{1,0:T(8,128)(2,1)S(1)}, bf16[32,896]{1,0:T(8,128)(2,1)S(1)}, u32[]{:S(2)}, u32[]{:S(2)}) collective-permute-start(bf16[32,896]{1,0:T(8,128)(2,1)S(1)} %convert_element_type.66), channel_id=1, source_target_pairs={{0,56},{8,64},{16,72},{24,80},{32,88},{40,96},{48,104},{56,112},{6... | collective-permute-start | bytes 172040 | tf_op jit(solution)/shard_map/ppermute | solution.py:191
  88.5 5.7 %collective-permute-start.7 = (bf16[32,896]{1,0:T(8,128)(2,1)S(1)}, bf16[32,896]{1,0:T(8,128)(2,1)S(1)}, u32[]{:S(2)}, u32[]{:S(2)}) collective-permute-start(bf16[32,896]{1,0:T(8,128)(2,1)S(1)} %convert_element_type.66), channel_id=1, source_target_pairs={{0,64},{8,72},{16,80},{24,88},{32,96},{40,104},{48,112},{56,120},{... | collective-permute-start | bytes 172040 | tf_op jit(solution)/shard_map/ppermute | solution.py:191
  94.2 6.3 %collective-permute-start.8 = (bf16[32,896]{1,0:T(8,128)(2,1)S(1)}, bf16[32,896]{1,0:T(8,128)(2,1)S(1)}, u32[]{:S(2)}, u32[]{:S(2)}) collective-permute-start(bf16[32,896]{1,0:T(8,128)(2,1)S(1)} %convert_element_type.66), channel_id=1, source_target_pairs={{0,72},{8,80},{16,88},{24,96},{32,104},{40,112},{48,120},{56,0},{6... | collective-permute-start | bytes 172040 | tf_op jit(solution)/shard_map/ppermute | solution.py:191
  100.5 6.6 %collective-permute-start.9 = (bf16[32,896]{1,0:T(8,128)(2,1)S(1)}, bf16[32,896]{1,0:T(8,128)(2,1)S(1)}, u32[]{:S(2)}, u32[]{:S(2)}) collective-permute-start(bf16[32,896]{1,0:T(8,128)(2,1)S(1)} %convert_element_type.66), channel_id=1, source_target_pairs={{0,80},{8,88},{16,96},{24,104},{32,112},{40,120},{48,0},{56,8},{64... | collective-permute-start | bytes 172040 | tf_op jit(solution)/shard_map/ppermute | solution.py:191
  107.1 5.1 %collective-permute-start.10 = (bf16[32,896]{1,0:T(8,128)(2,1)S(1)}, bf16[32,896]{1,0:T(8,128)(2,1)S(1)}, u32[]{:S(2)}, u32[]{:S(2)}) collective-permute-start(bf16[32,896]{1,0:T(8,128)(2,1)S(1)} %convert_element_type.66), channel_id=1, source_target_pairs={{0,88},{8,96},{16,104},{24,112},{32,120},{40,0},{48,8},{56,16},{64... | collective-permute-start | bytes 172040 | tf_op jit(solution)/shard_map/ppermute | solution.py:191
  116.2 2.0 collective-permute-start.15
  140.5 11.6 %copy-start.7 = (bf16[4,64,448]{2,1,0:T(8,128)(2,1)}, bf16[4,64,448]{2,1,0:T(8,128)(2,1)S(1)}, u32[]{:S(2)}) copy-start(bf16[4,64,448]{2,1,0:T(8,128)(2,1)S(1)} %all-reduce.1) | copy-start | bytes 688132
  141.4 5.2 %collective-permute-start.18 = (bf16[160,7168]{1,0:T(8,128)(2,1)}, bf16[160,7168]{1,0:T(8,128)(2,1)}, u32[]{:S(2)}, u32[]{:S(2)}) collective-permute-start(bf16[160,7168]{1,0:T(8,128)(2,1)} %param.25), channel_id=1, source_target_pairs={{0,1},{1,0},{2,3},{3,2},{4,5},{5,4},{6,7},{7,6},{8,9},{9,8},{10,11... | collective-permute-start | bytes 6881288 | tf_op jit(solution)/shard_map/ppermute | solution.py:188
  141.5 58.8 %collective-permute-start.16 = (bf16[7168,160]{0,1:T(8,128)(2,1)}, bf16[7168,160]{0,1:T(8,128)(2,1)}, u32[]{:S(2)}, u32[]{:S(2)}) collective-permute-start(bf16[7168,160]{0,1:T(8,128)(2,1)} %param.23), channel_id=1, source_target_pairs={{0,1},{1,0},{2,3},{3,2},{4,5},{5,4},{6,7},{7,6},{8,9},{9,8},{10,11... | collective-permute-start | bytes 6881288 | tf_op jit(solution)/shard_map/ppermute | solution.py:186
  142.0 62.0 %collective-permute-start.17 = (bf16[7168,160]{0,1:T(8,128)(2,1)}, bf16[7168,160]{0,1:T(8,128)(2,1)}, u32[]{:S(2)}, u32[]{:S(2)}) collective-permute-start(bf16[7168,160]{0,1:T(8,128)(2,1)} %param.24), channel_id=1, source_target_pairs={{0,1},{1,0},{2,3},{3,2},{4,5},{5,4},{6,7},{7,6},{8,9},{9,8},{10,11... | collective-permute-start | bytes 6881288 | tf_op jit(solution)/shard_map/ppermute | solution.py:187
  146.5 46.6 %copy-start.10 = (f32[7168]{0:T(1024)S(1)}, f32[7168]{0:T(1024)}, u32[]{:S(2)}) copy-start(f32[7168]{0:T(1024)} %param.22) | copy-start | bytes 86020
  190.0 3.2 %copy-start.4 = (bf16[256,7168]{0,1:T(8,128)(2,1)S(1)}, bf16[256,7168]{0,1:T(8,128)(2,1)}, u32[]{:S(2)}) copy-start(bf16[256,7168]{0,1:T(8,128)(2,1)} %all-gather.2.cloned.1.call-done) | copy-start | bytes 11010052
  193.2 3.2 %copy-start.6 = (bf16[7168,160]{0,1:T(8,128)(2,1)S(1)}, bf16[7168,160]{0,1:T(8,128)(2,1)}, u32[]{:S(2)}) copy-start(bf16[7168,160]{0,1:T(8,128)(2,1)} %param.23) | copy-start | bytes 6881284
  200.3 3.8 %copy-start.3 = (bf16[256,7168]{0,1:T(8,128)(2,1)S(1)}, bf16[256,7168]{0,1:T(8,128)(2,1)}, u32[]{:S(2)}) copy-start(bf16[256,7168]{0,1:T(8,128)(2,1)} %copy-done.2) | copy-start | bytes 11010052
  206.6 3.6 %copy-start.5 = (bf16[160,16,448]{2,1,0:T(8,128)(2,1)S(1)}, bf16[160,16,448]{2,1,0:T(8,128)(2,1)}, u32[]{:S(2)}) copy-start(bf16[160,16,448]{2,1,0:T(8,128)(2,1)} %reshape.121) | copy-start | bytes 6881284
  216.2 62.5 %all-to-all-start = ((bf16[64,64,448]{2,1,0:T(8,128)(2,1)}), bf16[64,64,448]{2,1,0:T(8,128)(2,1)}, u32[]{:S(2)}, u32[]{:S(2)}) async-start(bf16[64,64,448]{2,1,0:T(8,128)(2,1)} %bitcast.81), calls=%async_computation | async-start | bytes 8388608 | tf_op jit(solution)/shard_map/all_to_all | solution.py:243
  224.6 58.6 %copy-start.1 = (bf16[896,448]{0,1:T(8,128)(2,1)S(1)}, bf16[896,448]{0,1:T(8,128)(2,1)}, u32[]{:S(2)}) copy-start(bf16[896,448]{0,1:T(8,128)(2,1)} %param.20) | copy-start | bytes 2408452
  (3 other events, 5.9 us)
Sparse Core Ops, SparseCore 0:
  141.5 48.4 all-gather.1

commit v10 on v7

--- a/solution.py
+++ b/solution.py
@@ -14,7 +14,7 @@
 
 epsilon = 1e-05
 masked_value = -1e30
-key_block = 1792
+key_block = 3584
 
 
 def _cache_kernel(live_ref, q_ref, k_ref, v_ref, owner_ref, rowreq_ref, m_out, l_out, acc_out, m_s, l_s, acc_s, *, scale):
@@ -202,7 +202,7 @@
     mine = lax.dynamic_index_in_dim(parts, core, 1, keepdims=False)
     theirs = lax.dynamic_index_in_dim(parts, 1 - core, 1, keepdims=False)
     side_partial = mine + lax.ppermute(theirs, "core", swap)
-    side_rows = lax.psum(side_partial, "y").astype(jnp.bfloat16)
+    side_rows = lax.psum(side_partial.astype(jnp.bfloat16), "y")
     stream = lax.dynamic_index_in_dim(side_rows, lax.axis_index("y"), 0, keepdims=False)
     side_rows = side_rows.reshape(y_count * tokens_out, columns)
     side_stream = lax.all_gather(side_rows, "req", axis=1, tiled=True)
@@ -212,25 +212,17 @@
         jnp.bfloat16
     )
 
-    def hidden_of(gate_w, up_w):
-        gate = jnp.dot(normed, gate_w, preferred_element_type=jnp.float32)
-        up = jnp.dot(normed, up_w, preferred_element_type=jnp.float32)
-        hidden = (jax.nn.silu(gate) * up).astype(jnp.bfloat16)
-        return hidden.reshape(y_count, tokens_out, hidden.shape[1])
-
-    def down_of(hidden, down_w):
-        return jnp.einsum(
-            "ysh,hrf->rysf",
-            hidden,
-            down_w,
-            preferred_element_type=jnp.float32,
-        )
-
-    def blocks_of(down_w):
-        return down_w.reshape(down_w.shape[0], req_count, columns)
-
-    product = down_of(hidden_of(gate_weight, up_weight), blocks_of(down_weight)) + down_of(
-        hidden_of(gate_partner, up_partner), blocks_of(down_partner)
+    gate_pair = jnp.concatenate([gate_weight, gate_partner], axis=1)
+    up_pair = jnp.concatenate([up_weight, up_partner], axis=1)
+    down_pair = jnp.concatenate([down_weight, down_partner], axis=0)
+    gate = jnp.dot(normed, gate_pair, preferred_element_type=jnp.float32)
+    up = jnp.dot(normed, up_pair, preferred_element_type=jnp.float32)
+    hidden = (jax.nn.silu(gate) * up).astype(jnp.bfloat16)
+    product = jnp.einsum(
+        "ysh,hrf->rysf",
+        hidden.reshape(y_count, tokens_out, hidden.shape[1]),
+        down_pair.reshape(down_pair.shape[0], req_count, columns),
+        preferred_element_type=jnp.float32,
     )
     pieces = product.astype(jnp.bfloat16).reshape(req_count * y_count, tokens_out, columns)
     received = lax.all_to_all(pieces, ("req", "y"), 0, 0, tiled=True)

time: 235 us -> 249 us (1.060)
  waiting for transfers between devices: 93 us -> 134 us
  blocking collectives: 48.8 us -> 26.8 us
  local copies, waits for them, and re-layouts: 24.8 us -> 18.7 us
    psum x0 -> x1, waiting for transfers between devices: none -> 41.7 us  [per_device(): side_rows = lax.psum(side_partial.astype(jnp.bfloat16), 'y')]
    psum x1 -> x0, blocking collectives: 22.3 us -> none  [per_device(): side_rows = lax.psum(side_partial, 'y').astype(jnp.bfloat16)]
    all_gather x1, waiting for transfers between devices: 36.8 us -> 31.7 us  [per_device(): side_stream = lax.all_gather(side_rows, 'req', axis=1, tiled=True)]
    convert_element_type x3 -> x1, local copies, waits for them, and re-layouts: 4.86 us -> 0.16 us  [per_device(): hidden = (jax.nn.silu(gate) * up).astype(jnp.bfloat16)]
    concatenate x0 -> x1, other arithmetic: none -> 4.08 us  [per_device(): down_pair = jnp.concatenate([down_weight, down_partner], axis=0)]
    ppermute x1, waiting for transfers between devices: 0.01 us -> 4.05 us  [per_device(): down_partner = lax.ppermute(down_weight, 'core', swap)]
    dot_general x6 -> x3, matrix products: 16.2 us -> 17.9 us  [the longest x1 8.48 us: per_device(): jnp.einsum('ysh,hrf->rysf', hidden.reshape(y_count, tokens_out, hidden.sh...]
    reshape x2 -> x1, local copies, waits for them, and re-layouts: 10 us -> 9.94 us  [per_device(): down_pair.reshape(down_pair.shape[0], req_count, columns)]
  transfers between devices with their start and end apart: 6 -> 7, of which waited for: 3 -> 5; matrix products, arithmetic and copies ran while one was open for 10% -> 9% of each run, Pallas kernels for 0% -> 0%
where the time goes in v10:
time: 249 us; the launch traced here: 248 us
  waiting for transfers between devices  134 us (54%)
  blocking collectives  26.8 us (11%)
  matrix products  20.5 us (8%)
  local copies, waits for them, and re-layouts  18.7 us (8%)
  other arithmetic  16.2 us (7%)
  between operations  14.3 us (6%)
  starting transfers between devices  9.11 us (4%)
  Pallas kernels  9.11 us (4%)
    all_to_all x1, waiting for transfers between devices, per_device(): received = lax.all_to_all(pieces, ('req', 'y'), 0, 0, tiled=True)  54.3 us
    psum x1, waiting for transfers between devices, per_device(): side_rows = lax.psum(side_partial.astype(jnp.bfloat16), 'y')  41.7 us
    all_gather x1, waiting for transfers between devices, per_device(): side_stream = lax.all_gather(side_rows, 'req', axis=1, tiled=True)  31.7 us
    all_gather x1, blocking collectives, per_device(): lax.all_gather(attended, 'req', axis=0, tiled=True)  26.8 us
    reshape x1, local copies, waits for them, and re-layouts, per_device(): down_pair.reshape(down_pair.shape[0], req_count, columns)  9.94 us
    pallas_call x1, Pallas kernels, cache_attention(): pl.pallas_call(functools.partial(_cache_kernel, scale=scale), grid_spec=g...  9.11 us
    dot_general x1, matrix products, per_device(): jnp.einsum('ysh,hrf->rysf', hidden.reshape(y_count, tokens_out, hidden.sh...  8.48 us
    all_to_all x1, starting transfers between devices, per_device(): received = lax.all_to_all(pieces, ('req', 'y'), 0, 0, tiled=True)  8.31 us
  transfers between devices with their start and end apart: 7, of which 5 were waited for; matrix products, arithmetic and copies ran while one was open for 9% of the time, Pallas kernels for 0%

profile of v10, /device:TPU:0, one launch (start us, length us, event | category | flops | bytes accessed | tf_op | source)
XLA Modules:
  0.0 248.4 jit_solution(5852073589613080004)
XLA Ops:
  6.5 1.6 convert_reduce_fusion.1
  8.8 1.6 reshape.41.owner_ref
  10.4 0.7 broadcast_in_dim.20
  11.2 0.7 reshape_reshape.4.rowreq_ref
  12.1 0.9 reshape_squeeze_reshape.4.q_ref
  13.0 0.9 fusion.31
  14.1 9.1 %shard_map.127 = (f32[224,1]{1,0:T(8,128)}, f32[224,1]{1,0:T(8,128)}, f32[224,128]{1,0:T(8,128)}) custom-call(s32[1]{0:T(128)} %bitcast.live_ref, bf16[224,128]{1,0:T(8,128)(2,1)} %copy-done.2, bf16[17920,128]{1,0:T(8,128)(2,1)} %k_ref.1, bf16[17920,128]{1,0:T(8,128)(2,1)} %v_ref.1, s32[1,17920]{1,0:T(1,128)} %reshape.41.owner_ref, ...), custom_call_target="tpu_custom_call" | custom-call | flops 2055208960 | bytes 9418752 | tf_op jit(solution)/shard_map/pallas_call | solution.py:86
  23.2 1.0 maximum_reduce_fusion
  24.4 1.1 fusion.23
  25.6 1.1 fusion.17
  26.9 26.8 %all_gather.6 = bf16[512,896]{1,0:T(8,128)(2,1)S(1)} all-gather(bf16[32,896]{1,0:T(8,128)(2,1)S(1)} %convert_element_type.52), channel_id=1, replica_groups=mesh['req'=16,'y'=4,'core'=2] {'req'}, dimensions={0}, use_global_device_ids=true | all-gather | bytes 974848 | tf_op jit(solution)/shard_map/all_gather | solution.py:191
  53.7 0.7 fusion.32
  54.5 1.7 dynamic_update_slice.3
  56.3 0.3 copy.37
  56.8 1.9 collective-permute-done
  58.7 0.8 fusion.21
  59.5 41.7 %all-reduce.2.cloned.1.call-done = bf16[4,64,448]{2,1,0:T(8,128)(2,1)} async-done(((bf16[4,64,448]{2,1,0:T(8,128)(2,1)}), bf16[4,64,448]{2,1,0:T(8,128)(2,1)}) %all-reduce.2.cloned.1.call-update) | async-done | bytes 229392 | tf_op jit(solution)/shard_map/psum | solution.py:205
  101.2 1.8 copy.38
  103.1 0.5 collective-permute-start.2
  103.7 4.0 %collective-permute-done.1 = bf16[160,7168]{1,0:T(8,128)(2,1)S(1)} collective-permute-done((bf16[160,7168]{1,0:T(8,128)(2,1)}, bf16[160,7168]{1,0:T(8,128)(2,1)S(1)}, u32[]{:S(2)}, u32[]{:S(2)}) %collective-permute-start.1) | collective-permute-done | bytes 2293792 | tf_op jit(solution)/shard_map/ppermute | solution.py:188
  107.7 4.1 %pad_maximum_fusion = bf16[320,7168]{1,0:T(8,128)(2,1)} fusion(bf16[160,7168]{1,0:T(8,128)(2,1)S(1)} %collective-permute-done.1, bf16[160,7168]{1,0:T(8,128)(2,1)} %param.25), kind=kLoop, calls=%fused_computation.8 | loop fusion | flops 9175040 | bytes 9175040 | tf_op jit(solution)/shard_map/concatenate | solution.py:217
  111.8 9.9 %reshape.43 = bf16[320,16,448]{2,1,0:T(8,128)(2,1)} reshape(bf16[320,7168]{1,0:T(8,128)(2,1)} %pad_maximum_fusion) | data formatting | bytes 9175040 | tf_op jit(solution)/shard_map/reshape | solution.py:224
  121.7 31.7 %all-gather.2.cloned.1.call-done = bf16[256,7168]{0,1:T(8,128)(2,1)} async-done(((bf16[256,448]{0,1:T(8,128)(2,1)}), bf16[256,7168]{0,1:T(8,128)(2,1)}) %all-gather.2.cloned.1.call-update) | async-done | bytes 3670032 | tf_op jit(solution)/shard_map/all_gather | solution.py:208
  153.4 3.0 %fusion = f32[256]{0:T(256)S(1)} fusion(bf16[256,7168]{0,1:T(8,128)(2,1)} %all-gather.2.cloned.1.call-done), kind=kLoop, calls=%fused_computation.3 | loop fusion | flops 5504768 | bytes 3671040 | tf_op jit(solution)/shard_map/reduce_sum | solution.py:210
  156.5 6.0 %fusion.5 = f32[256,320]{0,1:T(8,128)S(1)} fusion(bf16[7168,160]{0,1:T(8,128)(2,1)} %collective-permute-done.2, bf16[7168,160]{0,1:T(8,128)(2,1)S(1)} %copy-done.5, bf16[256,7168]{0,1:T(8,128)(2,1)} %all-gather.2.cloned.1.call-done, f32[7168]{0:T(1024)S(1)} %copy-done.7, f32[256]{0:T(256)S(1)} %add_rsqrt_fusion), kind=kOutput, calls=%fused_computation.9 | convolution fusion | flops 1190920192 | bytes 8614912 | tf_op jit(solution)/shard_map/dot_general | solution.py:218
  162.5 3.4 %multiply_convert_fusion = bf16[256,320]{0,1:T(8,128)(2,1)S(1)} fusion(f32[256,320]{0,1:T(8,128)S(1)} %fusion.5, bf16[256,7168]{0,1:T(8,128)(2,1)S(1)} %copy-done.1, f32[7168]{0:T(1024)S(1)} %copy-done.7, f32[256]{0:T(256)S(1)} %add_rsqrt_fusion, bf16[7168,160]{0,1:T(8,128)(2,1)} %collective-permute-done.3, bf16[7168,160]{0,1:T(8,128)(2,1)S(1)} %copy-done.6), kind=kOutput, calls=%fused_computation.26 | convolution fusion | flops 1191411712 | bytes 8778752 | tf_op jit(solution)/shard_map/dot_general | solution.py:219
  165.9 0.2 copy.39
  166.1 8.5 %fusion.13 = bf16[16,448,4,64]{1,3,2,0:T(8,128)(2,1)} fusion(bf16[4,64,320,1]{2,1,0,3:T(8,128)(2,1)S(1)} %bitcast.33, bf16[320,16,448,1]{2,1,0,3:T(8,128)(2,1)} %bitcast.28), kind=kOutput, calls=%fused_computation.17 | convolution fusion | flops 1176240128 | bytes 8421376 | tf_op jit(solution)/shard_map/ysh,hrf->rysf/dot_general | solution.py:221
  174.6 8.3 %all-to-all-start = ((bf16[64,64,448]{2,1,0:T(8,128)(2,1)}), bf16[64,64,448]{2,1,0:T(8,128)(2,1)}, u32[]{:S(2)}, u32[]{:S(2)}) async-start(bf16[64,64,448]{2,1,0:T(8,128)(2,1)} %bitcast.29), calls=%async_computation | async-start | bytes 8388608 | tf_op jit(solution)/shard_map/all_to_all | solution.py:228
  182.9 54.3 %all-to-all-done = bf16[64,64,448]{2,1,0:T(8,128)(2,1)} async-done(((bf16[64,64,448]{2,1,0:T(8,128)(2,1)}), bf16[64,64,448]{2,1,0:T(8,128)(2,1)}, u32[]{:S(2)}, u32[]{:S(2)}) %all-to-all-start) | async-done | bytes 3670048 | tf_op jit(solution)/shard_map/all_to_all | solution.py:228
  237.2 2.9 %convert_reduce_fusion = f32[64,448]{1,0:T(8,128)S(1)} fusion(bf16[64,64,448]{2,1,0:T(8,128)(2,1)} %all-to-all-done), kind=kLoop, calls=%fused_computation.2 | loop fusion | flops 3641344 | bytes 3784704 | tf_op jit(solution)/shard_map/reduce_sum | solution.py:229
  240.0 1.5 fusion.22
  (38 shorter events, 1.4 us)
Async XLA Ops:
  6.5 47.2 %copy-start = (bf16[896,448]{0,1:T(8,128)(2,1)S(1)}, bf16[896,448]{0,1:T(8,128)(2,1)}, u32[]{:S(2)}) copy-start(bf16[896,448]{0,1:T(8,128)(2,1)} %param.20) | copy-start | bytes 2408452
  6.5 94.6 %all-reduce.2.cloned.1.call-start = ((), (), s32[]{:S(2)}) async-start(), calls=%async_computation.1 | async-start | bytes 524288 | tf_op jit(solution)/shard_map/psum | solution.py:205
  13.0 1.1 copy-start.2
  14.0 10.2 %copy-start.4 = (s32[32]{0:T(128)S(1)}, s32[32]{0:T(128)}, u32[]{:S(2)}) copy-start(s32[32]{0:T(128)} %param.18) | copy-start | bytes 388
  14.1 11.5 %copy-start.8 = (bf16[32,128]{1,0:T(8,128)(2,1)S(1)}, bf16[32,128]{1,0:T(8,128)(2,1)}, u32[]{:S(2)}) copy-start(bf16[32,128]{1,0:T(8,128)(2,1)} %param.15) | copy-start | bytes 24580
  14.1 12.7 %copy-start.3 = (bf16[64,448]{1,0:T(8,128)(2,1)S(1)}, bf16[64,448]{1,0:T(8,128)(2,1)}, u32[]{:S(2)}) copy-start(bf16[64,448]{1,0:T(8,128)(2,1)} %param.21) | copy-start | bytes 172036
  56.7 2.0 collective-permute-start
  59.4 94.0 %all-gather.2.cloned.1.call-start = ((), (), s32[]{:S(2)}) async-start(), calls=%async_computation.2 | async-start | bytes 3899392 | tf_op jit(solution)/shard_map/all_gather | solution.py:208
  103.0 4.7 %collective-permute-start.1 = (bf16[160,7168]{1,0:T(8,128)(2,1)}, bf16[160,7168]{1,0:T(8,128)(2,1)S(1)}, u32[]{:S(2)}, u32[]{:S(2)}) collective-permute-start(bf16[160,7168]{1,0:T(8,128)(2,1)} %param.25), channel_id=1, source_target_pairs={{0,1},{1,0},{2,3},{3,2},{4,5},{5,4},{6,7},{7,6},{8,9},{9,8},{10,11... | collective-permute-start | bytes 6881288 | tf_op jit(solution)/shard_map/ppermute | solution.py:188
  103.1 53.4 %collective-permute-start.2 = (bf16[7168,160]{0,1:T(8,128)(2,1)}, bf16[7168,160]{0,1:T(8,128)(2,1)}, u32[]{:S(2)}, u32[]{:S(2)}) collective-permute-start(bf16[7168,160]{0,1:T(8,128)(2,1)} %param.23), channel_id=1, source_target_pairs={{0,1},{1,0},{2,3},{3,2},{4,5},{5,4},{6,7},{7,6},{8,9},{9,8},{10,11... | collective-permute-start | bytes 6881288 | tf_op jit(solution)/shard_map/ppermute | solution.py:186
  103.6 58.9 %collective-permute-start.3 = (bf16[7168,160]{0,1:T(8,128)(2,1)}, bf16[7168,160]{0,1:T(8,128)(2,1)}, u32[]{:S(2)}, u32[]{:S(2)}) collective-permute-start(bf16[7168,160]{0,1:T(8,128)(2,1)} %param.24), channel_id=1, source_target_pairs={{0,1},{1,0},{2,3},{3,2},{4,5},{5,4},{6,7},{7,6},{8,9},{9,8},{10,11... | collective-permute-start | bytes 6881288 | tf_op jit(solution)/shard_map/ppermute | solution.py:187
  111.8 44.7 %copy-start.5 = (bf16[7168,160]{0,1:T(8,128)(2,1)S(1)}, bf16[7168,160]{0,1:T(8,128)(2,1)}, u32[]{:S(2)}) copy-start(bf16[7168,160]{0,1:T(8,128)(2,1)} %param.23) | copy-start | bytes 6881284
  111.8 44.7 %copy-start.7 = (f32[7168]{0:T(1024)S(1)}, f32[7168]{0:T(1024)}, u32[]{:S(2)}) copy-start(f32[7168]{0:T(1024)} %param.22) | copy-start | bytes 86020
  156.5 6.0 %copy-start.1 = (bf16[256,7168]{0,1:T(8,128)(2,1)S(1)}, bf16[256,7168]{0,1:T(8,128)(2,1)}, u32[]{:S(2)}) copy-start(bf16[256,7168]{0,1:T(8,128)(2,1)} %all-gather.2.cloned.1.call-done) | copy-start | bytes 11010052
  156.5 6.0 %copy-start.6 = (bf16[7168,160]{0,1:T(8,128)(2,1)S(1)}, bf16[7168,160]{0,1:T(8,128)(2,1)}, u32[]{:S(2)}) copy-start(bf16[7168,160]{0,1:T(8,128)(2,1)} %param.24) | copy-start | bytes 6881284
  174.6 62.6 %all-to-all-start = ((bf16[64,64,448]{2,1,0:T(8,128)(2,1)}), bf16[64,64,448]{2,1,0:T(8,128)(2,1)}, u32[]{:S(2)}, u32[]{:S(2)}) async-start(bf16[64,64,448]{2,1,0:T(8,128)(2,1)} %bitcast.29), calls=%async_computation | async-start | bytes 8388608 | tf_op jit(solution)/shard_map/all_to_all | solution.py:228
Sparse Core Ops, SparseCore 0:
  59.6 41.5 all-reduce.1
  103.3 50.1 all-gather.1

commit v11 on v10

--- a/solution.py
+++ b/solution.py
@@ -14,10 +14,10 @@
 
 epsilon = 1e-05
 masked_value = -1e30
-key_block = 3584
-
-
-def _cache_kernel(live_ref, q_ref, k_ref, v_ref, owner_ref, rowreq_ref, m_out, l_out, acc_out, m_s, l_s, acc_s, *, scale):
+key_block = 1792
+
+
+def _cache_kernel(live_ref, q_ref, k_ref, v_ref, owner_ref, rowreq_ref, nk_ref, nv_ref, tokreq_ref, out_ref, m_s, l_s, acc_s, *, scale, group):
     i = pl.program_id(0)
 
     @pl.when(i == 0)
@@ -42,12 +42,23 @@
 
     @pl.when(i == pl.num_programs(0) - 1)
     def _done():
-        m_out[...] = m_s[...]
-        l_out[...] = l_s[...]
-        acc_out[...] = acc_s[...]
-
-
-def cache_attention(query_rows, cache_keys, cache_values, cache_req, row_req, live_blocks, block, scale):
+        scores = lax.dot_general(q_ref[...], nk_ref[...], (((1,), (1,)), ((), ())),
+                                 preferred_element_type=jnp.float32) * scale
+        shape = scores.shape
+        row_tok = lax.broadcasted_iota(jnp.int32, shape, 0) // group
+        col_tok = lax.broadcasted_iota(jnp.int32, shape, 1)
+        visible = (tokreq_ref[...] == rowreq_ref[...]) & (col_tok <= row_tok)
+        masked = jnp.where(visible, scores, masked_value)
+        running = m_s[...]
+        new_max = jnp.maximum(running, jnp.max(masked, axis=1, keepdims=True))
+        weights = jnp.where(visible, jnp.exp(masked - new_max), 0.0).astype(jnp.bfloat16)
+        factor = jnp.exp(running - new_max)
+        denominator = l_s[...] * factor + jnp.sum(weights.astype(jnp.float32), axis=1, keepdims=True)
+        weighted = acc_s[...] * factor + jnp.dot(weights, nv_ref[...], preferred_element_type=jnp.float32)
+        out_ref[...] = (weighted / denominator).astype(out_ref.dtype)
+
+
+def cache_attention(query_rows, cache_keys, cache_values, cache_req, row_req, live_blocks, block, scale, new_keys, new_values, tok_req, group):
     rows, hd = query_rows.shape
     pool = cache_keys.shape[0]
     nb = pool // block
@@ -68,12 +79,11 @@
             pl.BlockSpec((block, hd), kv_map),
             pl.BlockSpec((1, block), own_map),
             pl.BlockSpec((rows, 1), full),
+            pl.BlockSpec(new_keys.shape, full),
+            pl.BlockSpec(new_values.shape, full),
+            pl.BlockSpec((1, tok_req.shape[0]), full),
         ],
-        out_specs=[
-            pl.BlockSpec((rows, 1), full),
-            pl.BlockSpec((rows, 1), full),
-            pl.BlockSpec((rows, hd), full),
-        ],
+        out_specs=pl.BlockSpec((rows, hd), full),
         scratch_shapes=[
             pltpu.VMEM((rows, 1), jnp.float32),
             pltpu.VMEM((rows, 1), jnp.float32),
@@ -83,19 +93,15 @@
     flops = 4 * rows * pool * hd
     cost = pl.CostEstimate(flops=flops, transcendentals=rows * pool,
                            bytes_accessed=2 * pool * hd * 2 + pool * 4 + rows * hd * 6)
-    m, l, acc = pl.pallas_call(
-        functools.partial(_cache_kernel, scale=scale),
+    return pl.pallas_call(
+        functools.partial(_cache_kernel, scale=scale, group=group),
         grid_spec=grid_spec,
-        out_shape=[
-            jax.ShapeDtypeStruct((rows, 1), jnp.float32),
-            jax.ShapeDtypeStruct((rows, 1), jnp.float32),
-            jax.ShapeDtypeStruct((rows, hd), jnp.float32),
-        ],
+        out_shape=jax.ShapeDtypeStruct((rows, hd), jnp.bfloat16),
         compiler_params=pltpu.CompilerParams(dimension_semantics=("arbitrary",)),
         cost_estimate=cost,
     )(live_blocks.reshape(1).astype(jnp.int32), query_rows, cache_keys, cache_values,
-      cache_req.reshape(1, pool), row_req.reshape(rows, 1))
-    return m[:, 0], l[:, 0], acc
+      cache_req.reshape(1, pool), row_req.reshape(rows, 1), new_keys, new_values,
+      tok_req.reshape(1, tok_req.shape[0]))
 
 
 def attend(queries, new_keys, new_values, cache_keys, cache_values, tok_req, cache_req):
@@ -113,24 +119,6 @@
     live_slots = jnp.sum((cache_req >= 0).astype(jnp.int32))
     live_blocks = (live_slots + block_width - 1) // block_width
 
-    def update(carried, block_keys, block_values, visible):
-        running_max, denominator, weighted = carried[0]
-        query_rows = grouped[:, 0].reshape(row_count, head_dim)
-        scores = (
-            jnp.einsum("qd,kd->qk", query_rows, block_keys, preferred_element_type=jnp.float32)
-            * score_scale
-        )
-        masked = jnp.where(visible, scores, masked_value)
-        new_max = jnp.maximum(running_max, jnp.max(masked, axis=1))
-        weights = jnp.where(visible, jnp.exp(masked - new_max[:, None]), 0.0).astype(jnp.bfloat16)
-        factor = jnp.exp(running_max - new_max)
-        denominator = denominator * factor + jnp.sum(weights.astype(jnp.float32), axis=1)
-        weighted = weighted * factor[:, None] + jnp.dot(
-            weights, block_values, preferred_element_type=jnp.float32
-        )
-        renewed = [(new_max, denominator, weighted)]
-        return tuple(renewed)
-
     initial = tuple(
         (
             (
@@ -142,25 +130,12 @@
         )
     )
 
-    carried = (
-        cache_attention(
-            grouped[:, 0].reshape(row_count, head_dim), cache_keys, cache_values,
-            cache_req, row_req, live_blocks, block_width, score_scale,
-        ),
-    )
-    causal = (tok_req[None, :] == row_req[:, None]) & (
-        jnp.arange(tokens_here, dtype=jnp.int32)[None, :] <= row_tok[:, None]
-    )
-    carried = update(carried, new_keys, new_values, causal)
-    per_head = [
-        (weighted / denominator[:, None]).reshape(tokens_here, group_size, head_dim)
-        for running_max, denominator, weighted in carried
-    ]
-    return (
-        jnp.stack(per_head, axis=1)
-        .reshape(tokens_here, kv_here * group_size * head_dim)
-        .astype(jnp.bfloat16)
-    )
+    result = cache_attention(
+        grouped[:, 0].reshape(row_count, head_dim), cache_keys, cache_values,
+        cache_req, row_req, live_blocks, block_width, score_scale,
+        new_keys, new_values, tok_req, group_size,
+    )
+    return result.reshape(tokens_here, kv_here * group_size * head_dim)
 
 
 def per_device(
@@ -186,7 +161,9 @@
     gate_partner = lax.ppermute(gate_weight, "core", swap)
     up_partner = lax.ppermute(up_weight, "core", swap)
     down_partner = lax.ppermute(down_weight, "core", swap)
-    attended = attend(queries, new_keys, new_values, cache_keys, cache_values, tok_req, cache_req)
+    attended = attend(
+        queries, new_keys, new_values, cache_keys, cache_values, tok_req, cache_req
+    )
     partial_out = jnp.dot(
         lax.all_gather(attended, "req", axis=0, tiled=True),
         out_weight,
@@ -202,7 +179,7 @@
     mine = lax.dynamic_index_in_dim(parts, core, 1, keepdims=False)
     theirs = lax.dynamic_index_in_dim(parts, 1 - core, 1, keepdims=False)
     side_partial = mine + lax.ppermute(theirs, "core", swap)
-    side_rows = lax.psum(side_partial.astype(jnp.bfloat16), "y")
+    side_rows = lax.psum(side_partial, "y").astype(jnp.bfloat16)
     stream = lax.dynamic_index_in_dim(side_rows, lax.axis_index("y"), 0, keepdims=False)
     side_rows = side_rows.reshape(y_count * tokens_out, columns)
     side_stream = lax.all_gather(side_rows, "req", axis=1, tiled=True)
@@ -252,6 +229,4 @@
         P(("req",) + tp, None),
     )
     out_specs = P(tp, "req")
-    return jax.shard_map(
-        per_device, mesh=split, in_specs=in_specs, out_specs=out_specs, check_vma=False
-    )
+    return jax.shard_map(per_device, mesh=split, in_specs=in_specs, out_specs=out_specs, check_vma=False)

time: 249 us -> 223 us (0.90)
  waiting for transfers between devices: 134 us -> 89 us
  blocking collectives: 26.8 us -> 48.8 us
  other arithmetic: 16.2 us -> 12.5 us
    psum x1 -> x0, waiting for transfers between devices: 41.7 us -> none  [per_device(): side_rows = lax.psum(side_partial.astype(jnp.bfloat16), 'y')]
    psum x0 -> x1, blocking collectives: none -> 22.3 us  [per_device(): side_rows = lax.psum(side_partial, 'y').astype(jnp.bfloat16)]
    all_gather x1, waiting for transfers between devices: 31.7 us -> 28.8 us  [per_device(): side_stream = lax.all_gather(side_rows, 'req', axis=1, tiled=True)]
  transfers between devices with their start and end apart: 7 -> 6, of which waited for: 5 -> 4; matrix products, arithmetic and copies ran while one was open for 9% -> 10% of each run, Pallas kernels for 0% -> 0%
where the time goes in v11:
time: 223 us; the launch traced here: 222 us
  waiting for transfers between devices  89 us (40%)
  blocking collectives  48.8 us (22%)
  local copies, waits for them, and re-layouts  18.7 us (8%)
  matrix products  18.6 us (8%)
  between operations  14.2 us (6%)
  other arithmetic  12.5 us (6%)
  Pallas kernels  11 us (5%)
  starting transfers between devices  9.08 us (4%)
    all_to_all x1, waiting for transfers between devices, per_device(): received = lax.all_to_all(pieces, ('req', 'y'), 0, 0, tiled=True)  54.3 us
    all_gather x1, waiting for transfers between devices, per_device(): side_stream = lax.all_gather(side_rows, 'req', axis=1, tiled=True)  28.8 us
    all_gather x1, blocking collectives, per_device(): lax.all_gather(attended, 'req', axis=0, tiled=True)  26.5 us
    psum x1, blocking collectives, per_device(): side_rows = lax.psum(side_partial, 'y').astype(jnp.bfloat16)  22.3 us
    pallas_call x1, Pallas kernels, cache_attention(): pl.pallas_call(functools.partial(_cache_kernel, scale=scale, group=group)...  11 us
    reshape x1, local copies, waits for them, and re-layouts, per_device(): down_pair.reshape(down_pair.shape[0], req_count, columns)  9.92 us
    dot_general x1, matrix products, per_device(): jnp.einsum('ysh,hrf->rysf', hidden.reshape(y_count, tokens_out, hidden.sh...  8.48 us
    all_to_all x1, starting transfers between devices, per_device(): received = lax.all_to_all(pieces, ('req', 'y'), 0, 0, tiled=True)  8.32 us
  transfers between devices with their start and end apart: 6, of which 4 were waited for; matrix products, arithmetic and copies ran while one was open for 10% of the time, Pallas kernels for 0%

profile of v11, /device:TPU:0, one launch (start us, length us, event | category | flops | bytes accessed | tf_op | source)
XLA Modules:
  0.0 221.9 jit_solution(6426449595482933353)
XLA Ops:
  6.5 1.6 convert_reduce_fusion.1
  8.8 1.6 reshape.39.owner_ref
  10.4 1.5 reshape_squeeze_reshape.3.q_ref
  11.9 0.7 broadcast_in_dim.2
  12.6 0.7 reshape_reshape.4.rowreq_ref
  13.4 11.0 %shard_map.127 = bf16[224,128]{1,0:T(8,128)(2,1)} custom-call(s32[1]{0:T(128)} %bitcast.live_ref, bf16[224,128]{1,0:T(8,128)(2,1)} %reshape_squeeze_reshape.3.q_ref, bf16[17920,128]{1,0:T(8,128)(2,1)} %k_ref.1, bf16[17920,128]{1,0:T(8,128)(2,1)} %v_ref.1, s32[1,17920]{1,0:T(1,128)} %reshape.39.owner_ref, s32[224,1]{1,0:T(8,128)} %reshape_reshape.4.rowreq_ref, ...), custom_call_target="tpu_custom_call" | custom-call | flops 2055208960 | bytes 9418752 | tf_op jit(solution)/shard_map/pallas_call | solution.py:96
  24.3 0.9 reshape.41
  25.2 0.1 copy.30
  25.4 26.5 %all_gather.6 = bf16[512,896]{1,0:T(8,128)(2,1)S(1)} all-gather(bf16[32,896]{1,0:T(8,128)(2,1)S(1)} %reshape.41), channel_id=1, replica_groups=mesh['req'=16,'y'=4,'core'=2] {'req'}, dimensions={0}, use_global_device_ids=true | all-gather | bytes 974848 | tf_op jit(solution)/shard_map/all_gather | solution.py:168
  51.9 0.7 fusion.25
  52.6 0.1 convert_add_fusion
  52.7 1.7 dynamic_update_slice.3
  54.5 0.3 copy.31
  55.0 1.9 collective-permute-done
  57.0 22.3 %all-reduce.1 = bf16[4,64,448]{2,1,0:T(8,128)(2,1)S(1)} all-reduce(f32[4,64,448]{2,1,0:T(8,128)S(1)} %bitcast_add_fusion), channel_id=1, replica_groups=mesh['req'=16,'y'=4,'core'=2] {'y'}, use_global_device_ids=true, to_apply=%region_1.2 | all-reduce | flops 114688 | bytes 688128 | tf_op jit(solution)/shard_map/psum | solution.py:182
  79.3 0.8 copy.32
  80.1 0.1 collective-permute-start.1
  80.2 0.5 collective-permute-start.2
  80.7 0.1 collective-permute-start.3
  80.8 4.0 %collective-permute-done.1 = bf16[160,7168]{1,0:T(8,128)(2,1)S(1)} collective-permute-done((bf16[160,7168]{1,0:T(8,128)(2,1)}, bf16[160,7168]{1,0:T(8,128)(2,1)S(1)}, u32[]{:S(2)}, u32[]{:S(2)}) %collective-permute-start.1) | collective-permute-done | bytes 2293792 | tf_op jit(solution)/shard_map/ppermute | solution.py:163
  84.9 4.1 %pad_maximum_fusion = bf16[320,7168]{1,0:T(8,128)(2,1)} fusion(bf16[160,7168]{1,0:T(8,128)(2,1)S(1)} %collective-permute-done.1, bf16[160,7168]{1,0:T(8,128)(2,1)} %param.25), kind=kLoop, calls=%fused_computation.8 | loop fusion | flops 9175040 | bytes 9175040 | tf_op jit(solution)/shard_map/concatenate | solution.py:194
  89.0 9.9 %reshape.43 = bf16[320,16,448]{2,1,0:T(8,128)(2,1)} reshape(bf16[320,7168]{1,0:T(8,128)(2,1)} %pad_maximum_fusion) | data formatting | bytes 9175040 | tf_op jit(solution)/shard_map/reshape | solution.py:201
  98.9 28.8 %all-gather.2.cloned.1.call-done = bf16[256,7168]{0,1:T(8,128)(2,1)} async-done(((bf16[256,448]{0,1:T(8,128)(2,1)}), bf16[256,7168]{0,1:T(8,128)(2,1)}) %all-gather.2.cloned.1.call-update) | async-done | bytes 3670032 | tf_op jit(solution)/shard_map/all_gather | solution.py:185
  127.7 3.0 %fusion = f32[256]{0:T(256)S(1)} fusion(bf16[256,7168]{0,1:T(8,128)(2,1)} %all-gather.2.cloned.1.call-done), kind=kLoop, calls=%fused_computation.3 | loop fusion | flops 5504768 | bytes 3671040 | tf_op jit(solution)/shard_map/reduce_sum | solution.py:187
  130.7 6.1 %fusion.5 = f32[256,320]{0,1:T(8,128)S(1)} fusion(bf16[7168,160]{0,1:T(8,128)(2,1)} %collective-permute-done.2, bf16[7168,160]{0,1:T(8,128)(2,1)S(1)} %copy-done.3, bf16[256,7168]{0,1:T(8,128)(2,1)} %all-gather.2.cloned.1.call-done, f32[7168]{0:T(1024)S(1)} %copy-done.5, f32[256]{0:T(256)S(1)} %add_rsqrt_fusion), kind=kOutput, calls=%fused_computation.9 | convolution fusion | flops 1190920192 | bytes 8614912 | tf_op jit(solution)/shard_map/dot_general | solution.py:195
  136.9 3.3 %multiply_convert_fusion = bf16[256,320]{0,1:T(8,128)(2,1)S(1)} fusion(f32[256,320]{0,1:T(8,128)S(1)} %fusion.5, bf16[256,7168]{0,1:T(8,128)(2,1)S(1)} %copy-done.1, f32[7168]{0:T(1024)S(1)} %copy-done.5, f32[256]{0:T(256)S(1)} %add_rsqrt_fusion, bf16[7168,160]{0,1:T(8,128)(2,1)} %collective-permute-done.3, bf16[7168,160]{0,1:T(8,128)(2,1)S(1)} %copy-done.4), kind=kOutput, calls=%fused_computation.20 | convolution fusion | flops 1191411712 | bytes 8778752 | tf_op jit(solution)/shard_map/dot_general | solution.py:196
  140.2 0.2 copy.33
  140.4 8.5 %fusion.13 = bf16[16,448,4,64]{1,3,2,0:T(8,128)(2,1)} fusion(bf16[4,64,320,1]{2,1,0,3:T(8,128)(2,1)S(1)} %bitcast.26, bf16[320,16,448,1]{2,1,0,3:T(8,128)(2,1)} %bitcast.21), kind=kOutput, calls=%fused_computation.17 | convolution fusion | flops 1176240128 | bytes 8421376 | tf_op jit(solution)/shard_map/ysh,hrf->rysf/dot_general | solution.py:198
  148.9 8.3 %all-to-all-start = ((bf16[64,64,448]{2,1,0:T(8,128)(2,1)}), bf16[64,64,448]{2,1,0:T(8,128)(2,1)}, u32[]{:S(2)}, u32[]{:S(2)}) async-start(bf16[64,64,448]{2,1,0:T(8,128)(2,1)} %bitcast.22), calls=%async_computation | async-start | bytes 8388608 | tf_op jit(solution)/shard_map/all_to_all | solution.py:205
  157.2 54.3 %all-to-all-done = bf16[64,64,448]{2,1,0:T(8,128)(2,1)} async-done(((bf16[64,64,448]{2,1,0:T(8,128)(2,1)}), bf16[64,64,448]{2,1,0:T(8,128)(2,1)}, u32[]{:S(2)}, u32[]{:S(2)}) %all-to-all-start) | async-done | bytes 3670048 | tf_op jit(solution)/shard_map/all_to_all | solution.py:205
  211.5 2.9 %convert_reduce_fusion = f32[64,448]{1,0:T(8,128)S(1)} fusion(bf16[64,64,448]{2,1,0:T(8,128)(2,1)} %all-to-all-done), kind=kLoop, calls=%fused_computation.2 | loop fusion | flops 3641344 | bytes 3784704 | tf_op jit(solution)/shard_map/reduce_sum | solution.py:206
  214.4 0.6 fusion.18
  (20 shorter events, 0.3 us)
Async XLA Ops:
  6.5 45.4 %copy-start = (bf16[896,448]{0,1:T(8,128)(2,1)S(1)}, bf16[896,448]{0,1:T(8,128)(2,1)}, u32[]{:S(2)}) copy-start(bf16[896,448]{0,1:T(8,128)(2,1)} %param.20) | copy-start | bytes 2408452
  6.5 121.1 %all-gather.2.cloned.1.call-start = ((), (), s32[]{:S(2)}) async-start(), calls=%async_computation.1 | async-start | bytes 3899392 | tf_op jit(solution)/shard_map/all_gather | solution.py:185
  13.4 11.9 %copy-start.2 = (bf16[64,448]{1,0:T(8,128)(2,1)S(1)}, bf16[64,448]{1,0:T(8,128)(2,1)}, u32[]{:S(2)}) copy-start(bf16[64,448]{1,0:T(8,128)(2,1)} %param.21) | copy-start | bytes 172036
  54.9 2.0 collective-permute-start
  80.1 4.7 %collective-permute-start.1 = (bf16[160,7168]{1,0:T(8,128)(2,1)}, bf16[160,7168]{1,0:T(8,128)(2,1)S(1)}, u32[]{:S(2)}, u32[]{:S(2)}) collective-permute-start(bf16[160,7168]{1,0:T(8,128)(2,1)} %param.25), channel_id=1, source_target_pairs={{0,1},{1,0},{2,3},{3,2},{4,5},{5,4},{6,7},{7,6},{8,9},{9,8},{10,11... | collective-permute-start | bytes 6881288 | tf_op jit(solution)/shard_map/ppermute | solution.py:163
  80.2 50.5 %collective-permute-start.2 = (bf16[7168,160]{0,1:T(8,128)(2,1)}, bf16[7168,160]{0,1:T(8,128)(2,1)}, u32[]{:S(2)}, u32[]{:S(2)}) collective-permute-start(bf16[7168,160]{0,1:T(8,128)(2,1)} %param.23), channel_id=1, source_target_pairs={{0,1},{1,0},{2,3},{3,2},{4,5},{5,4},{6,7},{7,6},{8,9},{9,8},{10,11... | collective-permute-start | bytes 6881288 | tf_op jit(solution)/shard_map/ppermute | solution.py:161
  80.7 56.2 %collective-permute-start.3 = (bf16[7168,160]{0,1:T(8,128)(2,1)}, bf16[7168,160]{0,1:T(8,128)(2,1)}, u32[]{:S(2)}, u32[]{:S(2)}) collective-permute-start(bf16[7168,160]{0,1:T(8,128)(2,1)} %param.24), channel_id=1, source_target_pairs={{0,1},{1,0},{2,3},{3,2},{4,5},{5,4},{6,7},{7,6},{8,9},{9,8},{10,11... | collective-permute-start | bytes 6881288 | tf_op jit(solution)/shard_map/ppermute | solution.py:162
  89.0 41.8 %copy-start.3 = (bf16[7168,160]{0,1:T(8,128)(2,1)S(1)}, bf16[7168,160]{0,1:T(8,128)(2,1)}, u32[]{:S(2)}) copy-start(bf16[7168,160]{0,1:T(8,128)(2,1)} %param.23) | copy-start | bytes 6881284
  89.0 41.8 %copy-start.5 = (f32[7168]{0:T(1024)S(1)}, f32[7168]{0:T(1024)}, u32[]{:S(2)}) copy-start(f32[7168]{0:T(1024)} %param.22) | copy-start | bytes 86020
  130.7 6.2 %copy-start.1 = (bf16[256,7168]{0,1:T(8,128)(2,1)S(1)}, bf16[256,7168]{0,1:T(8,128)(2,1)}, u32[]{:S(2)}) copy-start(bf16[256,7168]{0,1:T(8,128)(2,1)} %all-gather.2.cloned.1.call-done) | copy-start | bytes 11010052
  130.7 6.2 %copy-start.4 = (bf16[7168,160]{0,1:T(8,128)(2,1)S(1)}, bf16[7168,160]{0,1:T(8,128)(2,1)}, u32[]{:S(2)}) copy-start(bf16[7168,160]{0,1:T(8,128)(2,1)} %param.24) | copy-start | bytes 6881284
  148.9 62.6 %all-to-all-start = ((bf16[64,64,448]{2,1,0:T(8,128)(2,1)}), bf16[64,64,448]{2,1,0:T(8,128)(2,1)}, u32[]{:S(2)}, u32[]{:S(2)}) async-start(bf16[64,64,448]{2,1,0:T(8,128)(2,1)} %bitcast.22), calls=%async_computation | async-start | bytes 8388608 | tf_op jit(solution)/shard_map/all_to_all | solution.py:205
Sparse Core Ops, SparseCore 0:
  80.3 47.3 all-gather.1
